TPU v7x, 512 devices: a whole 4x8x8 slice. The times are simulated.
512 devices in a mesh: frames: 64 (over x, y, core), tex: 8 (over z).
Axes of the slice: x: 4, y: 8, z: 8, core: 2. Of those that a mesh axis runs over, the one named last changes fastest.
Arguments:
- texture: bfloat16 [512, 16384], P('tex'), may hold values from -6 to 6
- requests: int32 [512, 32], P(('frames', 'tex')), may hold values from 0 to 63, as said below
- block_slot: int32 [512, 32], P(('frames', 'tex')), may hold values from 0 to 31
- texel_cell: int32 [512, 4096], P(('frames', 'tex')), may hold values from 0 to 960
- uv_frac: float32 [512, 2, 4096], P(('frames', 'tex')), may hold values from 0 to 1
- conv_weight: bfloat16 [32, 144], replicated, may hold values from -0.5 to 0.5
- cotangent: bfloat16 [512, 32, 4096], P(('frames', 'tex')), may hold values from -6 to 6
Outputs:
- rendered: bfloat16 [512, 32, 4096], P(('frames', 'tex'))
- texture_grad: float32 [512, 16384], P('tex', 'frames')
- weight_grad: float32 [32, 144], replicated
Inputs may be any that keep to these rules, and one draw needn't show every extreme that they name: The 4 tile numbers one renderer requests from one owner are distinct.
All inputs are finite; a program needn't handle non-finite values.
Results may differ from a plain program's by a relative error of at most 0.007.
Values may be sent and summed in bfloat16 or wider, within the bound.
No kernel may reach another device: no remote copies, remote signals or barrier semaphores. Data moves between devices by JAX's collectives and lax.ppermute only.
A program may use at most 64 MiB of HBM per device.

v0:
```python
import math

import jax
import jax.numpy as jnp
from jax import lax
from jax.sharding import PartitionSpec as P

CH = 16


def taps_and_weights(cell_row, frac_row, side):
    column = cell_row % (side - 1)
    row_index = cell_row // (side - 1)
    corner = row_index * side + column
    texel_taps = jnp.stack([corner, corner + 1, corner + side, corner + side + 1])
    frac_x = frac_row[0]
    frac_y = frac_row[1]
    weights = jnp.stack(
        [
            (1.0 - frac_x) * (1.0 - frac_y),
            frac_x * (1.0 - frac_y),
            (1.0 - frac_x) * frac_y,
            frac_x * frac_y,
        ]
    )
    return (texel_taps, weights)


def sample_matrix(texel_taps, weights, texel):
    positions = lax.broadcasted_iota(jnp.int32, (texel_taps.shape[1], texel), 1)
    matrix = jnp.zeros((texel_taps.shape[1], texel), jnp.float32)
    for number in range(4):
        matrix = matrix + jnp.where(
            texel_taps[number][:, None] == positions, weights[number][:, None], jnp.float32(0.0)
        )
    return matrix.astype(jnp.bfloat16)


def shifted(picture, shift_y, shift_x):
    height = picture.shape[1]
    width = picture.shape[2]
    padded_input = jnp.pad(picture, ((0, 0), (1, 1), (1, 1)))
    return padded_input[:, 1 + shift_y : 1 + shift_y + height, 1 + shift_x : 1 + shift_x + width]


def render_one(fetched, slot_row, cell_row, frac_row, conv_weight, cot_row):
    visible = fetched.shape[0]
    channels = fetched.shape[1]
    texel = fetched.shape[2]
    side = math.isqrt(texel)
    height = slot_row.shape[0]
    width = cell_row.shape[0] // height
    group_size = math.gcd(height, 16)
    group_count = height // group_size
    texel_taps, weights = taps_and_weights(cell_row, frac_row, side)
    taps_grouped = texel_taps.reshape(4, group_count, group_size * width).transpose(1, 0, 2)
    weights_grouped = weights.reshape(4, group_count, group_size * width).transpose(1, 0, 2)
    slots_grouped = slot_row.reshape(group_count, group_size)

    def forward(inputs):
        taps_part, weights_part, slots_part = inputs
        texture_lookup = sample_matrix(taps_part, weights_part, texel).reshape(
            group_size, width, texel
        )
        selected_entries = jnp.take(fetched, slots_part, axis=0)
        feature_maps = jnp.einsum(
            "qfm,qzm->qfz", selected_entries, texture_lookup, preferred_element_type=jnp.float32
        )
        return feature_maps.astype(jnp.bfloat16)

    grouped_features = lax.map(forward, (taps_grouped, weights_grouped, slots_grouped))
    feature_maps = grouped_features.transpose(2, 0, 1, 3).reshape(channels, height, width)
    offsets = [(shift_y, shift_x) for shift_y in (-1, 0, 1) for shift_x in (-1, 0, 1)]
    columns = jnp.concatenate(
        [shifted(feature_maps, shift_y, shift_x) for shift_y, shift_x in offsets], axis=0
    )
    columns = columns.reshape(9 * channels, height * width)
    preact = jnp.dot(conv_weight, columns, preferred_element_type=jnp.float32)
    sigmoid_pre = jax.nn.sigmoid(preact)
    rendered = (preact * sigmoid_pre).astype(jnp.bfloat16)
    pre_grad = (
        cot_row.astype(jnp.float32) * sigmoid_pre * (1.0 + preact * (1.0 - sigmoid_pre))
    ).astype(jnp.bfloat16)
    weight_local = jnp.einsum("op,kp->ok", pre_grad, columns, preferred_element_type=jnp.float32)
    col_grad = jnp.einsum("ok,op->kp", conv_weight, pre_grad, preferred_element_type=jnp.float32)
    col_grad = col_grad.reshape(9, channels, height, width)
    feat_grad = jnp.zeros((channels, height, width), jnp.float32)
    for number in range(9):
        shift_y, shift_x = offsets[number]
        feat_grad = feat_grad + shifted(col_grad[number], -shift_y, -shift_x)
    feat_grad = feat_grad.astype(jnp.bfloat16)
    grad_grouped = feat_grad.reshape(channels, group_count, group_size, width).transpose(1, 2, 0, 3)
    slot_numbers = jnp.arange(visible, dtype=jnp.int32)

    def backward(totals, inputs):
        taps_part, weights_part, slots_part, gradient_portion = inputs
        texture_lookup = sample_matrix(taps_part, weights_part, texel).reshape(
            group_size, width, texel
        )
        texel_gradient = jnp.einsum(
            "rzs,rsu->rzu", gradient_portion, texture_lookup, preferred_element_type=jnp.float32
        )
        selector = (slots_part[:, None] == slot_numbers[None, :]).astype(jnp.float32)
        added = jnp.einsum("gv,gct->vct", selector, texel_gradient, precision=lax.Precision.HIGHEST)
        return (totals + added, None)

    start = jnp.zeros((visible, channels, texel), jnp.float32)
    slot_grad, unused = lax.scan(
        backward, start, (taps_grouped, weights_grouped, slots_grouped, grad_grouped)
    )
    return (rendered, slot_grad.reshape(visible, channels * texel), weight_local)


def per_device(texture, requests, block_slot, texel_cell, uv_frac, conv_weight, cotangent):
    owners = lax.axis_size("tex")
    frame_count = lax.axis_size("frames")
    tile_count = texture.shape[0]
    tile_width = texture.shape[1]
    wanted_ids = requests.reshape(owners, -1)
    wanted = lax.all_to_all(wanted_ids, "tex", split_axis=0, concat_axis=0, tiled=True)
    served = jnp.take(texture, wanted.reshape(-1), axis=0).reshape(
        wanted.shape[0], wanted.shape[1], tile_width
    )
    returned_tiles = lax.all_to_all(served, "tex", split_axis=0, concat_axis=0, tiled=True)
    fetched = returned_tiles
    per_owner = fetched.shape[1]
    visible = owners * per_owner
    fetched = fetched.reshape(visible, CH, tile_width // CH)
    rendered, slot_grad, weight_local = render_one(
        fetched, block_slot[0], texel_cell[0], uv_frac[0], conv_weight, cotangent[0]
    )
    tile_numbers = jnp.arange(tile_count, dtype=jnp.int32)
    returned = lax.all_to_all(
        slot_grad.reshape(owners, per_owner, tile_width),
        "tex",
        split_axis=0,
        concat_axis=0,
        tiled=True,
    )
    returned_rows = returned.reshape(visible, tile_width)
    owned_flat = wanted.reshape(-1)
    selector = (tile_numbers[:, None] == owned_flat[None, :]).astype(jnp.float32)
    pool_grad = jnp.dot(selector, returned_rows, precision=lax.Precision.HIGHEST)
    texture_grad = lax.psum_scatter(pool_grad, "frames", scatter_dimension=1, tiled=True)
    norm_scale = 1.0 / math.sqrt(frame_count * owners * cotangent.shape[2])
    weight_grad = lax.psum(weight_local, ("frames", "tex")) * norm_scale
    return (rendered[None], texture_grad, weight_grad)


def solution(mesh):
    placed = (
        P("tex", None),
        P(("frames", "tex"), None),
        P(("frames", "tex"), None),
        P(("frames", "tex"), None),
        P(("frames", "tex"), None, None),
        P(),
        P(("frames", "tex"), None, None),
    )
    return jax.shard_map(
        per_device,
        mesh=mesh,
        in_specs=placed,
        out_specs=(P(("frames", "tex"), None, None), P("tex", "frames"), P()),
        check_vma=False,
    )
```

profile of v0, /device:TPU:1, one launch (start us, length us, event | category | flops | bytes accessed | tf_op | source)
XLA Modules:
  0.0 332.7 jit_solution(9305829083828627682)
XLA Ops:
  9.8 10.9 %all-to-all-start = ((s32[8,1,4]{2,1,0:T(1,128)}), s32[8,1,4]{2,1,0:T(1,128)S(1)}, u32[]{:S(2)}, u32[]{:S(2)}) async-start(s32[8,1,4]{2,1,0:T(1,128)} %bitcast.12), calls=%async_computation | async-start | bytes 8192 | tf_op jit(solution)/shard_map/all_to_all | solution.py:120
  21.5 5.6 %all-to-all-done = s32[8,1,4]{2,1,0:T(1,128)S(1)} async-done(((s32[8,1,4]{2,1,0:T(1,128)}), s32[8,1,4]{2,1,0:T(1,128)S(1)}, u32[]{:S(2)}, u32[]{:S(2)}) %all-to-all-start) | async-done | bytes 160 | tf_op jit(solution)/shard_map/all_to_all | solution.py:120
  30.5 2.7 broadcast_select_fusion
  33.3 3.6 %all-to-all-start.1 = ((bf16[8,4,16384]{2,1,0:T(4,128)(2,1)}), bf16[8,4,16384]{2,1,0:T(4,128)(2,1)S(1)}, u32[]{:S(2)}, u32[]{:S(2)}) async-start(bf16[8,4,16384]{2,1,0:T(4,128)(2,1)} %broadcast_select_fusion), calls=%async_computation.1 | async-start | bytes 2097152 | tf_op jit(solution)/shard_map/all_to_all | solution.py:124
  37.9 28.1 %all-to-all-done.1 = bf16[8,4,16384]{2,1,0:T(4,128)(2,1)S(1)} async-done(((bf16[8,4,16384]{2,1,0:T(4,128)(2,1)}), bf16[8,4,16384]{2,1,0:T(4,128)(2,1)S(1)}, u32[]{:S(2)}, u32[]{:S(2)}) %all-to-all-start.1) | async-done | bytes 1048608 | tf_op jit(solution)/shard_map/all_to_all | solution.py:124
  65.9 1.6 reshape.367
  67.5 16.0 %while.21 = (s32[]{:T(128)}, bf16[2,16,16,128]{3,2,1,0:T(8,128)(2,1)S(1)}, s32[2,16]{1,0:T(2,128)S(1)}, bf16[32,16,1024]{2,1,0:T(8,128)(2,1)}, s32[2,4,2048]{2,1...) while((s32[]{:T(128)}, ...), condition=%wide.region_1.2_spmd, body=%wide.region_0.1_spmd.sunk | while | flops 92570768 | bytes 1840149 | solution.py:71
  67.7 1.8 gather_fusion
  69.5 6.1 %fusion.58 = bf16[2,16,16,128]{3,2,1,0:T(8,128)(2,1)S(1)} fusion(bf16[2,16,16,128]{3,2,1,0:T(8,128)(2,1)S(1)} %get-tuple-element.284, s32[]{:T(128)S(6)} %copy.61, f32[16,128]{1,0:T(8,128)S(1)} %bitcast.200, s32[16,128]{1,0:T(8,128)S(1)} %bitcast.204, f32[16,128]{1,0:T(8,128)S(1)} %bitcast.198, s32[16,128]{1,0:T(8,128)S(1)} %bitcast.202, ...), kind=kOutput, calls=%fused_computation.11.clone.1 | convolution fusion | flops 92569600 | bytes 655876 | tf_op jit(solution)/shard_map/while/body/eval_jaxpr/qfm,qzm->qfz/dot_general | solution.py:66
  75.7 1.8 gather_fusion
  77.5 6.1 %fusion.58 = bf16[2,16,16,128]{3,2,1,0:T(8,128)(2,1)S(1)} fusion(bf16[2,16,16,128]{3,2,1,0:T(8,128)(2,1)S(1)} %get-tuple-element.284, s32[]{:T(128)S(6)} %copy.61, f32[16,128]{1,0:T(8,128)S(1)} %bitcast.200, s32[16,128]{1,0:T(8,128)S(1)} %bitcast.204, f32[16,128]{1,0:T(8,128)S(1)} %bitcast.198, s32[16,128]{1,0:T(8,128)S(1)} %bitcast.202, ...), kind=kOutput, calls=%fused_computation.11.clone.1 | convolution fusion | flops 92569600 | bytes 655876 | tf_op jit(solution)/shard_map/while/body/eval_jaxpr/qfm,qzm->qfz/dot_general | solution.py:66
  87.4 22.6 %while.22 = (s32[]{:T(128)}, f32[32,16,1024]{2,0,1:T(8,128)}, s32[2,16]{1,0:T(2,128)S(1)}, bf16[2,16,16,128]{3,2,1,0:T(8,128)(2,1)S(1)}, s32[2,4,2048]{2,1,0:T(4...) while((s32[]{:T(128)}, f32[32,16,1024]{2,0,1:T(8,128)}, ...), condition=%wide.region_3.4_spmd.clone, body=%wide.region_2.3_spmd.clone.sunk | while | flops 193987072 | bytes 23331268 | solution.py:108
  87.6 7.3 %fusion.62 = f32[16,16,1024]{2,1,0:T(8,128)S(1)} fusion(f32[16,128]{1,0:T(8,128)S(1)} %bitcast.208, s32[16,128]{1,0:T(8,128)S(1)} %bitcast.212, f32[16,128]{1,0:T(8,128)S(1)} %bitcast.206, s32[16,128]{1,0:T(8,128)S(1)} %bitcast.210, f32[16,128]{1,0:T(8,128)S(1)} %bitcast.207, s32[16,128]{1,0:T(8,128)S(1)} %bitcast.211, f32[16,128]{1,0:T(8,128)S(1)} %bitcast.205, ...), kind=kOutput, calls=%fused_computation.36.clone.1 | convolution fusion | flops 92274688 | bytes 1179652 | tf_op jit(solution)/shard_map/while/body/eval_jaxpr/rzs,rsu->rzu/dot_general | solution.py:100
  94.8 2.6 select_add_fusion.2
  98.9 7.3 %fusion.62 = f32[16,16,1024]{2,1,0:T(8,128)S(1)} fusion(f32[16,128]{1,0:T(8,128)S(1)} %bitcast.208, s32[16,128]{1,0:T(8,128)S(1)} %bitcast.212, f32[16,128]{1,0:T(8,128)S(1)} %bitcast.206, s32[16,128]{1,0:T(8,128)S(1)} %bitcast.210, f32[16,128]{1,0:T(8,128)S(1)} %bitcast.207, s32[16,128]{1,0:T(8,128)S(1)} %bitcast.211, f32[16,128]{1,0:T(8,128)S(1)} %bitcast.205, ...), kind=kOutput, calls=%fused_computation.36.clone.1 | convolution fusion | flops 92274688 | bytes 1179652 | tf_op jit(solution)/shard_map/while/body/eval_jaxpr/rzs,rsu->rzu/dot_general | solution.py:100
  106.1 2.6 select_add_fusion.2
  110.0 4.1 %copy.26 = f32[32,16,1024]{2,1,0:T(8,128)} copy(f32[32,16,1024]{2,0,1:T(8,128)} %get-tuple-element.73) | data formatting | bytes 4194304 | tf_op jit(solution)/shard_map/while | solution.py:108
  114.2 3.7 %reshape_reshape.3 = f32[8,4,16384]{2,1,0:T(4,128)} reshape(f32[32,16,1024]{2,1,0:T(8,128)} %copy.26) | data formatting | bytes 4194304 | tf_op jit(solution)/shard_map/reshape;reshape | solution.py:134
  117.9 4.3 %all-to-all-start.2 = ((f32[8,4,16384]{2,1,0:T(4,128)}), f32[8,4,16384]{2,1,0:T(4,128)}, u32[]{:S(2)}, u32[]{:S(2)}) async-start(f32[8,4,16384]{2,1,0:T(4,128)} %reshape_reshape.3), calls=%async_computation.2 | async-start | bytes 4194304 | tf_op jit(solution)/shard_map/all_to_all | solution.py:133
  122.5 47.8 %all-to-all-done.2 = f32[8,4,16384]{2,1,0:T(4,128)} async-done(((f32[8,4,16384]{2,1,0:T(4,128)}), f32[8,4,16384]{2,1,0:T(4,128)}, u32[]{:S(2)}, u32[]{:S(2)}) %all-to-all-start.2) | async-done | bytes 2097184 | tf_op jit(solution)/shard_map/all_to_all | solution.py:133
  170.4 3.0 reshape.371
  173.3 5.4 %fusion.34 = f32[64,16384]{1,0:T(8,128)} fusion(f32[32,16384]{1,0:T(8,128)} %reshape.371, s32[32]{0:T(128)S(1)} %reshape.369), kind=kOutput, calls=%fused_computation.113 | convolution fusion | flops 402655232 | bytes 6291584 | tf_op jit(solution)/shard_map/dot_general | solution.py:143
  181.1 101.6 %psum.7 = f32[32,144]{1,0:T(8,128)S(1)} all-reduce(f32[32,144]{1,0:T(8,128)} %fusion.40), channel_id=1, replica_groups=mesh['frames'=64,'tex'=8] {'frames','tex'}, use_global_device_ids=true, to_apply=%region_5.6 | all-reduce | flops 4608 | bytes 36864 | tf_op jit(solution)/shard_map/psum | solution.py:146
  283.3 42.6 %reduce-scatter.2.cloned.1.call-done = f32[64,256]{1,0:T(8,128)} async-done(((f32[64,16384]{1,0:T(8,128)}), f32[64,256]{1,0:T(8,128)}) %reduce-scatter.2.cloned.1.call-update) | async-done | bytes 65552 | tf_op jit(solution)/shard_map/reduce_scatter | solution.py:144
  (91 shorter events, 17.9 us)
Async XLA Ops:
  7.2 20.9 %copy-start = (bf16[64,16384]{1,0:T(8,128)(2,1)S(1)}, bf16[64,16384]{1,0:T(8,128)(2,1)}, u32[]{:S(2)}) copy-start(bf16[64,16384]{1,0:T(8,128)(2,1)} %param.11) | copy-start | bytes 6291460
  9.8 17.3 %all-to-all-start = ((s32[8,1,4]{2,1,0:T(1,128)}), s32[8,1,4]{2,1,0:T(1,128)S(1)}, u32[]{:S(2)}, u32[]{:S(2)}) async-start(s32[8,1,4]{2,1,0:T(1,128)} %bitcast.12), calls=%async_computation | async-start | bytes 8192 | tf_op jit(solution)/shard_map/all_to_all | solution.py:120
  30.5 6.4 %copy-start.8 = (s32[1,32]{1,0:T(1,128)S(1)}, s32[1,32]{1,0:T(1,128)}, u32[]{:S(2)}) copy-start(s32[1,32]{1,0:T(1,128)} %param.13) | copy-start | bytes 388
  30.5 7.2 %copy-start.5 = (f32[1,2,4096]{2,1,0:T(2,128)S(1)}, f32[1,2,4096]{2,1,0:T(2,128)}, u32[]{:S(2)}) copy-start(f32[1,2,4096]{2,1,0:T(2,128)} %param.15) | copy-start | bytes 98308
  33.3 32.7 %all-to-all-start.1 = ((bf16[8,4,16384]{2,1,0:T(4,128)(2,1)}), bf16[8,4,16384]{2,1,0:T(4,128)(2,1)S(1)}, u32[]{:S(2)}, u32[]{:S(2)}) async-start(bf16[8,4,16384]{2,1,0:T(4,128)(2,1)} %broadcast_select_fusion), calls=%async_computation.1 | async-start | bytes 2097152 | tf_op jit(solution)/shard_map/all_to_all | solution.py:124
  83.5 0.9 copy-start.6
  83.5 1.0 copy-start.7
  84.5 1.1 copy-start.3
  87.6 7.3 %copy-start.1 = (f32[32,16,1024]{2,0,1:T(8,128)S(1)}, f32[32,16,1024]{2,0,1:T(8,128)}, u32[]{:S(2)}) copy-start(f32[32,16,1024]{2,0,1:T(8,128)} %get-tuple-element.317) | copy-start | bytes 6291460 | tf_op jit(solution)/shard_map/while
  97.4 1.3 copy-start.2
  98.9 7.3 %copy-start.1 = (f32[32,16,1024]{2,0,1:T(8,128)S(1)}, f32[32,16,1024]{2,0,1:T(8,128)}, u32[]{:S(2)}) copy-start(f32[32,16,1024]{2,0,1:T(8,128)} %get-tuple-element.317) | copy-start | bytes 6291460 | tf_op jit(solution)/shard_map/while
  108.7 1.3 copy-start.2
  117.9 52.5 %all-to-all-start.2 = ((f32[8,4,16384]{2,1,0:T(4,128)}), f32[8,4,16384]{2,1,0:T(4,128)}, u32[]{:S(2)}, u32[]{:S(2)}) async-start(f32[8,4,16384]{2,1,0:T(4,128)} %reshape_reshape.3), calls=%async_computation.2 | async-start | bytes 4194304 | tf_op jit(solution)/shard_map/all_to_all | solution.py:133
  122.2 203.7 %reduce-scatter.2.cloned.1.call-start = ((), (), s32[]{:S(2)}) async-start(), calls=%async_computation.4 | async-start | bytes 4259840 | tf_op jit(solution)/shard_map/reduce_scatter | solution.py:144
  178.7 1.3 copy-start.4
Sparse Core Ops, SparseCore 0:
  178.8 146.9 reduce-scatter.1
where the time goes:
time: 337 us; the launch traced here: 333 us
  waiting for transfers between devices  124 us (37%)
  blocking collectives  102 us (30%)
  matrix products  39.9 us (12%)
  local copies, waits for them, and re-layouts  25.9 us (8%)
  starting transfers between devices  19 us (6%)
  between operations  14.3 us (4%)
  other arithmetic  7.73 us (2%)
    psum x1, blocking collectives, per_device(): weight_grad = lax.psum(weight_local, ('frames', 'tex')) * norm_scale  102 us
    all_to_all x1, waiting for transfers between devices, per_device(): lax.all_to_all(slot_grad.reshape(owners, per_owner, tile_width), 'tex', s...  47.8 us
    reduce_scatter x1, waiting for transfers between devices, per_device(): lax.psum_scatter(pool_grad, 'frames', scatter_dimension=1, tiled=True)  42.6 us
    all_to_all x1, waiting for transfers between devices, per_device(): lax.all_to_all(served, 'tex', split_axis=0, concat_axis=0, tiled=True)  28.1 us
    dot_general x2, matrix products, backward(): jnp.einsum('rzs,rsu->rzu', gradient_portion, texture_lookup, preferred_el...  14.5 us
    dot_general x2, matrix products, forward(): jnp.einsum('qfm,qzm->qfz', selected_entries, texture_lookup, preferred_el...  12.1 us
    all_to_all x1, starting transfers between devices, per_device(): lax.all_to_all(wanted_ids, 'tex', split_axis=0, concat_axis=0, tiled=True)  10.9 us
  transfers between devices with their start and end apart: 4, of which 4 were waited for; matrix products, arithmetic and copies ran while one was open for 1% of the time, Pallas kernels for 0%

commit v1 on v0

--- a/solution.py
+++ b/solution.py
@@ -129,19 +129,18 @@
     rendered, slot_grad, weight_local = render_one(
         fetched, block_slot[0], texel_cell[0], uv_frac[0], conv_weight, cotangent[0]
     )
+    columns = tile_width // frame_count
+    spread = slot_grad.reshape(visible, frame_count, columns).transpose(1, 0, 2)
+    gathered = lax.all_to_all(spread, "frames", split_axis=0, concat_axis=0, tiled=True)
+    gathered = gathered.reshape(frame_count, owners, per_owner, columns)
+    senders = lax.all_gather(requests[0], "frames").reshape(frame_count, owners, per_owner)
     tile_numbers = jnp.arange(tile_count, dtype=jnp.int32)
-    returned = lax.all_to_all(
-        slot_grad.reshape(owners, per_owner, tile_width),
-        "tex",
-        split_axis=0,
-        concat_axis=0,
-        tiled=True,
+    selector = (senders[None] == tile_numbers[:, None, None, None]).astype(jnp.float32)
+    partial = jnp.einsum(
+        "qfoj,fojc->oqc", selector, gathered, precision=lax.Precision.HIGHEST
     )
-    returned_rows = returned.reshape(visible, tile_width)
-    owned_flat = wanted.reshape(-1)
-    selector = (tile_numbers[:, None] == owned_flat[None, :]).astype(jnp.float32)
-    pool_grad = jnp.dot(selector, returned_rows, precision=lax.Precision.HIGHEST)
-    texture_grad = lax.psum_scatter(pool_grad, "frames", scatter_dimension=1, tiled=True)
+    texture_grad = lax.psum_scatter(partial, "tex", scatter_dimension=0, tiled=True)
+    texture_grad = texture_grad.reshape(tile_count, columns)
     norm_scale = 1.0 / math.sqrt(frame_count * owners * cotangent.shape[2])
     weight_grad = lax.psum(weight_local, ("frames", "tex")) * norm_scale
     return (rendered[None], texture_grad, weight_grad)

time: 337 us -> 318 us (0.944)
  waiting for transfers between devices: 124 us -> 32.9 us
  blocking collectives: 102 us -> 173 us
  starting transfers between devices: 19 us -> 25.6 us
    all_gather x0 -> x1, blocking collectives: none -> 77.5 us  [per_device(): lax.all_gather(requests[0], 'frames')]
    all_to_all x1, waiting for transfers between devices: 47.8 us -> 0.01 us  [per_device(): lax.all_to_all(spread, 'frames', split_axis=0, concat_axis=0, tiled=True)]
    reduce_scatter x1, waiting for transfers between devices: 42.6 us -> 0.01 us  [per_device(): lax.psum_scatter(partial, 'tex', scatter_dimension=0, tiled=True)]
    all_to_all x1, starting transfers between devices: 4.34 us -> 11.1 us  [per_device(): lax.all_to_all(spread, 'frames', split_axis=0, concat_axis=0, tiled=True)]
    psum x1, blocking collectives: 102 us -> 95.1 us  [per_device(): weight_grad = lax.psum(weight_local, ('frames', 'tex')) * norm_scale]
    transpose x0 -> x1, local copies, waits for them, and re-layouts: none -> 4.13 us  [per_device(): spread = slot_grad.reshape(visible, frame_count, columns).transpose(1, 0, 2)]
    dot_general x1, matrix products: 5.37 us -> 1.87 us  [per_device(): jnp.einsum('qfoj,fojc->oqc', selector, gathered, precision=lax.Precision....]
  transfers between devices with their start and end apart: 4 -> 4, of which waited for: 4 -> 2; matrix products, arithmetic and copies ran while one was open for 1% -> 1% of each run, Pallas kernels for 0% -> 0%
where the time goes in v1:
time: 318 us; the launch traced here: 317 us
  blocking collectives  173 us (54%)
  matrix products  37 us (12%)
  waiting for transfers between devices  32.9 us (10%)
  local copies, waits for them, and re-layouts  26.6 us (8%)
  starting transfers between devices  25.6 us (8%)
  between operations  14.4 us (5%)
  other arithmetic  7.69 us (2%)
    psum x1, blocking collectives, per_device(): weight_grad = lax.psum(weight_local, ('frames', 'tex')) * norm_scale  95.1 us
    all_gather x1, blocking collectives, per_device(): lax.all_gather(requests[0], 'frames')  77.5 us
    all_to_all x1, waiting for transfers between devices, per_device(): lax.all_to_all(served, 'tex', split_axis=0, concat_axis=0, tiled=True)  28.8 us
    dot_general x2, matrix products, backward(): jnp.einsum('rzs,rsu->rzu', gradient_portion, texture_lookup, preferred_el...  12.8 us
    dot_general x2, matrix products, forward(): jnp.einsum('qfm,qzm->qfz', selected_entries, texture_lookup, preferred_el...  12.1 us
    all_to_all x1, starting transfers between devices, per_device(): lax.all_to_all(spread, 'frames', split_axis=0, concat_axis=0, tiled=True)  11.1 us
    all_to_all x1, starting transfers between devices, per_device(): lax.all_to_all(wanted_ids, 'tex', split_axis=0, concat_axis=0, tiled=True)  10.9 us
    dot_general x2, matrix products, backward(): jnp.einsum('gv,gct->vct', selector, texel_gradient, precision=lax.Precisi...  7.51 us
  transfers between devices with their start and end apart: 4, of which 2 were waited for; matrix products, arithmetic and copies ran while one was open for 1% of the time, Pallas kernels for 0%

profile of v1, /device:TPU:1, one launch (start us, length us, event | category | flops | bytes accessed | tf_op | source)
XLA Modules:
  0.0 316.8 jit_solution(3174709285711801497)
XLA Ops:
  9.8 10.9 %all-to-all-start = ((s32[8,1,4]{2,1,0:T(1,128)}), s32[8,1,4]{2,1,0:T(1,128)S(1)}, u32[]{:S(2)}, u32[]{:S(2)}) async-start(s32[8,1,4]{2,1,0:T(1,128)} %bitcast.12), calls=%async_computation | async-start | bytes 8192 | tf_op jit(solution)/shard_map/all_to_all | solution.py:120
  23.1 4.1 %all-to-all-done = s32[8,1,4]{2,1,0:T(1,128)S(1)} async-done(((s32[8,1,4]{2,1,0:T(1,128)}), s32[8,1,4]{2,1,0:T(1,128)S(1)}, u32[]{:S(2)}, u32[]{:S(2)}) %all-to-all-start) | async-done | bytes 160 | tf_op jit(solution)/shard_map/all_to_all | solution.py:120
  30.5 2.7 broadcast_select_fusion
  33.3 3.6 %all-to-all-start.1 = ((bf16[8,4,16384]{2,1,0:T(4,128)(2,1)}), bf16[8,4,16384]{2,1,0:T(4,128)(2,1)S(1)}, u32[]{:S(2)}, u32[]{:S(2)}) async-start(bf16[8,4,16384]{2,1,0:T(4,128)(2,1)} %broadcast_select_fusion), calls=%async_computation.1 | async-start | bytes 2097152 | tf_op jit(solution)/shard_map/all_to_all | solution.py:124
  37.1 28.8 %all-to-all-done.1 = bf16[8,4,16384]{2,1,0:T(4,128)(2,1)S(1)} async-done(((bf16[8,4,16384]{2,1,0:T(4,128)(2,1)}), bf16[8,4,16384]{2,1,0:T(4,128)(2,1)S(1)}, u32[]{:S(2)}, u32[]{:S(2)}) %all-to-all-start.1) | async-done | bytes 1048608 | tf_op jit(solution)/shard_map/all_to_all | solution.py:124
  65.9 1.6 reshape.367
  67.5 16.0 %while.21 = (s32[]{:T(128)}, bf16[2,16,16,128]{3,2,1,0:T(8,128)(2,1)S(1)}, s32[2,16]{1,0:T(2,128)S(1)}, bf16[32,16,1024]{2,1,0:T(8,128)(2,1)}, s32[2,4,2048]{2,1...) while((s32[]{:T(128)}, ...), condition=%wide.region_1.2_spmd, body=%wide.region_0.1_spmd.sunk | while | flops 92570768 | bytes 1840141 | solution.py:71
  67.6 1.8 gather_fusion
  69.5 6.1 %fusion.57 = bf16[2,16,16,128]{3,2,1,0:T(8,128)(2,1)S(1)} fusion(bf16[2,16,16,128]{3,2,1,0:T(8,128)(2,1)S(1)} %get-tuple-element.284, s32[]{:T(128)} %get-tuple-element.283, f32[16,128]{1,0:T(8,128)S(1)} %bitcast.209, s32[16,128]{1,0:T(8,128)S(1)} %bitcast.213, f32[16,128]{1,0:T(8,128)S(1)} %bitcast.207, s32[16,128]{1,0:T(8,128)S(1)} %bitcast.211, ...), kind=kOutput, calls=%fused_computation.11.clone.1 | convolution fusion | flops 92569600 | bytes 655876 | tf_op jit(solution)/shard_map/while/body/eval_jaxpr/qfm,qzm->qfz/dot_general | solution.py:66
  75.7 1.8 gather_fusion
  77.5 6.1 %fusion.57 = bf16[2,16,16,128]{3,2,1,0:T(8,128)(2,1)S(1)} fusion(bf16[2,16,16,128]{3,2,1,0:T(8,128)(2,1)S(1)} %get-tuple-element.284, s32[]{:T(128)} %get-tuple-element.283, f32[16,128]{1,0:T(8,128)S(1)} %bitcast.209, s32[16,128]{1,0:T(8,128)S(1)} %bitcast.213, f32[16,128]{1,0:T(8,128)S(1)} %bitcast.207, s32[16,128]{1,0:T(8,128)S(1)} %bitcast.211, ...), kind=kOutput, calls=%fused_computation.11.clone.1 | convolution fusion | flops 92569600 | bytes 655876 | tf_op jit(solution)/shard_map/while/body/eval_jaxpr/qfm,qzm->qfz/dot_general | solution.py:66
  88.1 20.5 %while.22 = (s32[]{:T(128)}, f32[32,16,1024]{2,0,1:T(8,128)}, s32[2,16]{1,0:T(2,128)S(1)}, bf16[2,16,16,128]{3,2,1,0:T(8,128)(2,1)}, s32[2,4,2048]{2,1,0:T(4,128...) while((s32[]{:T(128)}, f32[32,16,1024]{2,0,1:T(8,128)}, ...), condition=%wide.region_3.4_spmd.clone, body=%wide.region_2.3_spmd.clone.sunk | while | flops 193987072 | bytes 6554495 | solution.py:108
  88.2 6.4 %fusion.61 = f32[16,16,1024]{2,1,0:T(8,128)S(1)} fusion(f32[16,128]{1,0:T(8,128)S(1)} %bitcast.217, s32[16,128]{1,0:T(8,128)S(1)} %bitcast.221, f32[16,128]{1,0:T(8,128)S(1)} %bitcast.215, s32[16,128]{1,0:T(8,128)S(1)} %bitcast.219, f32[16,128]{1,0:T(8,128)S(1)} %bitcast.216, s32[16,128]{1,0:T(8,128)S(1)} %bitcast.220, f32[16,128]{1,0:T(8,128)S(1)} %bitcast.214, ...), kind=kOutput, calls=%fused_computation.36.clone.1 | convolution fusion | flops 92274688 | bytes 1180160 | tf_op jit(solution)/shard_map/while/body/eval_jaxpr/rzs,rsu->rzu/dot_general | solution.py:100
  94.6 3.0 select_add_fusion.2
  97.6 6.4 %fusion.61 = f32[16,16,1024]{2,1,0:T(8,128)S(1)} fusion(f32[16,128]{1,0:T(8,128)S(1)} %bitcast.217, s32[16,128]{1,0:T(8,128)S(1)} %bitcast.221, f32[16,128]{1,0:T(8,128)S(1)} %bitcast.215, s32[16,128]{1,0:T(8,128)S(1)} %bitcast.219, f32[16,128]{1,0:T(8,128)S(1)} %bitcast.216, s32[16,128]{1,0:T(8,128)S(1)} %bitcast.220, f32[16,128]{1,0:T(8,128)S(1)} %bitcast.214, ...), kind=kOutput, calls=%fused_computation.36.clone.1 | convolution fusion | flops 92274688 | bytes 1180160 | tf_op jit(solution)/shard_map/while/body/eval_jaxpr/rzs,rsu->rzu/dot_general | solution.py:100
  104.0 4.5 %select_add_fusion.2 = f32[32,16,1024]{2,0,1:T(8,128)} fusion(f32[32,16,1024]{2,0,1:T(8,128)} %get-tuple-element.317, f32[16,16,1024]{2,1,0:T(8,128)S(1)} %fusion.61, pred[]{:T(512)S(6)} %compare.12, s32[16]{0:T(128)S(1)} %fusion.62), kind=kOutput, calls=%fused_computation.37.clone.1 | convolution fusion | flops 101712384 | bytes 5242945 | tf_op jit(solution)/shard_map/while/body/eval_jaxpr/gv,gct->vct/dot_general | solution.py:104
  108.6 4.1 %copy.29 = f32[32,16,1024]{2,1,0:T(8,128)} copy(f32[32,16,1024]{2,0,1:T(8,128)} %get-tuple-element.73) | data formatting | bytes 4194304 | tf_op jit(solution)/shard_map/while | solution.py:108
  112.7 2.9 reshape_reshape.3
  115.6 4.1 %copy.30 = f32[64,32,256]{2,1,0:T(8,128)} copy(f32[64,32,256]{2,0,1:T(8,128)} %bitcast.186) | data formatting | bytes 4194304 | tf_op jit(solution)/shard_map/transpose | solution.py:133
  119.7 11.1 %all-to-all-start.2 = ((f32[64,32,256]{2,1,0:T(8,128)}), f32[64,32,256]{2,1,0:T(8,128)}, u32[]{:S(2)}, u32[]{:S(2)}) async-start(f32[64,32,256]{2,1,0:T(8,128)} %copy.30), calls=%async_computation.2 | async-start | bytes 4194304 | tf_op jit(solution)/shard_map/all_to_all | solution.py:134
  130.9 77.5 %all-gather = s32[64,1,32]{2,1,0:T(1,128)S(1)} all-gather(s32[1,1,32]{2,1,0:T(1,128)S(1)} %bitcast.230), channel_id=1, replica_groups=mesh['frames'=64,'tex'=8] {'frames'}, dimensions={0}, use_global_device_ids=true | all-gather | bytes 8320 | tf_op jit(solution)/shard_map/all_gather | solution.py:136
  208.4 2.8 copy.31
  211.3 1.9 convolution_bitcast_fusion.2
  214.3 95.1 %psum.7 = f32[32,144]{1,0:T(8,128)S(1)} all-reduce(f32[32,144]{1,0:T(8,128)} %fusion.39), channel_id=1, replica_groups=mesh['frames'=64,'tex'=8] {'frames','tex'}, use_global_device_ids=true, to_apply=%region_5.6 | all-reduce | flops 4608 | bytes 36864 | tf_op jit(solution)/shard_map/psum | solution.py:145
  (85 shorter events, 15.2 us)
Async XLA Ops:
  7.2 20.7 %copy-start = (bf16[64,16384]{1,0:T(8,128)(2,1)S(1)}, bf16[64,16384]{1,0:T(8,128)(2,1)}, u32[]{:S(2)}) copy-start(bf16[64,16384]{1,0:T(8,128)(2,1)} %param.11) | copy-start | bytes 6291460
  9.8 17.3 %all-to-all-start = ((s32[8,1,4]{2,1,0:T(1,128)}), s32[8,1,4]{2,1,0:T(1,128)S(1)}, u32[]{:S(2)}, u32[]{:S(2)}) async-start(s32[8,1,4]{2,1,0:T(1,128)} %bitcast.12), calls=%async_computation | async-start | bytes 8192 | tf_op jit(solution)/shard_map/all_to_all | solution.py:120
  30.5 6.3 %copy-start.4 = (s32[1,4096]{1,0:T(1,128)S(1)}, s32[1,4096]{1,0:T(1,128)}, u32[]{:S(2)}) copy-start(s32[1,4096]{1,0:T(1,128)} %param.14) | copy-start | bytes 49156
  33.3 32.7 %all-to-all-start.1 = ((bf16[8,4,16384]{2,1,0:T(4,128)(2,1)}), bf16[8,4,16384]{2,1,0:T(4,128)(2,1)S(1)}, u32[]{:S(2)}, u32[]{:S(2)}) async-start(bf16[8,4,16384]{2,1,0:T(4,128)(2,1)} %broadcast_select_fusion), calls=%async_computation.1 | async-start | bytes 2097152 | tf_op jit(solution)/shard_map/all_to_all | solution.py:124
  83.5 0.9 copy-start.3
  83.5 1.0 copy-start.6
  84.5 1.1 copy-start.1
  119.7 11.2 %copy-start.5 = (s32[1,32]{1,0:T(1,128)S(1)}, s32[1,32]{1,0:T(1,128)}, u32[]{:S(2)}) copy-start(s32[1,32]{1,0:T(1,128)} %param.12) | copy-start | bytes 388
  119.7 88.7 %all-to-all-start.2 = ((f32[64,32,256]{2,1,0:T(8,128)}), f32[64,32,256]{2,1,0:T(8,128)}, u32[]{:S(2)}, u32[]{:S(2)}) async-start(f32[64,32,256]{2,1,0:T(8,128)} %copy.30), calls=%async_computation.2 | async-start | bytes 4194304 | tf_op jit(solution)/shard_map/all_to_all | solution.py:134
  130.8 179.2 %reduce-scatter.2.cloned.1.call-start = ((), (), s32[]{:S(2)}) async-start(), calls=%async_computation.4 | async-start | bytes 589824 | tf_op jit(solution)/shard_map/reduce_scatter | solution.py:142
  211.2 1.9 copy-start.2
Sparse Core Ops, SparseCore 0:
  213.3 29.5 reduce-scatter.1

commit v2 on v1

--- a/solution.py
+++ b/solution.py
@@ -130,19 +130,45 @@
         fetched, block_slot[0], texel_cell[0], uv_frac[0], conv_weight, cotangent[0]
     )
     columns = tile_width // frame_count
+    weight_size = weight_local.size
+    chunk = -(-weight_size // frame_count)
+    request_count = requests.shape[1]
+    extra = -(-(chunk + request_count) // columns)
+    weight_rows = jnp.pad(weight_local.reshape(-1), (0, chunk * frame_count - weight_size))
+    side_row = jnp.concatenate(
+        [
+            weight_rows.reshape(frame_count, chunk),
+            jnp.broadcast_to(requests.astype(jnp.float32), (frame_count, request_count)),
+            jnp.zeros((frame_count, extra * columns - chunk - request_count), jnp.float32),
+        ],
+        axis=1,
+    ).reshape(frame_count, extra, columns)
     spread = slot_grad.reshape(visible, frame_count, columns).transpose(1, 0, 2)
+    spread = jnp.concatenate([spread, side_row], axis=1)
     gathered = lax.all_to_all(spread, "frames", split_axis=0, concat_axis=0, tiled=True)
-    gathered = gathered.reshape(frame_count, owners, per_owner, columns)
-    senders = lax.all_gather(requests[0], "frames").reshape(frame_count, owners, per_owner)
+    side = gathered[:, visible:].reshape(frame_count, extra * columns)
+    frame_weight = jnp.sum(side[:, :chunk], axis=0)
+    senders = side[:, chunk : chunk + request_count].astype(jnp.int32)
+    senders = senders.reshape(frame_count, owners, per_owner)
+    gathered = gathered[:, :visible].reshape(frame_count, owners, per_owner, columns)
     tile_numbers = jnp.arange(tile_count, dtype=jnp.int32)
     selector = (senders[None] == tile_numbers[:, None, None, None]).astype(jnp.float32)
     partial = jnp.einsum(
         "qfoj,fojc->oqc", selector, gathered, precision=lax.Precision.HIGHEST
     )
-    texture_grad = lax.psum_scatter(partial, "tex", scatter_dimension=0, tiled=True)
-    texture_grad = texture_grad.reshape(tile_count, columns)
+    weight_tail = -(-chunk // columns) * columns
+    weight_block = jnp.pad(frame_weight, (0, weight_tail - chunk)).reshape(1, -1, columns)
+    partial = jnp.concatenate(
+        [partial, jnp.broadcast_to(weight_block, (owners,) + weight_block.shape[1:])], axis=1
+    )
+    collected = jnp.sum(lax.all_to_all(partial, "tex", 0, 0, tiled=True), axis=0)
+    texture_grad = collected[:tile_count]
+    chunk_total = collected[tile_count:].reshape(-1)[:chunk]
+    shared = lax.all_to_all(
+        jnp.broadcast_to(chunk_total[None], (frame_count, chunk)), "frames", 0, 0, tiled=True
+    )
     norm_scale = 1.0 / math.sqrt(frame_count * owners * cotangent.shape[2])
-    weight_grad = lax.psum(weight_local, ("frames", "tex")) * norm_scale
+    weight_grad = shared.reshape(-1)[:weight_size].reshape(weight_local.shape) * norm_scale
     return (rendered[None], texture_grad, weight_grad)
 
 

time: 318 us -> 232 us (0.73)
  blocking collectives: 173 us -> 94.4 us
  between operations: 14.4 us -> 1.01 us
  waiting for transfers between devices: 32.9 us -> 41.4 us
  starting transfers between devices: 25.6 us -> 20.5 us
    psum x1 -> x0, blocking collectives: 95.1 us -> none  [per_device(): weight_grad = lax.psum(weight_local, ('frames', 'tex')) * norm_scale]
    all_to_all x0 -> x2, blocking collectives: none -> 94.4 us  [the longest x1 72.6 us: per_device(): lax.all_to_all(spread, 'frames', split_axis=0, concat_axis=0, tiled=True)]
    all_gather x1 -> x0, blocking collectives: 77.5 us -> none  [per_device(): lax.all_gather(requests[0], 'frames')]
    all_to_all x1, waiting for transfers between devices: 0.01 us -> 8.61 us  [per_device(): lax.all_to_all(jnp.broadcast_to(chunk_total[None], (frame_count, chunk)),...]
    all_to_all x1, starting transfers between devices: 11.1 us -> 6.08 us  [per_device(): lax.all_to_all(jnp.broadcast_to(chunk_total[None], (frame_count, chunk)),...]
    transpose x1 -> x0, local copies, waits for them, and re-layouts: 4.13 us -> none  [per_device(): spread = slot_grad.reshape(visible, frame_count, columns).transpose(1, 0, 2)]
    slice x0 -> x6, local copies, waits for them, and re-layouts: none -> 3.48 us  [the longest x3 2.81 us: per_device(): gathered[:, :visible].reshape(frame_count, owners, per_owner, columns)]
  transfers between devices with their start and end apart: 4 -> 3, of which waited for: 2 -> 3; matrix products, arithmetic and copies ran while one was open for 1% -> 1% of each run, Pallas kernels for 0% -> 0%
where the time goes in v2:
time: 232 us; the launch traced here: 231 us
  blocking collectives  94.4 us (41%)
  waiting for transfers between devices  41.4 us (18%)
  matrix products  37.3 us (16%)
  local copies, waits for them, and re-layouts  26.9 us (12%)
  starting transfers between devices  20.5 us (9%)
  other arithmetic  9.27 us (4%)
    all_to_all x1, blocking collectives, per_device(): lax.all_to_all(spread, 'frames', split_axis=0, concat_axis=0, tiled=True)  72.6 us
    all_to_all x1, waiting for transfers between devices, per_device(): lax.all_to_all(served, 'tex', split_axis=0, concat_axis=0, tiled=True)  28.8 us
    all_to_all x1, blocking collectives, per_device(): lax.all_to_all(partial, 'tex', 0, 0, tiled=True)  21.8 us
    dot_general x2, matrix products, backward(): jnp.einsum('rzs,rsu->rzu', gradient_portion, texture_lookup, preferred_el...  14.5 us
    dot_general x2, matrix products, forward(): jnp.einsum('qfm,qzm->qfz', selected_entries, texture_lookup, preferred_el...  12.1 us
    all_to_all x1, starting transfers between devices, per_device(): lax.all_to_all(wanted_ids, 'tex', split_axis=0, concat_axis=0, tiled=True)  10.9 us
    all_to_all x1, waiting for transfers between devices, per_device(): lax.all_to_all(jnp.broadcast_to(chunk_total[None], (frame_count, chunk)),...  8.61 us
    dot_general x2, matrix products, backward(): jnp.einsum('gv,gct->vct', selector, texel_gradient, precision=lax.Precisi...  7.51 us
  transfers between devices with their start and end apart: 3, of which 3 were waited for; matrix products, arithmetic and copies ran while one was open for 1% of the time, Pallas kernels for 0%

profile of v2, /device:TPU:1, one launch (start us, length us, event | category | flops | bytes accessed | tf_op | source)
XLA Modules:
  0.0 230.9 jit_solution(14899733210795449664)
XLA Ops:
  3.3 10.9 %all-to-all-start = ((s32[8,1,4]{2,1,0:T(1,128)}), s32[8,1,4]{2,1,0:T(1,128)S(1)}, u32[]{:S(2)}, u32[]{:S(2)}) async-start(s32[8,1,4]{2,1,0:T(1,128)} %bitcast.12), calls=%async_computation | async-start | bytes 8192 | tf_op jit(solution)/shard_map/all_to_all | solution.py:120
  16.7 3.9 %all-to-all-done = s32[8,1,4]{2,1,0:T(1,128)S(1)} async-done(((s32[8,1,4]{2,1,0:T(1,128)}), s32[8,1,4]{2,1,0:T(1,128)S(1)}, u32[]{:S(2)}, u32[]{:S(2)}) %all-to-all-start) | async-done | bytes 160 | tf_op jit(solution)/shard_map/all_to_all | solution.py:120
  24.1 2.7 %broadcast_select_fusion = bf16[8,4,16384]{2,1,0:T(4,128)(2,1)} fusion(bf16[8,4,16384]{2,1,0:T(4,128)(2,1)} %gather.11, pred[8,4]{1,0:T(8,128)(4,1)S(1)} %copy.24), kind=kLoop, calls=%fused_computation.61 | loop fusion | flops 524288 | bytes 2097184 | tf_op jit(solution)/shard_map/jit(_take)/select_n | solution.py:121
  26.8 3.6 %all-to-all-start.1 = ((bf16[8,4,16384]{2,1,0:T(4,128)(2,1)}), bf16[8,4,16384]{2,1,0:T(4,128)(2,1)S(1)}, u32[]{:S(2)}, u32[]{:S(2)}) async-start(bf16[8,4,16384]{2,1,0:T(4,128)(2,1)} %broadcast_select_fusion), calls=%async_computation.1 | async-start | bytes 2097152 | tf_op jit(solution)/shard_map/all_to_all | solution.py:124
  30.7 28.8 %all-to-all-done.1 = bf16[8,4,16384]{2,1,0:T(4,128)(2,1)S(1)} async-done(((bf16[8,4,16384]{2,1,0:T(4,128)(2,1)}), bf16[8,4,16384]{2,1,0:T(4,128)(2,1)S(1)}, u32[]{:S(2)}, u32[]{:S(2)}) %all-to-all-start.1) | async-done | bytes 1048608 | tf_op jit(solution)/shard_map/all_to_all | solution.py:124
  59.5 1.6 reshape.391
  61.1 16.0 %while.21 = (s32[]{:T(128)}, bf16[2,16,16,128]{3,2,1,0:T(8,128)(2,1)S(1)}, s32[2,16]{1,0:T(2,128)S(1)}, bf16[32,16,1024]{2,1,0:T(8,128)(2,1)}, s32[2,4,2048]{2,1...) while((s32[]{:T(128)}, ...), condition=%wide.region_1.2_spmd, body=%wide.region_0.1_spmd.sunk | while | flops 92570768 | bytes 1840141 | solution.py:71
  61.2 1.8 gather_fusion
  63.0 6.1 %fusion.57 = bf16[2,16,16,128]{3,2,1,0:T(8,128)(2,1)S(1)} fusion(bf16[2,16,16,128]{3,2,1,0:T(8,128)(2,1)S(1)} %get-tuple-element.286, s32[]{:T(128)} %get-tuple-element.285, f32[16,128]{1,0:T(8,128)S(1)} %bitcast.216, s32[16,128]{1,0:T(8,128)S(1)} %bitcast.220, f32[16,128]{1,0:T(8,128)S(1)} %bitcast.214, s32[16,128]{1,0:T(8,128)S(1)} %bitcast.218, ...), kind=kOutput, calls=%fused_computation.11.clone.1 | convolution fusion | flops 92569600 | bytes 655876 | tf_op jit(solution)/shard_map/while/body/eval_jaxpr/qfm,qzm->qfz/dot_general | solution.py:66
  69.2 1.8 gather_fusion
  71.0 6.1 %fusion.57 = bf16[2,16,16,128]{3,2,1,0:T(8,128)(2,1)S(1)} fusion(bf16[2,16,16,128]{3,2,1,0:T(8,128)(2,1)S(1)} %get-tuple-element.286, s32[]{:T(128)} %get-tuple-element.285, f32[16,128]{1,0:T(8,128)S(1)} %bitcast.216, s32[16,128]{1,0:T(8,128)S(1)} %bitcast.220, f32[16,128]{1,0:T(8,128)S(1)} %bitcast.214, s32[16,128]{1,0:T(8,128)S(1)} %bitcast.218, ...), kind=kOutput, calls=%fused_computation.11.clone.1 | convolution fusion | flops 92569600 | bytes 655876 | tf_op jit(solution)/shard_map/while/body/eval_jaxpr/qfm,qzm->qfz/dot_general | solution.py:66
  81.5 22.2 %while.22 = (s32[]{:T(128)}, f32[32,16,1024]{2,0,1:T(8,128)}, s32[2,16]{1,0:T(2,128)S(1)}, bf16[2,16,16,128]{3,2,1,0:T(8,128)(2,1)S(1)}, s32[2,4,2048]{2,1,0:T(4...) while((s32[]{:T(128)}, f32[32,16,1024]{2,0,1:T(8,128)}, ...), condition=%wide.region_3.4_spmd.clone, body=%wide.region_2.3_spmd.clone.sunk | while | flops 193987072 | bytes 6553987 | solution.py:108
  81.6 7.3 %fusion.61 = f32[16,16,1024]{2,1,0:T(8,128)S(1)} fusion(f32[16,128]{1,0:T(8,128)S(1)} %bitcast.224, s32[16,128]{1,0:T(8,128)S(1)} %bitcast.228, f32[16,128]{1,0:T(8,128)S(1)} %bitcast.222, s32[16,128]{1,0:T(8,128)S(1)} %bitcast.226, f32[16,128]{1,0:T(8,128)S(1)} %bitcast.223, s32[16,128]{1,0:T(8,128)S(1)} %bitcast.227, f32[16,128]{1,0:T(8,128)S(1)} %bitcast.221, ...), kind=kOutput, calls=%fused_computation.36.clone.1 | convolution fusion | flops 92274688 | bytes 1179652 | tf_op jit(solution)/shard_map/while/body/eval_jaxpr/rzs,rsu->rzu/dot_general | solution.py:100
  88.9 3.0 %select_add_fusion.2 = f32[32,16,1024]{2,0,1:T(8,128)} fusion(f32[32,16,1024]{2,0,1:T(8,128)} %get-tuple-element.319, f32[16,16,1024]{2,1,0:T(8,128)S(1)} %fusion.61, pred[]{:T(512)S(6)} %compare.13, s32[16]{0:T(128)S(1)} %fusion.62), kind=kOutput, calls=%fused_computation.37.clone.1 | convolution fusion | flops 101712384 | bytes 5242945 | tf_op jit(solution)/shard_map/while/body/eval_jaxpr/gv,gct->vct/dot_general | solution.py:104
  91.9 7.3 %fusion.61 = f32[16,16,1024]{2,1,0:T(8,128)S(1)} fusion(f32[16,128]{1,0:T(8,128)S(1)} %bitcast.224, s32[16,128]{1,0:T(8,128)S(1)} %bitcast.228, f32[16,128]{1,0:T(8,128)S(1)} %bitcast.222, s32[16,128]{1,0:T(8,128)S(1)} %bitcast.226, f32[16,128]{1,0:T(8,128)S(1)} %bitcast.223, s32[16,128]{1,0:T(8,128)S(1)} %bitcast.227, f32[16,128]{1,0:T(8,128)S(1)} %bitcast.221, ...), kind=kOutput, calls=%fused_computation.36.clone.1 | convolution fusion | flops 92274688 | bytes 1179652 | tf_op jit(solution)/shard_map/while/body/eval_jaxpr/rzs,rsu->rzu/dot_general | solution.py:100
  99.2 4.5 %select_add_fusion.2 = f32[32,16,1024]{2,0,1:T(8,128)} fusion(f32[32,16,1024]{2,0,1:T(8,128)} %get-tuple-element.319, f32[16,16,1024]{2,1,0:T(8,128)S(1)} %fusion.61, pred[]{:T(512)S(6)} %compare.13, s32[16]{0:T(128)S(1)} %fusion.62), kind=kOutput, calls=%fused_computation.37.clone.1 | convolution fusion | flops 101712384 | bytes 5242945 | tf_op jit(solution)/shard_map/while/body/eval_jaxpr/gv,gct->vct/dot_general | solution.py:104
  103.7 4.1 %copy.28 = f32[32,16,1024]{2,1,0:T(8,128)} copy(f32[32,16,1024]{2,0,1:T(8,128)} %get-tuple-element.73) | data formatting | bytes 4194304 | tf_op jit(solution)/shard_map/while | solution.py:108
  107.9 2.9 %reshape_reshape.4 = f32[32,64,256]{2,1,0:T(8,128)} reshape(f32[32,16,1024]{2,1,0:T(8,128)} %copy.28) | data formatting | bytes 4194304 | tf_op jit(solution)/shard_map/reshape;reshape | solution.py:146
  110.8 1.8 pad_maximum_fusion
  113.9 72.6 %all_to_all.30 = f32[64,33,256]{2,1,0:T(8,128)S(1)} all-to-all(f32[64,33,256]{2,1,0:T(8,128)S(1)} %copy.29), channel_id=1, replica_groups=mesh['frames'=64,'tex'=8] {'frames'}, dimensions={0} | all-to-all | bytes 4325376 | tf_op jit(solution)/shard_map/all_to_all | solution.py:148
  188.4 1.6 slice-done
  192.3 21.8 %all_to_all.31 = f32[8,65,256]{2,1,0:T(8,128)S(1)} all-to-all(f32[8,65,256]{2,1,0:T(8,128)S(1)} %pad_maximum_fusion.1), channel_id=1, replica_groups=mesh['frames'=64,'tex'=8] {'tex'}, dimensions={0} | all-to-all | bytes 1064960 | tf_op jit(solution)/shard_map/all_to_all | solution.py:164
  214.8 6.1 %all-to-all-start.4 = ((f32[64,1,72]{2,1,0:T(1,128)}), f32[64,1,72]{2,1,0:T(1,128)S(1)}, u32[]{:S(2)}, u32[]{:S(2)}) async-start(f32[64,1,72]{2,1,0:T(1,128)} %broadcast_in_dim.138), calls=%async_computation.4 | async-start | bytes 65536 | tf_op jit(solution)/shard_map/all_to_all | solution.py:167
  221.5 8.6 %all-to-all-done.4 = f32[64,1,72]{2,1,0:T(1,128)S(1)} async-done(((f32[64,1,72]{2,1,0:T(1,128)}), f32[64,1,72]{2,1,0:T(1,128)S(1)}, u32[]{:S(2)}, u32[]{:S(2)}) %all-to-all-start.4) | async-done | bytes 18464 | tf_op jit(solution)/shard_map/all_to_all | solution.py:167
  (97 shorter events, 21.0 us)
Async XLA Ops:
  0.6 20.8 %copy-start = (bf16[64,16384]{1,0:T(8,128)(2,1)S(1)}, bf16[64,16384]{1,0:T(8,128)(2,1)}, u32[]{:S(2)}) copy-start(bf16[64,16384]{1,0:T(8,128)(2,1)} %param.11) | copy-start | bytes 6291460
  3.3 17.3 %all-to-all-start = ((s32[8,1,4]{2,1,0:T(1,128)}), s32[8,1,4]{2,1,0:T(1,128)S(1)}, u32[]{:S(2)}, u32[]{:S(2)}) async-start(s32[8,1,4]{2,1,0:T(1,128)} %bitcast.12), calls=%async_computation | async-start | bytes 8192 | tf_op jit(solution)/shard_map/all_to_all | solution.py:120
  24.1 6.3 %copy-start.3 = (s32[1,4096]{1,0:T(1,128)S(1)}, s32[1,4096]{1,0:T(1,128)}, u32[]{:S(2)}) copy-start(s32[1,4096]{1,0:T(1,128)} %param.14) | copy-start | bytes 49156
  26.8 32.7 %all-to-all-start.1 = ((bf16[8,4,16384]{2,1,0:T(4,128)(2,1)}), bf16[8,4,16384]{2,1,0:T(4,128)(2,1)S(1)}, u32[]{:S(2)}, u32[]{:S(2)}) async-start(bf16[8,4,16384]{2,1,0:T(4,128)(2,1)} %broadcast_select_fusion), calls=%async_computation.1 | async-start | bytes 2097152 | tf_op jit(solution)/shard_map/all_to_all | solution.py:124
  77.1 0.9 copy-start.2
  77.1 1.0 copy-start.4
  186.6 1.5 copy-start.1
  188.4 1.6 slice-start
  214.8 15.3 %all-to-all-start.4 = ((f32[64,1,72]{2,1,0:T(1,128)}), f32[64,1,72]{2,1,0:T(1,128)S(1)}, u32[]{:S(2)}, u32[]{:S(2)}) async-start(f32[64,1,72]{2,1,0:T(1,128)} %broadcast_in_dim.138), calls=%async_computation.4 | async-start | bytes 65536 | tf_op jit(solution)/shard_map/all_to_all | solution.py:167

commit v3 on v2

--- a/solution.py
+++ b/solution.py
@@ -133,24 +133,29 @@
     weight_size = weight_local.size
     chunk = -(-weight_size // frame_count)
     request_count = requests.shape[1]
-    extra = -(-(chunk + request_count) // columns)
     weight_rows = jnp.pad(weight_local.reshape(-1), (0, chunk * frame_count - weight_size))
+    weight_rows = weight_rows.reshape(frame_count, chunk)
+    weight_high = weight_rows.astype(jnp.bfloat16)
+    weight_low = (weight_rows - weight_high.astype(jnp.float32)).astype(jnp.bfloat16)
+    extra = -(-(2 * chunk + request_count) // columns)
     side_row = jnp.concatenate(
         [
-            weight_rows.reshape(frame_count, chunk),
-            jnp.broadcast_to(requests.astype(jnp.float32), (frame_count, request_count)),
-            jnp.zeros((frame_count, extra * columns - chunk - request_count), jnp.float32),
+            weight_high,
+            weight_low,
+            jnp.broadcast_to(requests.astype(jnp.bfloat16), (frame_count, request_count)),
+            jnp.zeros((frame_count, extra * columns - 2 * chunk - request_count), jnp.bfloat16),
         ],
         axis=1,
     ).reshape(frame_count, extra, columns)
     spread = slot_grad.reshape(visible, frame_count, columns).transpose(1, 0, 2)
-    spread = jnp.concatenate([spread, side_row], axis=1)
+    spread = jnp.concatenate([spread.astype(jnp.bfloat16), side_row], axis=1)
     gathered = lax.all_to_all(spread, "frames", split_axis=0, concat_axis=0, tiled=True)
-    side = gathered[:, visible:].reshape(frame_count, extra * columns)
-    frame_weight = jnp.sum(side[:, :chunk], axis=0)
-    senders = side[:, chunk : chunk + request_count].astype(jnp.int32)
+    side = gathered[:, visible:].reshape(frame_count, extra * columns).astype(jnp.float32)
+    frame_weight = jnp.sum(side[:, :chunk] + side[:, chunk : 2 * chunk], axis=0)
+    senders = side[:, 2 * chunk : 2 * chunk + request_count].astype(jnp.int32)
     senders = senders.reshape(frame_count, owners, per_owner)
-    gathered = gathered[:, :visible].reshape(frame_count, owners, per_owner, columns)
+    gathered = gathered[:, :visible].astype(jnp.float32)
+    gathered = gathered.reshape(frame_count, owners, per_owner, columns)
     tile_numbers = jnp.arange(tile_count, dtype=jnp.int32)
     selector = (senders[None] == tile_numbers[:, None, None, None]).astype(jnp.float32)
     partial = jnp.einsum(

time: 232 us -> 195 us (0.84)
  blocking collectives: 94.4 us -> 66.4 us
  local copies, waits for them, and re-layouts: 26.9 us -> 18.9 us
    all_to_all x1, blocking collectives: 72.6 us -> 44.6 us  [per_device(): lax.all_to_all(spread, 'frames', split_axis=0, concat_axis=0, tiled=True)]
    while x1 -> x0, local copies, waits for them, and re-layouts: 4.12 us -> none  [render_one(): lax.scan(backward, start, (taps_grouped, weights_grouped, slots_grouped,...]
    convert_element_type x0 -> x2, local copies, waits for them, and re-layouts: none -> 3.25 us  [per_device(): spread = jnp.concatenate([spread.astype(jnp.bfloat16), side_row], axis=1)]
    another operation x1 -> x0, local copies, waits for them, and re-layouts: 2.89 us -> none  [per_device(): spread = slot_grad.reshape(visible, frame_count, columns).transpose(1, 0, 2)]
  transfers between devices with their start and end apart: 3 -> 3, of which waited for: 3 -> 3; matrix products, arithmetic and copies ran while one was open for 1% -> 2% of each run, Pallas kernels for 0% -> 0%
where the time goes in v3:
time: 195 us; the launch traced here: 194 us
  blocking collectives  66.4 us (34%)
  waiting for transfers between devices  41.4 us (21%)
  matrix products  36.6 us (19%)
  starting transfers between devices  20.4 us (10%)
  local copies, waits for them, and re-layouts  18.9 us (10%)
  other arithmetic  9.4 us (5%)
    all_to_all x1, blocking collectives, per_device(): lax.all_to_all(spread, 'frames', split_axis=0, concat_axis=0, tiled=True)  44.6 us
    all_to_all x1, waiting for transfers between devices, per_device(): lax.all_to_all(served, 'tex', split_axis=0, concat_axis=0, tiled=True)  28.8 us
    all_to_all x1, blocking collectives, per_device(): lax.all_to_all(partial, 'tex', 0, 0, tiled=True)  21.8 us
    dot_general x2, matrix products, backward(): jnp.einsum('rzs,rsu->rzu', gradient_portion, texture_lookup, preferred_el...  14.5 us
    dot_general x2, matrix products, forward(): jnp.einsum('qfm,qzm->qfz', selected_entries, texture_lookup, preferred_el...  12.1 us
    all_to_all x1, starting transfers between devices, per_device(): lax.all_to_all(wanted_ids, 'tex', split_axis=0, concat_axis=0, tiled=True)  10.9 us
    all_to_all x1, waiting for transfers between devices, per_device(): lax.all_to_all(jnp.broadcast_to(chunk_total[None], (frame_count, chunk)),...  8.61 us
    dot_general x2, matrix products, backward(): jnp.einsum('gv,gct->vct', selector, texel_gradient, precision=lax.Precisi...  7.52 us
  transfers between devices with their start and end apart: 3, of which 3 were waited for; matrix products, arithmetic and copies ran while one was open for 2% of the time, Pallas kernels for 0%

profile of v3, /device:TPU:1, one launch (start us, length us, event | category | flops | bytes accessed | tf_op | source)
XLA Modules:
  0.0 194.2 jit_solution(16555089347331284646)
XLA Ops:
  1.2 1.5 convert_bitcast_fusion
  3.3 10.9 %all-to-all-start = ((s32[8,1,4]{2,1,0:T(1,128)}), s32[8,1,4]{2,1,0:T(1,128)S(1)}, u32[]{:S(2)}, u32[]{:S(2)}) async-start(s32[8,1,4]{2,1,0:T(1,128)} %bitcast.12), calls=%async_computation | async-start | bytes 8192 | tf_op jit(solution)/shard_map/all_to_all | solution.py:120
  16.7 3.9 %all-to-all-done = s32[8,1,4]{2,1,0:T(1,128)S(1)} async-done(((s32[8,1,4]{2,1,0:T(1,128)}), s32[8,1,4]{2,1,0:T(1,128)S(1)}, u32[]{:S(2)}, u32[]{:S(2)}) %all-to-all-start) | async-done | bytes 160 | tf_op jit(solution)/shard_map/all_to_all | solution.py:120
  24.1 2.8 %broadcast_select_fusion = bf16[8,4,16384]{2,1,0:T(4,128)(2,1)} fusion(bf16[8,4,16384]{2,1,0:T(4,128)(2,1)} %gather.11, pred[8,4]{1,0:T(8,128)(4,1)S(1)} %copy.24), kind=kLoop, calls=%fused_computation.61 | loop fusion | flops 524288 | bytes 2097184 | tf_op jit(solution)/shard_map/jit(_take)/select_n | solution.py:121
  26.8 3.6 %all-to-all-start.1 = ((bf16[8,4,16384]{2,1,0:T(4,128)(2,1)}), bf16[8,4,16384]{2,1,0:T(4,128)(2,1)S(1)}, u32[]{:S(2)}, u32[]{:S(2)}) async-start(bf16[8,4,16384]{2,1,0:T(4,128)(2,1)} %broadcast_select_fusion), calls=%async_computation.1 | async-start | bytes 2097152 | tf_op jit(solution)/shard_map/all_to_all | solution.py:124
  30.7 28.8 %all-to-all-done.1 = bf16[8,4,16384]{2,1,0:T(4,128)(2,1)S(1)} async-done(((bf16[8,4,16384]{2,1,0:T(4,128)(2,1)}), bf16[8,4,16384]{2,1,0:T(4,128)(2,1)S(1)}, u32[]{:S(2)}, u32[]{:S(2)}) %all-to-all-start.1) | async-done | bytes 1048608 | tf_op jit(solution)/shard_map/all_to_all | solution.py:124
  59.5 1.6 reshape.392
  61.1 16.0 %while.21 = (s32[]{:T(128)}, bf16[2,16,16,128]{3,2,1,0:T(8,128)(2,1)S(1)}, s32[2,16]{1,0:T(2,128)S(1)}, bf16[32,16,1024]{2,1,0:T(8,128)(2,1)}, s32[2,4,2048]{2,1...) while((s32[]{:T(128)}, ...), condition=%wide.region_1.2_spmd, body=%wide.region_0.1_spmd.sunk | while | flops 92570768 | bytes 1840141 | solution.py:71
  61.2 1.8 gather_fusion
  63.0 6.1 %fusion.58 = bf16[2,16,16,128]{3,2,1,0:T(8,128)(2,1)S(1)} fusion(bf16[2,16,16,128]{3,2,1,0:T(8,128)(2,1)S(1)} %get-tuple-element.288, s32[]{:T(128)} %get-tuple-element.287, f32[16,128]{1,0:T(8,128)S(1)} %bitcast.216, s32[16,128]{1,0:T(8,128)S(1)} %bitcast.220, f32[16,128]{1,0:T(8,128)S(1)} %bitcast.214, s32[16,128]{1,0:T(8,128)S(1)} %bitcast.218, ...), kind=kOutput, calls=%fused_computation.11.clone.1 | convolution fusion | flops 92569600 | bytes 655876 | tf_op jit(solution)/shard_map/while/body/eval_jaxpr/qfm,qzm->qfz/dot_general | solution.py:66
  69.2 1.8 gather_fusion
  71.1 6.1 %fusion.58 = bf16[2,16,16,128]{3,2,1,0:T(8,128)(2,1)S(1)} fusion(bf16[2,16,16,128]{3,2,1,0:T(8,128)(2,1)S(1)} %get-tuple-element.288, s32[]{:T(128)} %get-tuple-element.287, f32[16,128]{1,0:T(8,128)S(1)} %bitcast.216, s32[16,128]{1,0:T(8,128)S(1)} %bitcast.220, f32[16,128]{1,0:T(8,128)S(1)} %bitcast.214, s32[16,128]{1,0:T(8,128)S(1)} %bitcast.218, ...), kind=kOutput, calls=%fused_computation.11.clone.1 | convolution fusion | flops 92569600 | bytes 655876 | tf_op jit(solution)/shard_map/while/body/eval_jaxpr/qfm,qzm->qfz/dot_general | solution.py:66
  81.5 22.3 %while.22 = (s32[]{:T(128)}, f32[32,16,1024]{2,0,1:T(8,128)}, s32[2,16]{1,0:T(2,128)S(1)}, bf16[2,16,16,128]{3,2,1,0:T(8,128)(2,1)S(1)}, s32[2,4,2048]{2,1,0:T(4...) while((s32[]{:T(128)}, f32[32,16,1024]{2,0,1:T(8,128)}, ...), condition=%wide.region_3.4_spmd.clone, body=%wide.region_2.3_spmd.clone.sunk | while | flops 193987072 | bytes 6553987 | solution.py:108
  81.6 7.3 %fusion.62 = f32[16,16,1024]{2,1,0:T(8,128)S(1)} fusion(f32[16,128]{1,0:T(8,128)S(1)} %bitcast.224, s32[16,128]{1,0:T(8,128)S(1)} %bitcast.228, f32[16,128]{1,0:T(8,128)S(1)} %bitcast.222, s32[16,128]{1,0:T(8,128)S(1)} %bitcast.226, f32[16,128]{1,0:T(8,128)S(1)} %bitcast.223, s32[16,128]{1,0:T(8,128)S(1)} %bitcast.227, f32[16,128]{1,0:T(8,128)S(1)} %bitcast.221, ...), kind=kOutput, calls=%fused_computation.36.clone.1 | convolution fusion | flops 92274688 | bytes 1179652 | tf_op jit(solution)/shard_map/while/body/eval_jaxpr/rzs,rsu->rzu/dot_general | solution.py:100
  88.9 3.0 %select_add_fusion.2 = f32[32,16,1024]{2,0,1:T(8,128)} fusion(f32[32,16,1024]{2,0,1:T(8,128)} %get-tuple-element.321, f32[16,16,1024]{2,1,0:T(8,128)S(1)} %fusion.62, pred[]{:T(512)S(6)} %compare.13, s32[16]{0:T(128)S(1)} %fusion.63), kind=kOutput, calls=%fused_computation.37.clone.1 | convolution fusion | flops 101712384 | bytes 5242945 | tf_op jit(solution)/shard_map/while/body/eval_jaxpr/gv,gct->vct/dot_general | solution.py:104
  91.9 7.3 %fusion.62 = f32[16,16,1024]{2,1,0:T(8,128)S(1)} fusion(f32[16,128]{1,0:T(8,128)S(1)} %bitcast.224, s32[16,128]{1,0:T(8,128)S(1)} %bitcast.228, f32[16,128]{1,0:T(8,128)S(1)} %bitcast.222, s32[16,128]{1,0:T(8,128)S(1)} %bitcast.226, f32[16,128]{1,0:T(8,128)S(1)} %bitcast.223, s32[16,128]{1,0:T(8,128)S(1)} %bitcast.227, f32[16,128]{1,0:T(8,128)S(1)} %bitcast.221, ...), kind=kOutput, calls=%fused_computation.36.clone.1 | convolution fusion | flops 92274688 | bytes 1179652 | tf_op jit(solution)/shard_map/while/body/eval_jaxpr/rzs,rsu->rzu/dot_general | solution.py:100
  99.2 4.6 %select_add_fusion.2 = f32[32,16,1024]{2,0,1:T(8,128)} fusion(f32[32,16,1024]{2,0,1:T(8,128)} %get-tuple-element.321, f32[16,16,1024]{2,1,0:T(8,128)S(1)} %fusion.62, pred[]{:T(512)S(6)} %compare.13, s32[16]{0:T(128)S(1)} %fusion.63), kind=kOutput, calls=%fused_computation.37.clone.1 | convolution fusion | flops 101712384 | bytes 5242945 | tf_op jit(solution)/shard_map/while/body/eval_jaxpr/gv,gct->vct/dot_general | solution.py:104
  103.8 1.7 convert_element_type.86
  105.5 1.5 copy.28
  107.1 1.7 convert_element_type.87
  109.7 44.6 %all_to_all.30 = bf16[64,33,256]{2,1,0:T(8,128)(2,1)S(1)} all-to-all(bf16[64,33,256]{2,1,0:T(8,128)(2,1)S(1)} %copy.29), channel_id=1, replica_groups=mesh['frames'=64,'tex'=8] {'frames'}, dimensions={0} | all-to-all | bytes 2162688 | tf_op jit(solution)/shard_map/all_to_all | solution.py:152
  155.7 21.8 %all_to_all.31 = f32[8,65,256]{2,1,0:T(8,128)S(1)} all-to-all(f32[8,65,256]{2,1,0:T(8,128)S(1)} %pad_maximum_fusion.1), channel_id=1, replica_groups=mesh['frames'=64,'tex'=8] {'tex'}, dimensions={0} | all-to-all | bytes 1064960 | tf_op jit(solution)/shard_map/all_to_all | solution.py:169
  178.2 6.0 %all-to-all-start.4 = ((f32[64,1,72]{2,1,0:T(1,128)}), f32[64,1,72]{2,1,0:T(1,128)S(1)}, u32[]{:S(2)}, u32[]{:S(2)}) async-start(f32[64,1,72]{2,1,0:T(1,128)} %broadcast_in_dim.138), calls=%async_computation.4 | async-start | bytes 65536 | tf_op jit(solution)/shard_map/all_to_all | solution.py:172
  184.8 8.6 %all-to-all-done.4 = f32[64,1,72]{2,1,0:T(1,128)S(1)} async-done(((f32[64,1,72]{2,1,0:T(1,128)}), f32[64,1,72]{2,1,0:T(1,128)S(1)}, u32[]{:S(2)}, u32[]{:S(2)}) %all-to-all-start.4) | async-done | bytes 18464 | tf_op jit(solution)/shard_map/all_to_all | solution.py:172
  (97 shorter events, 16.3 us)
Async XLA Ops:
  0.6 20.8 %copy-start = (bf16[64,16384]{1,0:T(8,128)(2,1)S(1)}, bf16[64,16384]{1,0:T(8,128)(2,1)}, u32[]{:S(2)}) copy-start(bf16[64,16384]{1,0:T(8,128)(2,1)} %param.11) | copy-start | bytes 6291460
  3.3 17.3 %all-to-all-start = ((s32[8,1,4]{2,1,0:T(1,128)}), s32[8,1,4]{2,1,0:T(1,128)S(1)}, u32[]{:S(2)}, u32[]{:S(2)}) async-start(s32[8,1,4]{2,1,0:T(1,128)} %bitcast.12), calls=%async_computation | async-start | bytes 8192 | tf_op jit(solution)/shard_map/all_to_all | solution.py:120
  24.1 6.3 %copy-start.2 = (s32[1,4096]{1,0:T(1,128)S(1)}, s32[1,4096]{1,0:T(1,128)}, u32[]{:S(2)}) copy-start(s32[1,4096]{1,0:T(1,128)} %param.14) | copy-start | bytes 49156
  26.8 32.7 %all-to-all-start.1 = ((bf16[8,4,16384]{2,1,0:T(4,128)(2,1)}), bf16[8,4,16384]{2,1,0:T(4,128)(2,1)S(1)}, u32[]{:S(2)}, u32[]{:S(2)}) async-start(bf16[8,4,16384]{2,1,0:T(4,128)(2,1)} %broadcast_select_fusion), calls=%async_computation.1 | async-start | bytes 2097152 | tf_op jit(solution)/shard_map/all_to_all | solution.py:124
  77.1 0.9 copy-start.1
  77.1 1.0 copy-start.3
  178.2 15.3 %all-to-all-start.4 = ((f32[64,1,72]{2,1,0:T(1,128)}), f32[64,1,72]{2,1,0:T(1,128)S(1)}, u32[]{:S(2)}, u32[]{:S(2)}) async-start(f32[64,1,72]{2,1,0:T(1,128)} %broadcast_in_dim.138), calls=%async_computation.4 | async-start | bytes 65536 | tf_op jit(solution)/shard_map/all_to_all | solution.py:172

commit v4 on v3

--- a/solution.py
+++ b/solution.py
@@ -111,11 +111,56 @@
     return (rendered, slot_grad.reshape(visible, channels * texel), weight_local)
 
 
+def render_flat(fetched, slot_row, lookup, conv_weight, cot_row):
+    visible = fetched.shape[0]
+    channels = fetched.shape[1]
+    texel = fetched.shape[2]
+    height = slot_row.shape[0]
+    width = lookup.shape[1]
+    selected_entries = jnp.take(fetched, slot_row, axis=0)
+    feature_maps = jnp.einsum(
+        "qfm,qzm->fqz", selected_entries, lookup, preferred_element_type=jnp.float32
+    ).astype(jnp.bfloat16)
+    offsets = [(shift_y, shift_x) for shift_y in (-1, 0, 1) for shift_x in (-1, 0, 1)]
+    columns = jnp.concatenate(
+        [shifted(feature_maps, shift_y, shift_x) for shift_y, shift_x in offsets], axis=0
+    )
+    columns = columns.reshape(9 * channels, height * width)
+    preact = jnp.dot(conv_weight, columns, preferred_element_type=jnp.float32)
+    sigmoid_pre = jax.nn.sigmoid(preact)
+    rendered = (preact * sigmoid_pre).astype(jnp.bfloat16)
+    pre_grad = (
+        cot_row.astype(jnp.float32) * sigmoid_pre * (1.0 + preact * (1.0 - sigmoid_pre))
+    ).astype(jnp.bfloat16)
+    weight_local = jnp.einsum("op,kp->ok", pre_grad, columns, preferred_element_type=jnp.float32)
+    col_grad = jnp.einsum("ok,op->kp", conv_weight, pre_grad, preferred_element_type=jnp.float32)
+    col_grad = col_grad.reshape(9, channels, height, width)
+    feat_grad = jnp.zeros((channels, height, width), jnp.float32)
+    for number in range(9):
+        shift_y, shift_x = offsets[number]
+        feat_grad = feat_grad + shifted(col_grad[number], -shift_y, -shift_x)
+    feat_grad = feat_grad.astype(jnp.bfloat16)
+    texel_gradient = jnp.einsum(
+        "zrs,rsu->rzu", feat_grad, lookup, preferred_element_type=jnp.float32
+    )
+    slot_numbers = jnp.arange(visible, dtype=jnp.int32)
+    selector = (slot_row[:, None] == slot_numbers[None, :]).astype(jnp.float32)
+    slot_grad = jnp.einsum(
+        "gv,gct->vct", selector, texel_gradient, precision=lax.Precision.HIGHEST
+    )
+    return (rendered, slot_grad.reshape(visible, channels * texel), weight_local)
+
+
 def per_device(texture, requests, block_slot, texel_cell, uv_frac, conv_weight, cotangent):
     owners = lax.axis_size("tex")
     frame_count = lax.axis_size("frames")
     tile_count = texture.shape[0]
     tile_width = texture.shape[1]
+    texel = tile_width // CH
+    height = block_slot.shape[1]
+    texel_taps, weights = taps_and_weights(texel_cell[0], uv_frac[0], math.isqrt(texel))
+    lookup = sample_matrix(texel_taps, weights, texel).reshape(height, -1, texel)
+    lookup = lax.optimization_barrier(lookup)
     wanted_ids = requests.reshape(owners, -1)
     wanted = lax.all_to_all(wanted_ids, "tex", split_axis=0, concat_axis=0, tiled=True)
     served = jnp.take(texture, wanted.reshape(-1), axis=0).reshape(
@@ -126,8 +171,8 @@
     per_owner = fetched.shape[1]
     visible = owners * per_owner
     fetched = fetched.reshape(visible, CH, tile_width // CH)
-    rendered, slot_grad, weight_local = render_one(
-        fetched, block_slot[0], texel_cell[0], uv_frac[0], conv_weight, cotangent[0]
+    rendered, slot_grad, weight_local = render_flat(
+        fetched, block_slot[0], lookup, conv_weight, cotangent[0]
     )
     columns = tile_width // frame_count
     weight_size = weight_local.size

time: 195 us -> 176 us (0.903)
  matrix products: 36.6 us -> 16.1 us
  waiting for transfers between devices: 41.4 us -> 30.2 us
  other arithmetic: 9.4 us -> 19.6 us
  local copies, waits for them, and re-layouts: 18.9 us -> 21 us
    dot_general x9 -> x6, matrix products: 36.2 us -> 15.8 us  [the longest x1 5.93 us: render_flat(): jnp.einsum('qfm,qzm->fqz', selected_entries, lookup, preferred_element_ty...]
    all_to_all x1, waiting for transfers between devices: 28.8 us -> 18.6 us  [per_device(): lax.all_to_all(served, 'tex', split_axis=0, concat_axis=0, tiled=True)]
    convert_element_type x2 -> x1, other arithmetic: 2.22 us -> 10.5 us  [sample_matrix(): return matrix.astype(jnp.bfloat16)]
    unnamed x28 -> x21, local copies, waits for them, and re-layouts: 1.8 us -> 4.51 us
    gather x2 -> x1, local copies, waits for them, and re-layouts: 3.61 us -> 1.66 us  [render_flat(): selected_entries = jnp.take(fetched, slot_row, axis=0)]
  transfers between devices with their start and end apart: 3 -> 3, of which waited for: 3 -> 3; matrix products, arithmetic and copies ran while one was open for 2% -> 8% of each run, Pallas kernels for 0% -> 0%
where the time goes in v4:
time: 176 us; the launch traced here: 175 us
  blocking collectives  66.4 us (38%)
  waiting for transfers between devices  30.2 us (17%)
  starting transfers between devices  21.1 us (12%)
  local copies, waits for them, and re-layouts  21 us (12%)
  other arithmetic  19.6 us (11%)
  matrix products  16.1 us (9%)
    all_to_all x1, blocking collectives, per_device(): lax.all_to_all(spread, 'frames', split_axis=0, concat_axis=0, tiled=True)  44.6 us
    all_to_all x1, blocking collectives, per_device(): lax.all_to_all(partial, 'tex', 0, 0, tiled=True)  21.8 us
    all_to_all x1, waiting for transfers between devices, per_device(): lax.all_to_all(served, 'tex', split_axis=0, concat_axis=0, tiled=True)  18.6 us
    all_to_all x1, starting transfers between devices, per_device(): lax.all_to_all(wanted_ids, 'tex', split_axis=0, concat_axis=0, tiled=True)  10.9 us
    convert_element_type x1, other arithmetic, sample_matrix(): return matrix.astype(jnp.bfloat16)  10.5 us
    all_to_all x1, waiting for transfers between devices, per_device(): lax.all_to_all(jnp.broadcast_to(chunk_total[None], (frame_count, chunk)),...  7.76 us
    all_to_all x1, starting transfers between devices, per_device(): lax.all_to_all(jnp.broadcast_to(chunk_total[None], (frame_count, chunk)),...  6 us
    dot_general x1, matrix products, render_flat(): jnp.einsum('qfm,qzm->fqz', selected_entries, lookup, preferred_element_ty...  5.93 us
  transfers between devices with their start and end apart: 3, of which 3 were waited for; matrix products, arithmetic and copies ran while one was open for 8% of the time, Pallas kernels for 0%

profile of v4, /device:TPU:1, one launch (start us, length us, event | category | flops | bytes accessed | tf_op | source)
XLA Modules:
  0.0 175.3 jit_solution(5513218642732361540)
XLA Ops:
  1.2 1.5 convert_bitcast_fusion
  3.3 10.9 %all-to-all-start = ((s32[8,1,4]{2,1,0:T(1,128)}), s32[8,1,4]{2,1,0:T(1,128)S(1)}, u32[]{:S(2)}, u32[]{:S(2)}) async-start(s32[8,1,4]{2,1,0:T(1,128)} %bitcast.5), calls=%async_computation | async-start | bytes 8192 | tf_op jit(solution)/shard_map/all_to_all | solution.py:165
  16.9 3.8 %all-to-all-done = s32[8,1,4]{2,1,0:T(1,128)S(1)} async-done(((s32[8,1,4]{2,1,0:T(1,128)}), s32[8,1,4]{2,1,0:T(1,128)S(1)}, u32[]{:S(2)}, u32[]{:S(2)}) %all-to-all-start) | async-done | bytes 160 | tf_op jit(solution)/shard_map/all_to_all | solution.py:165
  21.6 1.2 gather_fusion
  22.8 1.2 gather.11
  24.0 2.7 %broadcast_select_fusion = bf16[8,4,16384]{2,1,0:T(4,128)(2,1)} fusion(bf16[8,4,16384]{2,1,0:T(4,128)(2,1)} %gather.11, pred[8,4]{1,0:T(8,128)(4,1)S(1)} %copy.20), kind=kLoop, calls=%fused_computation.22 | loop fusion | flops 524288 | bytes 2097184 | tf_op jit(solution)/shard_map/jit(_take)/select_n | solution.py:166
  26.8 4.2 %all-to-all-start.1 = ((bf16[8,4,16384]{2,1,0:T(4,128)(2,1)}), bf16[8,4,16384]{2,1,0:T(4,128)(2,1)}, u32[]{:S(2)}, u32[]{:S(2)}) async-start(bf16[8,4,16384]{2,1,0:T(4,128)(2,1)} %broadcast_select_fusion), calls=%async_computation.1 | async-start | bytes 2097152 | tf_op jit(solution)/shard_map/all_to_all | solution.py:169
  31.0 10.5 %add_convert_fusion = bf16[32,128,1024]{2,1,0:T(8,128)(2,1)} fusion(f32[32,128]{1,0:T(8,128)S(1)} %get-tuple-element.18, s32[32,128]{1,0:T(8,128)S(1)} %get-tuple-element.23, f32[32,128]{1,0:T(8,128)S(1)} %get-tuple-element.19, s32[32,128]{1,0:T(8,128)S(1)} %get-tuple-element.22, f32[32,128]{1,0:T(8,128)S(1)} %get-tuple-element.17, ...), kind=kLoop, calls=%fused_computation.2 | loop fusion | flops 50331648 | bytes 8519680 | tf_op jit(solution)/shard_map/convert_element_type | solution.py:36
  41.5 18.6 %all-to-all-done.1 = bf16[8,4,16384]{2,1,0:T(4,128)(2,1)} async-done(((bf16[8,4,16384]{2,1,0:T(4,128)(2,1)}), bf16[8,4,16384]{2,1,0:T(4,128)(2,1)}, u32[]{:S(2)}, u32[]{:S(2)}) %all-to-all-start.1) | async-done | bytes 1048608 | tf_op jit(solution)/shard_map/all_to_all | solution.py:169
  60.2 1.8 %reshape.291 = bf16[32,16,1024]{2,1,0:T(8,128)(2,1)S(1)} reshape(bf16[8,4,16384]{2,1,0:T(4,128)(2,1)} %all-to-all-done.1) | data formatting | bytes 2097152 | tf_op jit(solution)/shard_map/reshape | solution.py:173
  62.0 1.7 gather_fusion.1
  63.6 5.9 %fusion.8 = bf16[16,32,128]{2,0,1:T(8,128)(2,1)S(1)} fusion(bf16[32,128,1024]{2,1,0:T(8,128)(2,1)} %add_convert_fusion, bf16[32,16,1024]{2,1,0:T(8,128)(2,1)} %gather_fusion.1, pred[32]{0:T(512)(128)(4,1)S(1)} %compare_and_fusion.1), kind=kOutput, calls=%fused_computation.17 | convolution fusion | flops 134807552 | bytes 9568288 | tf_op jit(solution)/shard_map/qfm,qzm->fqz/dot_general | solution.py:121
  71.6 2.0 %convolution_bitcast_fusion = f32[144,4096]{1,0:T(8,128)} fusion(bf16[32,144]{1,0:T(8,128)(2,1)S(1)} %copy-done.3, f32[32,4096]{1,0:T(8,128)S(1)} %convolution_bitcast_fusion.1, bf16[1,32,4096]{2,1,0:T(8,128)(2,1)S(1)} %copy-done.2), kind=kOutput, calls=%fused_computation.7 | convolution fusion | flops 39059456 | bytes 3154944 | tf_op jit(solution)/shard_map/ok,op->kp/dot_general | solution.py:136
  73.7 1.8 slice_bitcast_fusion.4
  75.6 4.6 %fusion.27 = f32[32,16,1024]{2,1,0:T(8,128)S(1)} fusion(bf16[32,128,1024]{2,1,0:T(8,128)(2,1)} %add_convert_fusion, f32[16,32,128]{2,0,1:T(8,128)S(1)} %get-tuple-element.35, f32[16,32,128]{2,0,1:T(8,128)S(1)} %get-tuple-element.34, f32[16,32,128]{2,0,1:T(8,128)S(1)} %get-tuple-element.33, f32[16,32,128]{2,0,1:T(8,128)S(1)} %get-tuple-element.32, ...), kind=kOutput, calls=%fused_computation.76 | convolution fusion | flops 134807552 | bytes 12845056 | tf_op jit(solution)/shard_map/zrs,rsu->rzu/dot_general | solution.py:143
  80.3 2.4 %fusion.2 = bf16[32,16,1024]{2,0,1:T(8,128)(2,1)S(1)} fusion(f32[32,16,1024]{2,1,0:T(8,128)S(1)} %fusion.27, s32[32]{0:T(128)S(1)} %bitcast.114), kind=kOutput, calls=%fused_computation.11 | convolution fusion | flops 201851904 | bytes 3145856 | tf_op jit(solution)/shard_map/gv,gct->vct/dot_general | solution.py:148
  82.7 1.5 copy.32
  84.3 2.5 %convert_element_type.89 = bf16[32,64,256]{2,1,0:T(8,128)(2,1)} reshape(bf16[32,16,1024]{2,1,0:T(8,128)(2,1)} %copy.32) | data formatting | bytes 2097152 | tf_op jit(solution)/shard_map/convert_element_type | solution.py:196
  86.8 1.3 pad_maximum_fusion
  88.8 44.6 %all_to_all.30 = bf16[64,33,256]{2,1,0:T(8,128)(2,1)S(1)} all-to-all(bf16[64,33,256]{2,1,0:T(8,128)(2,1)S(1)} %copy.33), channel_id=1, replica_groups=mesh['frames'=64,'tex'=8] {'frames'}, dimensions={0} | all-to-all | bytes 2162688 | tf_op jit(solution)/shard_map/all_to_all | solution.py:197
  134.7 1.1 slice-done
  136.8 21.8 %all_to_all.31 = f32[8,65,256]{2,1,0:T(8,128)S(1)} all-to-all(f32[8,65,256]{2,1,0:T(8,128)S(1)} %pad_maximum_fusion.1), channel_id=1, replica_groups=mesh['frames'=64,'tex'=8] {'tex'}, dimensions={0} | all-to-all | bytes 1064960 | tf_op jit(solution)/shard_map/all_to_all | solution.py:214
  159.3 6.0 %all-to-all-start.4 = ((f32[64,1,72]{2,1,0:T(1,128)}), f32[64,1,72]{2,1,0:T(1,128)S(1)}, u32[]{:S(2)}, u32[]{:S(2)}) async-start(f32[64,1,72]{2,1,0:T(1,128)} %broadcast_in_dim.90), calls=%async_computation.4 | async-start | bytes 65536 | tf_op jit(solution)/shard_map/all_to_all | solution.py:217
  166.8 7.8 %all-to-all-done.4 = f32[64,1,72]{2,1,0:T(1,128)S(1)} async-done(((f32[64,1,72]{2,1,0:T(1,128)}), f32[64,1,72]{2,1,0:T(1,128)S(1)}, u32[]{:S(2)}, u32[]{:S(2)}) %all-to-all-start.4) | async-done | bytes 18464 | tf_op jit(solution)/shard_map/all_to_all | solution.py:217
  (68 shorter events, 12.9 us)
Async XLA Ops:
  0.6 21.0 %copy-start = (bf16[64,16384]{1,0:T(8,128)(2,1)S(1)}, bf16[64,16384]{1,0:T(8,128)(2,1)}, u32[]{:S(2)}) copy-start(bf16[64,16384]{1,0:T(8,128)(2,1)} %param.7) | copy-start | bytes 6291460
  3.3 17.3 %all-to-all-start = ((s32[8,1,4]{2,1,0:T(1,128)}), s32[8,1,4]{2,1,0:T(1,128)S(1)}, u32[]{:S(2)}, u32[]{:S(2)}) async-start(s32[8,1,4]{2,1,0:T(1,128)} %bitcast.5), calls=%async_computation | async-start | bytes 8192 | tf_op jit(solution)/shard_map/all_to_all | solution.py:165
  26.8 33.4 %all-to-all-start.1 = ((bf16[8,4,16384]{2,1,0:T(4,128)(2,1)}), bf16[8,4,16384]{2,1,0:T(4,128)(2,1)}, u32[]{:S(2)}, u32[]{:S(2)}) async-start(bf16[8,4,16384]{2,1,0:T(4,128)(2,1)} %broadcast_select_fusion), calls=%async_computation.1 | async-start | bytes 2097152 | tf_op jit(solution)/shard_map/all_to_all | solution.py:169
  31.0 10.5 %copy-start.4 = (s32[1,32]{1,0:T(1,128)S(1)}, s32[1,32]{1,0:T(1,128)}, u32[]{:S(2)}) copy-start(s32[1,32]{1,0:T(1,128)} %param.9) | copy-start | bytes 388
  69.6 0.9 copy-start.3
  70.1 1.0 copy-start.2
  133.3 1.1 copy-start.1
  134.6 1.2 slice-start
  159.3 15.3 %all-to-all-start.4 = ((f32[64,1,72]{2,1,0:T(1,128)}), f32[64,1,72]{2,1,0:T(1,128)S(1)}, u32[]{:S(2)}, u32[]{:S(2)}) async-start(f32[64,1,72]{2,1,0:T(1,128)} %broadcast_in_dim.90), calls=%async_computation.4 | async-start | bytes 65536 | tf_op jit(solution)/shard_map/all_to_all | solution.py:217

commit v5 on v4

--- a/solution.py
+++ b/solution.py
@@ -206,14 +206,24 @@
     partial = jnp.einsum(
         "qfoj,fojc->oqc", selector, gathered, precision=lax.Precision.HIGHEST
     )
-    weight_tail = -(-chunk // columns) * columns
-    weight_block = jnp.pad(frame_weight, (0, weight_tail - chunk)).reshape(1, -1, columns)
+    weight_high = frame_weight.astype(jnp.bfloat16)
+    weight_low = (frame_weight - weight_high.astype(jnp.float32)).astype(jnp.bfloat16)
+    weight_tail = -(-(2 * chunk) // columns) * columns
+    weight_block = jnp.pad(
+        jnp.concatenate([weight_high, weight_low]), (0, weight_tail - 2 * chunk)
+    ).reshape(1, -1, columns)
     partial = jnp.concatenate(
-        [partial, jnp.broadcast_to(weight_block, (owners,) + weight_block.shape[1:])], axis=1
-    )
-    collected = jnp.sum(lax.all_to_all(partial, "tex", 0, 0, tiled=True), axis=0)
+        [
+            partial.astype(jnp.bfloat16),
+            jnp.broadcast_to(weight_block, (owners,) + weight_block.shape[1:]),
+        ],
+        axis=1,
+    )
+    received = lax.all_to_all(partial, "tex", 0, 0, tiled=True).astype(jnp.float32)
+    collected = jnp.sum(received, axis=0)
     texture_grad = collected[:tile_count]
-    chunk_total = collected[tile_count:].reshape(-1)[:chunk]
+    weight_pair = collected[tile_count:].reshape(-1)
+    chunk_total = weight_pair[:chunk] + weight_pair[chunk : 2 * chunk]
     shared = lax.all_to_all(
         jnp.broadcast_to(chunk_total[None], (frame_count, chunk)), "frames", 0, 0, tiled=True
     )

time: 176 us -> 170 us (0.966)
  blocking collectives: 66.4 us -> 60 us
    all_to_all x1, blocking collectives: 21.8 us -> 15.5 us  [per_device(): lax.all_to_all(partial, 'tex', 0, 0, tiled=True).astype(jnp.float32)]
  transfers between devices with their start and end apart: 3 -> 3, of which waited for: 3 -> 3; matrix products, arithmetic and copies ran while one was open for 8% -> 9% of each run, Pallas kernels for 0% -> 0%
where the time goes in v5:
time: 170 us; the launch traced here: 169 us
  blocking collectives  60 us (35%)
  waiting for transfers between devices  30.2 us (18%)
  starting transfers between devices  21.1 us (12%)
  local copies, waits for them, and re-layouts  21 us (12%)
  other arithmetic  19.7 us (12%)
  matrix products  16.1 us (9%)
    all_to_all x1, blocking collectives, per_device(): lax.all_to_all(spread, 'frames', split_axis=0, concat_axis=0, tiled=True)  44.6 us
    all_to_all x1, waiting for transfers between devices, per_device(): lax.all_to_all(served, 'tex', split_axis=0, concat_axis=0, tiled=True)  18.6 us
    all_to_all x1, blocking collectives, per_device(): lax.all_to_all(partial, 'tex', 0, 0, tiled=True).astype(jnp.float32)  15.5 us
    all_to_all x1, starting transfers between devices, per_device(): lax.all_to_all(wanted_ids, 'tex', split_axis=0, concat_axis=0, tiled=True)  10.9 us
    convert_element_type x1, other arithmetic, sample_matrix(): return matrix.astype(jnp.bfloat16)  10.5 us
    all_to_all x1, waiting for transfers between devices, per_device(): lax.all_to_all(jnp.broadcast_to(chunk_total[None], (frame_count, chunk)),...  7.76 us
    all_to_all x1, starting transfers between devices, per_device(): lax.all_to_all(jnp.broadcast_to(chunk_total[None], (frame_count, chunk)),...  6.01 us
    dot_general x1, matrix products, render_flat(): jnp.einsum('qfm,qzm->fqz', selected_entries, lookup, preferred_element_ty...  5.93 us
  transfers between devices with their start and end apart: 3, of which 3 were waited for; matrix products, arithmetic and copies ran while one was open for 9% of the time, Pallas kernels for 0%

profile of v5, /device:TPU:1, one launch (start us, length us, event | category | flops | bytes accessed | tf_op | source)
XLA Modules:
  0.0 169.2 jit_solution(16307232965685690841)
XLA Ops:
  1.2 1.5 convert_bitcast_fusion
  3.3 10.9 %all-to-all-start = ((s32[8,1,4]{2,1,0:T(1,128)}), s32[8,1,4]{2,1,0:T(1,128)S(1)}, u32[]{:S(2)}, u32[]{:S(2)}) async-start(s32[8,1,4]{2,1,0:T(1,128)} %bitcast.5), calls=%async_computation | async-start | bytes 8192 | tf_op jit(solution)/shard_map/all_to_all | solution.py:165
  16.9 3.8 %all-to-all-done = s32[8,1,4]{2,1,0:T(1,128)S(1)} async-done(((s32[8,1,4]{2,1,0:T(1,128)}), s32[8,1,4]{2,1,0:T(1,128)S(1)}, u32[]{:S(2)}, u32[]{:S(2)}) %all-to-all-start) | async-done | bytes 160 | tf_op jit(solution)/shard_map/all_to_all | solution.py:165
  21.6 1.2 gather_fusion
  22.8 1.2 gather.11
  24.1 2.7 %broadcast_select_fusion = bf16[8,4,16384]{2,1,0:T(4,128)(2,1)} fusion(bf16[8,4,16384]{2,1,0:T(4,128)(2,1)} %gather.11, pred[8,4]{1,0:T(8,128)(4,1)S(1)} %copy.20), kind=kLoop, calls=%fused_computation.23 | loop fusion | flops 524288 | bytes 2097184 | tf_op jit(solution)/shard_map/jit(_take)/select_n | solution.py:166
  26.8 4.3 %all-to-all-start.1 = ((bf16[8,4,16384]{2,1,0:T(4,128)(2,1)}), bf16[8,4,16384]{2,1,0:T(4,128)(2,1)}, u32[]{:S(2)}, u32[]{:S(2)}) async-start(bf16[8,4,16384]{2,1,0:T(4,128)(2,1)} %broadcast_select_fusion), calls=%async_computation.1 | async-start | bytes 2097152 | tf_op jit(solution)/shard_map/all_to_all | solution.py:169
  31.0 10.5 %add_convert_fusion = bf16[32,128,1024]{2,1,0:T(8,128)(2,1)} fusion(f32[32,128]{1,0:T(8,128)S(1)} %get-tuple-element.18, s32[32,128]{1,0:T(8,128)S(1)} %get-tuple-element.23, f32[32,128]{1,0:T(8,128)S(1)} %get-tuple-element.19, s32[32,128]{1,0:T(8,128)S(1)} %get-tuple-element.22, f32[32,128]{1,0:T(8,128)S(1)} %get-tuple-element.17, ...), kind=kLoop, calls=%fused_computation.2 | loop fusion | flops 50331648 | bytes 8519680 | tf_op jit(solution)/shard_map/convert_element_type | solution.py:36
  41.6 18.6 %all-to-all-done.1 = bf16[8,4,16384]{2,1,0:T(4,128)(2,1)} async-done(((bf16[8,4,16384]{2,1,0:T(4,128)(2,1)}), bf16[8,4,16384]{2,1,0:T(4,128)(2,1)}, u32[]{:S(2)}, u32[]{:S(2)}) %all-to-all-start.1) | async-done | bytes 1048608 | tf_op jit(solution)/shard_map/all_to_all | solution.py:169
  60.2 1.8 %reshape.291 = bf16[32,16,1024]{2,1,0:T(8,128)(2,1)S(1)} reshape(bf16[8,4,16384]{2,1,0:T(4,128)(2,1)} %all-to-all-done.1) | data formatting | bytes 2097152 | tf_op jit(solution)/shard_map/reshape | solution.py:173
  62.0 1.7 gather_fusion.1
  63.7 5.9 %fusion.9 = bf16[16,32,128]{2,0,1:T(8,128)(2,1)S(1)} fusion(bf16[32,128,1024]{2,1,0:T(8,128)(2,1)} %add_convert_fusion, bf16[32,16,1024]{2,1,0:T(8,128)(2,1)} %gather_fusion.1, pred[32]{0:T(512)(128)(4,1)S(1)} %compare_and_fusion.1), kind=kOutput, calls=%fused_computation.18 | convolution fusion | flops 134807552 | bytes 9568288 | tf_op jit(solution)/shard_map/qfm,qzm->fqz/dot_general | solution.py:121
  71.6 2.0 %convolution_bitcast_fusion = f32[144,4096]{1,0:T(8,128)} fusion(bf16[32,144]{1,0:T(8,128)(2,1)S(1)} %copy-done.3, f32[32,4096]{1,0:T(8,128)S(1)} %convolution_bitcast_fusion.1, bf16[1,32,4096]{2,1,0:T(8,128)(2,1)S(1)} %copy-done.2), kind=kOutput, calls=%fused_computation.7 | convolution fusion | flops 39059456 | bytes 3154944 | tf_op jit(solution)/shard_map/ok,op->kp/dot_general | solution.py:136
  73.7 1.8 %slice_bitcast_fusion.4 = (f32[2,32,8,128]{3,2,1,0:T(8,128)S(1)}, f32[2,32,8,128]{3,2,1,0:T(8,128)S(1)}, f32[2,32,8,128]{3,2,1,0:T(8,128)S(1)}, f32[2,32,8,128]{...) fusion(f32[144,4096]{1,0:T(8,128)} %convolution_bitcast_fusion), kind=kLoop, calls=%fused_computation.72 | loop fusion | bytes 4718592
  75.7 4.6 %fusion.28 = f32[32,16,1024]{2,1,0:T(8,128)S(1)} fusion(bf16[32,128,1024]{2,1,0:T(8,128)(2,1)} %add_convert_fusion, f32[16,32,128]{2,0,1:T(8,128)S(1)} %get-tuple-element.37, f32[16,32,128]{2,0,1:T(8,128)S(1)} %get-tuple-element.36, f32[16,32,128]{2,0,1:T(8,128)S(1)} %get-tuple-element.35, f32[16,32,128]{2,0,1:T(8,128)S(1)} %get-tuple-element.34, ...), kind=kOutput, calls=%fused_computation.78 | convolution fusion | flops 134807552 | bytes 12845056 | tf_op jit(solution)/shard_map/zrs,rsu->rzu/dot_general | solution.py:143
  80.3 2.4 %fusion.2 = bf16[32,16,1024]{2,0,1:T(8,128)(2,1)S(1)} fusion(f32[32,16,1024]{2,1,0:T(8,128)S(1)} %fusion.28, s32[32]{0:T(128)S(1)} %bitcast.116), kind=kOutput, calls=%fused_computation.11 | convolution fusion | flops 201851904 | bytes 3145856 | tf_op jit(solution)/shard_map/gv,gct->vct/dot_general | solution.py:148
  82.8 1.5 copy.32
  84.3 2.5 %convert_element_type.104 = bf16[32,64,256]{2,1,0:T(8,128)(2,1)} reshape(bf16[32,16,1024]{2,1,0:T(8,128)(2,1)} %copy.32) | data formatting | bytes 2097152 | tf_op jit(solution)/shard_map/convert_element_type | solution.py:196
  86.9 1.3 pad_maximum_fusion
  88.8 44.6 %all_to_all.30 = bf16[64,33,256]{2,1,0:T(8,128)(2,1)S(1)} all-to-all(bf16[64,33,256]{2,1,0:T(8,128)(2,1)S(1)} %copy.33), channel_id=1, replica_groups=mesh['frames'=64,'tex'=8] {'frames'}, dimensions={0} | all-to-all | bytes 2162688 | tf_op jit(solution)/shard_map/all_to_all | solution.py:197
  134.8 1.1 slice-done
  136.9 15.5 %all_to_all.31 = bf16[8,65,256]{2,1,0:T(8,128)(2,1)S(1)} all-to-all(bf16[8,65,256]{2,1,0:T(8,128)(2,1)S(1)} %pad_maximum_fusion.1), channel_id=1, replica_groups=mesh['frames'=64,'tex'=8] {'tex'}, dimensions={0} | all-to-all | bytes 532480 | tf_op jit(solution)/shard_map/all_to_all | solution.py:222
  153.1 6.0 %all-to-all-start.4 = ((f32[64,1,72]{2,1,0:T(1,128)}), f32[64,1,72]{2,1,0:T(1,128)S(1)}, u32[]{:S(2)}, u32[]{:S(2)}) async-start(f32[64,1,72]{2,1,0:T(1,128)} %broadcast_in_dim.90), calls=%async_computation.4 | async-start | bytes 65536 | tf_op jit(solution)/shard_map/all_to_all | solution.py:227
  160.6 7.8 %all-to-all-done.4 = f32[64,1,72]{2,1,0:T(1,128)S(1)} async-done(((f32[64,1,72]{2,1,0:T(1,128)}), f32[64,1,72]{2,1,0:T(1,128)S(1)}, u32[]{:S(2)}, u32[]{:S(2)}) %all-to-all-start.4) | async-done | bytes 18464 | tf_op jit(solution)/shard_map/all_to_all | solution.py:227
  (69 shorter events, 13.1 us)
Async XLA Ops:
  0.6 21.0 %copy-start = (bf16[64,16384]{1,0:T(8,128)(2,1)S(1)}, bf16[64,16384]{1,0:T(8,128)(2,1)}, u32[]{:S(2)}) copy-start(bf16[64,16384]{1,0:T(8,128)(2,1)} %param.7) | copy-start | bytes 6291460
  3.3 17.3 %all-to-all-start = ((s32[8,1,4]{2,1,0:T(1,128)}), s32[8,1,4]{2,1,0:T(1,128)S(1)}, u32[]{:S(2)}, u32[]{:S(2)}) async-start(s32[8,1,4]{2,1,0:T(1,128)} %bitcast.5), calls=%async_computation | async-start | bytes 8192 | tf_op jit(solution)/shard_map/all_to_all | solution.py:165
  26.8 33.4 %all-to-all-start.1 = ((bf16[8,4,16384]{2,1,0:T(4,128)(2,1)}), bf16[8,4,16384]{2,1,0:T(4,128)(2,1)}, u32[]{:S(2)}, u32[]{:S(2)}) async-start(bf16[8,4,16384]{2,1,0:T(4,128)(2,1)} %broadcast_select_fusion), calls=%async_computation.1 | async-start | bytes 2097152 | tf_op jit(solution)/shard_map/all_to_all | solution.py:169
  31.0 10.5 %copy-start.4 = (s32[1,32]{1,0:T(1,128)S(1)}, s32[1,32]{1,0:T(1,128)}, u32[]{:S(2)}) copy-start(s32[1,32]{1,0:T(1,128)} %param.9) | copy-start | bytes 388
  69.6 0.9 copy-start.3
  70.2 1.0 copy-start.2
  133.4 1.1 copy-start.1
  134.6 1.2 slice-start
  153.1 15.3 %all-to-all-start.4 = ((f32[64,1,72]{2,1,0:T(1,128)}), f32[64,1,72]{2,1,0:T(1,128)S(1)}, u32[]{:S(2)}, u32[]{:S(2)}) async-start(f32[64,1,72]{2,1,0:T(1,128)} %broadcast_in_dim.90), calls=%async_computation.4 | async-start | bytes 65536 | tf_op jit(solution)/shard_map/all_to_all | solution.py:227

commit v6 on v5

--- a/solution.py
+++ b/solution.py
@@ -117,7 +117,7 @@
     texel = fetched.shape[2]
     height = slot_row.shape[0]
     width = lookup.shape[1]
-    selected_entries = jnp.take(fetched, slot_row, axis=0)
+    selected_entries = jnp.take(fetched, slot_row, axis=0, mode="clip")
     feature_maps = jnp.einsum(
         "qfm,qzm->fqz", selected_entries, lookup, preferred_element_type=jnp.float32
     ).astype(jnp.bfloat16)
@@ -163,14 +163,13 @@
     lookup = lax.optimization_barrier(lookup)
     wanted_ids = requests.reshape(owners, -1)
     wanted = lax.all_to_all(wanted_ids, "tex", split_axis=0, concat_axis=0, tiled=True)
-    served = jnp.take(texture, wanted.reshape(-1), axis=0).reshape(
-        wanted.shape[0], wanted.shape[1], tile_width
-    )
-    returned_tiles = lax.all_to_all(served, "tex", split_axis=0, concat_axis=0, tiled=True)
-    fetched = returned_tiles
-    per_owner = fetched.shape[1]
+    per_owner = wanted.shape[1]
     visible = owners * per_owner
-    fetched = fetched.reshape(visible, CH, tile_width // CH)
+    served = jnp.take(
+        texture.reshape(tile_count, CH, texel), wanted.reshape(-1), axis=0, mode="clip"
+    ).reshape(owners, per_owner * CH, texel)
+    fetched = lax.all_to_all(served, "tex", split_axis=0, concat_axis=0, tiled=True)
+    fetched = fetched.reshape(visible, CH, texel)
     rendered, slot_grad, weight_local = render_flat(
         fetched, block_slot[0], lookup, conv_weight, cotangent[0]
     )

time: 170 us -> 155 us (0.912)
  local copies, waits for them, and re-layouts: 21 us -> 13.3 us
  other arithmetic: 19.7 us -> 15.7 us
  waiting for transfers between devices: 30.2 us -> 27.5 us
  matrix products: 16.1 us -> 14.4 us
    all_to_all x1, waiting for transfers between devices: 3.82 us -> 1.03 us  [per_device(): lax.all_to_all(wanted_ids, 'tex', split_axis=0, concat_axis=0, tiled=True)]
    convert_element_type x2, local copies, waits for them, and re-layouts: 4.03 us -> 1.25 us  [per_device(): spread = jnp.concatenate([spread.astype(jnp.bfloat16), side_row], axis=1)]
    select_n x3 -> x0, other arithmetic: 2.72 us -> none  [the longest x2 2.72 us: per_device(): jnp.take(texture, wanted.reshape(-1), axis=0)]
    reshape x2 -> x0, local copies, waits for them, and re-layouts: 1.88 us -> none  [the longest x1 1.81 us: per_device(): fetched = fetched.reshape(visible, CH, tile_width // CH)]
    gather x3 -> x2, local copies, waits for them, and re-layouts: 4.09 us -> 2.27 us  [the longest x1 1.66 us: per_device(): jnp.take(texture.reshape(tile_count, CH, texel), wanted.reshape(-1), axis...]
    unnamed x21 -> x18, local copies, waits for them, and re-layouts: 4.5 us -> 4.31 us
  transfers between devices with their start and end apart: 3 -> 3, of which waited for: 3 -> 3; matrix products, arithmetic and copies ran while one was open for 9% -> 11% of each run, Pallas kernels for 0% -> 0%
where the time goes in v6:
time: 155 us; the launch traced here: 154 us
  blocking collectives  60.2 us (39%)
  waiting for transfers between devices  27.5 us (18%)
  starting transfers between devices  22.5 us (15%)
  other arithmetic  15.7 us (10%)
  matrix products  14.4 us (9%)
  local copies, waits for them, and re-layouts  13.3 us (9%)
    all_to_all x1, blocking collectives, per_device(): lax.all_to_all(spread, 'frames', split_axis=0, concat_axis=0, tiled=True)  44.7 us
    all_to_all x1, waiting for transfers between devices, per_device(): lax.all_to_all(served, 'tex', split_axis=0, concat_axis=0, tiled=True)  18.7 us
    all_to_all x1, blocking collectives, per_device(): lax.all_to_all(partial, 'tex', 0, 0, tiled=True).astype(jnp.float32)  15.5 us
    all_to_all x1, starting transfers between devices, per_device(): lax.all_to_all(wanted_ids, 'tex', split_axis=0, concat_axis=0, tiled=True)  10.9 us
    convert_element_type x1, other arithmetic, sample_matrix(): return matrix.astype(jnp.bfloat16)  10.5 us
    all_to_all x1, waiting for transfers between devices, per_device(): lax.all_to_all(jnp.broadcast_to(chunk_total[None], (frame_count, chunk)),...  7.76 us
    all_to_all x1, starting transfers between devices, per_device(): lax.all_to_all(jnp.broadcast_to(chunk_total[None], (frame_count, chunk)),...  6 us
    dot_general x1, matrix products, render_flat(): jnp.einsum('qfm,qzm->fqz', selected_entries, lookup, preferred_element_ty...  5.66 us
  transfers between devices with their start and end apart: 3, of which 3 were waited for; matrix products, arithmetic and copies ran while one was open for 11% of the time, Pallas kernels for 0%

profile of v6, /device:TPU:1, one launch (start us, length us, event | category | flops | bytes accessed | tf_op | source)
XLA Modules:
  0.0 154.4 jit_solution(9297810821621414355)
XLA Ops:
  1.2 1.4 convert_bitcast_fusion
  2.6 0.7 all_to_all.19
  3.2 10.9 %all-to-all-start = ((s32[8,1,4]{2,1,0:T(1,128)}), s32[8,1,4]{2,1,0:T(1,128)S(1)}, u32[]{:S(2)}, u32[]{:S(2)}) async-start(s32[8,1,4]{2,1,0:T(1,128)} %bitcast.4), calls=%async_computation | async-start | bytes 8192 | tf_op jit(solution)/shard_map/all_to_all | solution.py:165
  14.1 0.8 compare_reduce_fusion
  14.9 0.8 broadcast_divide_fusion
  15.7 0.9 fusion.49
  16.7 2.8 %copy.42 = bf16[8,8,16,1024]{3,2,1,0:T(8,128)(2,1)S(1)} copy(bf16[8,8,16,1024]{3,1,2,0:T(8,128)(2,1)} %bitcast.106) | data formatting | bytes 4194304
  19.5 1.0 all-to-all-done
  20.6 0.7 reduce.13
  21.3 1.7 %gather_fusion = bf16[32,16,1024]{2,1,0:T(8,128)(2,1)} fusion(bf16[64,16,1024]{2,1,0:T(8,128)(2,1)S(1)} %bitcast.103, s32[1024]{0:T(1024)S(1)} %pad_clamp_fusion.1), kind=kCustom, calls=%fused_computation | custom fusion | bytes 2097280 | tf_op jit(solution)/shard_map/jit(_take)/gather | solution.py:168
  23.0 5.6 %all-to-all-start.1 = ((bf16[8,64,1024]{2,1,0:T(8,128)(2,1)}), bf16[8,64,1024]{2,1,0:T(8,128)(2,1)S(1)}, u32[]{:S(2)}, u32[]{:S(2)}) async-start(bf16[8,64,1024]{2,1,0:T(8,128)(2,1)} %bitcast.5), calls=%async_computation.1 | async-start | bytes 2097152 | tf_op jit(solution)/shard_map/all_to_all | solution.py:171
  28.6 10.5 %add_convert_fusion = bf16[32,128,1024]{2,1,0:T(8,128)(2,1)} fusion(f32[32,128]{1,0:T(8,128)S(1)} %get-tuple-element.18, s32[32,128]{1,0:T(8,128)S(1)} %get-tuple-element.23, f32[32,128]{1,0:T(8,128)S(1)} %get-tuple-element.19, s32[32,128]{1,0:T(8,128)S(1)} %get-tuple-element.22, f32[32,128]{1,0:T(8,128)S(1)} %get-tuple-element.17, ...), kind=kLoop, calls=%fused_computation.2 | loop fusion | flops 50331648 | bytes 8519680 | tf_op jit(solution)/shard_map/convert_element_type | solution.py:36
  39.1 18.7 %all-to-all-done.1 = bf16[8,64,1024]{2,1,0:T(8,128)(2,1)S(1)} async-done(((bf16[8,64,1024]{2,1,0:T(8,128)(2,1)}), bf16[8,64,1024]{2,1,0:T(8,128)(2,1)S(1)}, u32[]{:S(2)}, u32[]{:S(2)}) %all-to-all-start.1) | async-done | bytes 1048608 | tf_op jit(solution)/shard_map/all_to_all | solution.py:171
  58.4 5.7 %fusion.9 = bf16[16,32,128]{2,0,1:T(8,128)(2,1)S(1)} fusion(bf16[32,128,1024]{2,1,0:T(8,128)(2,1)} %add_convert_fusion, bf16[32,16,1024]{2,1,0:T(8,128)(2,1)S(1)} %gather_fusion.1), kind=kOutput, calls=%fused_computation.18 | convolution fusion | flops 134283264 | bytes 9568256 | tf_op jit(solution)/shard_map/qfm,qzm->fqz/dot_general | solution.py:121
  66.7 4.6 %fusion.25 = f32[32,16,1024]{2,1,0:T(8,128)S(1)} fusion(bf16[32,128,1024]{2,1,0:T(8,128)(2,1)} %add_convert_fusion, f32[16,32,128]{2,0,1:T(8,128)S(1)} %get-tuple-element.37, f32[16,32,128]{2,0,1:T(8,128)S(1)} %get-tuple-element.36, f32[16,32,128]{2,0,1:T(8,128)S(1)} %get-tuple-element.35, f32[16,32,128]{2,0,1:T(8,128)S(1)} %get-tuple-element.34, ...), kind=kOutput, calls=%fused_computation.74 | convolution fusion | flops 134807552 | bytes 12845056 | tf_op jit(solution)/shard_map/zrs,rsu->rzu/dot_general | solution.py:143
  71.4 2.4 %fusion.2 = bf16[32,16,1024]{2,0,1:T(8,128)(2,1)S(1)} fusion(f32[32,16,1024]{2,1,0:T(8,128)S(1)} %fusion.25, s32[32]{0:T(128)S(1)} %bitcast.114), kind=kOutput, calls=%fused_computation.11 | convolution fusion | flops 201851904 | bytes 3145856 | tf_op jit(solution)/shard_map/gv,gct->vct/dot_general | solution.py:148
  74.4 0.7 convert_element_type.104
  75.9 44.7 %all_to_all.30 = bf16[64,33,256]{2,1,0:T(8,128)(2,1)S(1)} all-to-all(bf16[64,33,256]{2,1,0:T(8,128)(2,1)S(1)} %copy.27), channel_id=1, replica_groups=mesh['frames'=64,'tex'=8] {'frames'}, dimensions={0} | all-to-all | bytes 2162688 | tf_op jit(solution)/shard_map/all_to_all | solution.py:196
  122.1 15.5 %all_to_all.31 = bf16[8,65,256]{2,1,0:T(8,128)(2,1)S(1)} all-to-all(bf16[8,65,256]{2,1,0:T(8,128)(2,1)S(1)} %pad_maximum_fusion.1), channel_id=1, replica_groups=mesh['frames'=64,'tex'=8] {'tex'}, dimensions={0} | all-to-all | bytes 532480 | tf_op jit(solution)/shard_map/all_to_all | solution.py:221
  137.7 0.6 broadcast_in_dim.76
  138.4 6.0 %all-to-all-start.4 = ((f32[64,1,72]{2,1,0:T(1,128)}), f32[64,1,72]{2,1,0:T(1,128)S(1)}, u32[]{:S(2)}, u32[]{:S(2)}) async-start(f32[64,1,72]{2,1,0:T(1,128)} %broadcast_in_dim.76), calls=%async_computation.4 | async-start | bytes 65536 | tf_op jit(solution)/shard_map/all_to_all | solution.py:226
  144.4 0.8 fusion.24
  145.9 7.8 %all-to-all-done.4 = f32[64,1,72]{2,1,0:T(1,128)S(1)} async-done(((f32[64,1,72]{2,1,0:T(1,128)}), f32[64,1,72]{2,1,0:T(1,128)S(1)}, u32[]{:S(2)}, u32[]{:S(2)}) %all-to-all-start.4) | async-done | bytes 18464 | tf_op jit(solution)/shard_map/all_to_all | solution.py:226
  153.7 0.7 mul.76
  (56 shorter events, 7.6 us)
Async XLA Ops:
  0.6 64.3 %copy-start = (bf16[32,144]{1,0:T(8,128)(2,1)S(1)}, bf16[32,144]{1,0:T(8,128)(2,1)}, u32[]{:S(2)}) copy-start(bf16[32,144]{1,0:T(8,128)(2,1)} %param.12) | copy-start | bytes 27652
  3.2 17.3 %all-to-all-start = ((s32[8,1,4]{2,1,0:T(1,128)}), s32[8,1,4]{2,1,0:T(1,128)S(1)}, u32[]{:S(2)}, u32[]{:S(2)}) async-start(s32[8,1,4]{2,1,0:T(1,128)} %bitcast.4), calls=%async_computation | async-start | bytes 8192 | tf_op jit(solution)/shard_map/all_to_all | solution.py:165
  23.0 34.8 %all-to-all-start.1 = ((bf16[8,64,1024]{2,1,0:T(8,128)(2,1)}), bf16[8,64,1024]{2,1,0:T(8,128)(2,1)S(1)}, u32[]{:S(2)}, u32[]{:S(2)}) async-start(bf16[8,64,1024]{2,1,0:T(8,128)(2,1)} %bitcast.5), calls=%async_computation.1 | async-start | bytes 2097152 | tf_op jit(solution)/shard_map/all_to_all | solution.py:171
  28.6 10.5 %copy-start.2 = (s32[1,32]{1,0:T(1,128)S(1)}, s32[1,32]{1,0:T(1,128)}, u32[]{:S(2)}) copy-start(s32[1,32]{1,0:T(1,128)} %param.9) | copy-start | bytes 388
  64.1 1.2 copy-start.1
  138.4 15.3 %all-to-all-start.4 = ((f32[64,1,72]{2,1,0:T(1,128)}), f32[64,1,72]{2,1,0:T(1,128)S(1)}, u32[]{:S(2)}, u32[]{:S(2)}) async-start(f32[64,1,72]{2,1,0:T(1,128)} %broadcast_in_dim.76), calls=%async_computation.4 | async-start | bytes 65536 | tf_op jit(solution)/shard_map/all_to_all | solution.py:226

commit v7 on v6

--- a/solution.py
+++ b/solution.py
@@ -160,9 +160,9 @@
     height = block_slot.shape[1]
     texel_taps, weights = taps_and_weights(texel_cell[0], uv_frac[0], math.isqrt(texel))
     lookup = sample_matrix(texel_taps, weights, texel).reshape(height, -1, texel)
-    lookup = lax.optimization_barrier(lookup)
     wanted_ids = requests.reshape(owners, -1)
     wanted = lax.all_to_all(wanted_ids, "tex", split_axis=0, concat_axis=0, tiled=True)
+    lookup, wanted = lax.optimization_barrier((lookup, wanted))
     per_owner = wanted.shape[1]
     visible = owners * per_owner
     served = jnp.take(

time: 155 us -> 163 us (1.052)
  waiting for transfers between devices: 27.5 us -> 36.8 us
    all_to_all x1, waiting for transfers between devices: 18.7 us -> 29 us  [per_device(): lax.all_to_all(served, 'tex', split_axis=0, concat_axis=0, tiled=True)]
    unnamed x18 -> x20, local copies, waits for them, and re-layouts: 4.31 us -> 2.73 us
  transfers between devices with their start and end apart: 3 -> 3, of which waited for: 3 -> 2; matrix products, arithmetic and copies ran while one was open for 11% -> 10% of each run, Pallas kernels for 0% -> 0%
where the time goes in v7:
time: 163 us
  blocking collectives  60.2 us (37%)
  waiting for transfers between devices  36.8 us (23%)
  starting transfers between devices  23.5 us (14%)
  other arithmetic  15 us (9%)
  matrix products  14.4 us (9%)
  local copies, waits for them, and re-layouts  11.9 us (7%)
    all_to_all x1, blocking collectives, per_device(): lax.all_to_all(spread, 'frames', split_axis=0, concat_axis=0, tiled=True)  44.7 us
    all_to_all x1, waiting for transfers between devices, per_device(): lax.all_to_all(served, 'tex', split_axis=0, concat_axis=0, tiled=True)  29 us
    all_to_all x1, blocking collectives, per_device(): lax.all_to_all(partial, 'tex', 0, 0, tiled=True).astype(jnp.float32)  15.5 us
    all_to_all x1, starting transfers between devices, per_device(): lax.all_to_all(wanted_ids, 'tex', split_axis=0, concat_axis=0, tiled=True)  10.9 us
    convert_element_type x1, other arithmetic, sample_matrix(): return matrix.astype(jnp.bfloat16)  10.5 us
    all_to_all x1, waiting for transfers between devices, per_device(): lax.all_to_all(jnp.broadcast_to(chunk_total[None], (frame_count, chunk)),...  7.76 us
    all_to_all x1, starting transfers between devices, per_device(): lax.all_to_all(served, 'tex', split_axis=0, concat_axis=0, tiled=True)  6.65 us
    all_to_all x1, starting transfers between devices, per_device(): lax.all_to_all(jnp.broadcast_to(chunk_total[None], (frame_count, chunk)),...  6.01 us
  transfers between devices with their start and end apart: 3, of which 2 were waited for; matrix products, arithmetic and copies ran while one was open for 10% of the time, Pallas kernels for 0%

profile of v7, /device:TPU:1, one launch (start us, length us, event | category | flops | bytes accessed | tf_op | source)
XLA Modules:
  0.0 162.7 jit_solution(9371832332373598350)
XLA Ops:
  1.2 1.4 convert_bitcast_fusion
  2.6 0.7 all_to_all.21
  3.2 10.9 %all-to-all-start = ((s32[8,1,4]{2,1,0:T(1,128)}), s32[8,1,4]{2,1,0:T(1,128)S(1)}, u32[]{:S(2)}, u32[]{:S(2)}) async-start(s32[8,1,4]{2,1,0:T(1,128)} %bitcast.4), calls=%async_computation | async-start | bytes 8192 | tf_op jit(solution)/shard_map/all_to_all | solution.py:164
  14.1 0.8 compare_reduce_fusion
  14.9 0.8 broadcast_divide_fusion
  15.7 0.9 fusion.49
  16.6 10.5 %add_convert_fusion = bf16[32,128,1024]{2,1,0:T(8,128)(2,1)} fusion(f32[32,128]{1,0:T(8,128)S(1)} %get-tuple-element.22, s32[32,128]{1,0:T(8,128)S(1)} %get-tuple-element.27, f32[32,128]{1,0:T(8,128)S(1)} %get-tuple-element.23, s32[32,128]{1,0:T(8,128)S(1)} %get-tuple-element.26, f32[32,128]{1,0:T(8,128)S(1)} %get-tuple-element.21, ...), kind=kLoop, calls=%fused_computation.2 | loop fusion | flops 50331648 | bytes 8519680 | tf_op jit(solution)/shard_map/convert_element_type | solution.py:36
  27.1 1.2 copy.48
  28.6 1.7 %gather_fusion = bf16[32,16,1024]{2,1,0:T(8,128)(2,1)} fusion(bf16[64,16,1024]{2,1,0:T(8,128)(2,1)S(1)} %bitcast.104, s32[1024]{0:T(1024)S(1)} %pad_clamp_fusion.1), kind=kCustom, calls=%fused_computation | custom fusion | bytes 2097280 | tf_op jit(solution)/shard_map/jit(_take)/gather | solution.py:168
  30.3 6.6 %all-to-all-start.1 = ((bf16[8,64,1024]{2,1,0:T(8,128)(2,1)}), bf16[8,64,1024]{2,1,0:T(8,128)(2,1)S(1)}, u32[]{:S(2)}, u32[]{:S(2)}) async-start(bf16[8,64,1024]{2,1,0:T(8,128)(2,1)} %bitcast.6), calls=%async_computation.1 | async-start | bytes 2097152 | tf_op jit(solution)/shard_map/all_to_all | solution.py:171
  37.1 29.0 %all-to-all-done.1 = bf16[8,64,1024]{2,1,0:T(8,128)(2,1)S(1)} async-done(((bf16[8,64,1024]{2,1,0:T(8,128)(2,1)}), bf16[8,64,1024]{2,1,0:T(8,128)(2,1)S(1)}, u32[]{:S(2)}, u32[]{:S(2)}) %all-to-all-start.1) | async-done | bytes 1048608 | tf_op jit(solution)/shard_map/all_to_all | solution.py:171
  66.7 5.7 %fusion.9 = bf16[16,32,128]{2,0,1:T(8,128)(2,1)S(1)} fusion(bf16[32,128,1024]{2,1,0:T(8,128)(2,1)} %add_convert_fusion, bf16[32,16,1024]{2,1,0:T(8,128)(2,1)S(1)} %gather_fusion.1), kind=kOutput, calls=%fused_computation.18 | convolution fusion | flops 134283264 | bytes 9568256 | tf_op jit(solution)/shard_map/qfm,qzm->fqz/dot_general | solution.py:121
  75.0 4.6 %fusion.25 = f32[32,16,1024]{2,1,0:T(8,128)S(1)} fusion(bf16[32,128,1024]{2,1,0:T(8,128)(2,1)} %add_convert_fusion, f32[16,32,128]{2,0,1:T(8,128)S(1)} %get-tuple-element.41, f32[16,32,128]{2,0,1:T(8,128)S(1)} %get-tuple-element.40, f32[16,32,128]{2,0,1:T(8,128)S(1)} %get-tuple-element.39, f32[16,32,128]{2,0,1:T(8,128)S(1)} %get-tuple-element.38, ...), kind=kOutput, calls=%fused_computation.74 | convolution fusion | flops 134807552 | bytes 12845056 | tf_op jit(solution)/shard_map/zrs,rsu->rzu/dot_general | solution.py:143
  79.7 2.4 %fusion.2 = bf16[32,16,1024]{2,0,1:T(8,128)(2,1)S(1)} fusion(f32[32,16,1024]{2,1,0:T(8,128)S(1)} %fusion.25, s32[32]{0:T(128)S(1)} %bitcast.116), kind=kOutput, calls=%fused_computation.11 | convolution fusion | flops 201851904 | bytes 3145856 | tf_op jit(solution)/shard_map/gv,gct->vct/dot_general | solution.py:148
  82.7 0.7 convert_element_type.104
  83.6 0.6 copy.33
  84.2 44.7 %all_to_all.33 = bf16[64,33,256]{2,1,0:T(8,128)(2,1)S(1)} all-to-all(bf16[64,33,256]{2,1,0:T(8,128)(2,1)S(1)} %copy.33), channel_id=1, replica_groups=mesh['frames'=64,'tex'=8] {'frames'}, dimensions={0} | all-to-all | bytes 2162688 | tf_op jit(solution)/shard_map/all_to_all | solution.py:196
  130.5 15.5 %all_to_all.34 = bf16[8,65,256]{2,1,0:T(8,128)(2,1)S(1)} all-to-all(bf16[8,65,256]{2,1,0:T(8,128)(2,1)S(1)} %pad_maximum_fusion.1), channel_id=1, replica_groups=mesh['frames'=64,'tex'=8] {'tex'}, dimensions={0} | all-to-all | bytes 532480 | tf_op jit(solution)/shard_map/all_to_all | solution.py:221
  146.1 0.6 broadcast_in_dim.76
  146.7 6.0 %all-to-all-start.4 = ((f32[64,1,72]{2,1,0:T(1,128)}), f32[64,1,72]{2,1,0:T(1,128)S(1)}, u32[]{:S(2)}, u32[]{:S(2)}) async-start(f32[64,1,72]{2,1,0:T(1,128)} %broadcast_in_dim.76), calls=%async_computation.4 | async-start | bytes 65536 | tf_op jit(solution)/shard_map/all_to_all | solution.py:226
  152.7 0.8 fusion.24
  153.6 0.6 slice.176
  154.2 7.8 %all-to-all-done.4 = f32[64,1,72]{2,1,0:T(1,128)S(1)} async-done(((f32[64,1,72]{2,1,0:T(1,128)}), f32[64,1,72]{2,1,0:T(1,128)S(1)}, u32[]{:S(2)}, u32[]{:S(2)}) %all-to-all-start.4) | async-done | bytes 18464 | tf_op jit(solution)/shard_map/all_to_all | solution.py:226
  162.1 0.7 mul.76
  (59 shorter events, 6.5 us)
Async XLA Ops:
  0.6 72.6 %copy-start = (bf16[32,144]{1,0:T(8,128)(2,1)S(1)}, bf16[32,144]{1,0:T(8,128)(2,1)}, u32[]{:S(2)}) copy-start(bf16[32,144]{1,0:T(8,128)(2,1)} %param.12) | copy-start | bytes 27652
  3.2 25.1 %all-to-all-start = ((s32[8,1,4]{2,1,0:T(1,128)}), s32[8,1,4]{2,1,0:T(1,128)S(1)}, u32[]{:S(2)}, u32[]{:S(2)}) async-start(s32[8,1,4]{2,1,0:T(1,128)} %bitcast.4), calls=%async_computation | async-start | bytes 8192 | tf_op jit(solution)/shard_map/all_to_all | solution.py:164
  16.6 10.5 %copy-start.1 = (bf16[64,16384]{1,0:T(8,128)(2,1)S(1)}, bf16[64,16384]{1,0:T(8,128)(2,1)}, u32[]{:S(2)}) copy-start(bf16[64,16384]{1,0:T(8,128)(2,1)} %param.7) | copy-start | bytes 6291460
  28.6 8.5 %copy-start.3 = (s32[1,32]{1,0:T(1,128)S(1)}, s32[1,32]{1,0:T(1,128)}, u32[]{:S(2)}) copy-start(s32[1,32]{1,0:T(1,128)} %param.9) | copy-start | bytes 388
  30.3 35.8 %all-to-all-start.1 = ((bf16[8,64,1024]{2,1,0:T(8,128)(2,1)}), bf16[8,64,1024]{2,1,0:T(8,128)(2,1)S(1)}, u32[]{:S(2)}, u32[]{:S(2)}) async-start(bf16[8,64,1024]{2,1,0:T(8,128)(2,1)} %bitcast.6), calls=%async_computation.1 | async-start | bytes 2097152 | tf_op jit(solution)/shard_map/all_to_all | solution.py:171
  72.4 1.2 copy-start.2
  146.7 15.3 %all-to-all-start.4 = ((f32[64,1,72]{2,1,0:T(1,128)}), f32[64,1,72]{2,1,0:T(1,128)S(1)}, u32[]{:S(2)}, u32[]{:S(2)}) async-start(f32[64,1,72]{2,1,0:T(1,128)} %broadcast_in_dim.76), calls=%async_computation.4 | async-start | bytes 65536 | tf_op jit(solution)/shard_map/all_to_all | solution.py:226

commit v8 on v6

--- a/solution.py
+++ b/solution.py
@@ -6,6 +6,7 @@
 from jax.sharding import PartitionSpec as P
 
 CH = 16
+LANE = 128
 
 
 def taps_and_weights(cell_row, frac_row, side):
@@ -190,15 +191,17 @@
             jnp.zeros((frame_count, extra * columns - 2 * chunk - request_count), jnp.bfloat16),
         ],
         axis=1,
-    ).reshape(frame_count, extra, columns)
+    ).reshape(frame_count, extra * columns // LANE, LANE)
     spread = slot_grad.reshape(visible, frame_count, columns).transpose(1, 0, 2)
-    spread = jnp.concatenate([spread.astype(jnp.bfloat16), side_row], axis=1)
+    spread = spread.astype(jnp.bfloat16).reshape(frame_count, visible * columns // LANE, LANE)
+    spread = jnp.concatenate([spread, side_row], axis=1)
     gathered = lax.all_to_all(spread, "frames", split_axis=0, concat_axis=0, tiled=True)
-    side = gathered[:, visible:].reshape(frame_count, extra * columns).astype(jnp.float32)
+    grad_rows = visible * columns // LANE
+    side = gathered[:, grad_rows:].reshape(frame_count, extra * columns).astype(jnp.float32)
     frame_weight = jnp.sum(side[:, :chunk] + side[:, chunk : 2 * chunk], axis=0)
     senders = side[:, 2 * chunk : 2 * chunk + request_count].astype(jnp.int32)
     senders = senders.reshape(frame_count, owners, per_owner)
-    gathered = gathered[:, :visible].astype(jnp.float32)
+    gathered = gathered[:, :grad_rows].astype(jnp.float32)
     gathered = gathered.reshape(frame_count, owners, per_owner, columns)
     tile_numbers = jnp.arange(tile_count, dtype=jnp.int32)
     selector = (senders[None] == tile_numbers[:, None, None, None]).astype(jnp.float32)
@@ -210,18 +213,19 @@
     weight_tail = -(-(2 * chunk) // columns) * columns
     weight_block = jnp.pad(
         jnp.concatenate([weight_high, weight_low]), (0, weight_tail - 2 * chunk)
-    ).reshape(1, -1, columns)
+    ).reshape(1, -1, LANE)
     partial = jnp.concatenate(
         [
-            partial.astype(jnp.bfloat16),
+            partial.astype(jnp.bfloat16).reshape(owners, tile_count * columns // LANE, LANE),
             jnp.broadcast_to(weight_block, (owners,) + weight_block.shape[1:]),
         ],
         axis=1,
     )
     received = lax.all_to_all(partial, "tex", 0, 0, tiled=True).astype(jnp.float32)
     collected = jnp.sum(received, axis=0)
-    texture_grad = collected[:tile_count]
-    weight_pair = collected[tile_count:].reshape(-1)
+    tile_rows = tile_count * columns // LANE
+    texture_grad = collected[:tile_rows].reshape(tile_count, columns)
+    weight_pair = collected[tile_rows:].reshape(-1)
     chunk_total = weight_pair[:chunk] + weight_pair[chunk : 2 * chunk]
     shared = lax.all_to_all(
         jnp.broadcast_to(chunk_total[None], (frame_count, chunk)), "frames", 0, 0, tiled=True

time: 155 us -> 153 us (0.987)
  blocking collectives: 60.2 us -> 56.7 us
    all_to_all x1, blocking collectives: 44.7 us -> 41.7 us  [per_device(): lax.all_to_all(spread, 'frames', split_axis=0, concat_axis=0, tiled=True)]
    reshape x0 -> x6, local copies, waits for them, and re-layouts: none -> 1.86 us  [the longest x1 0.71 us: per_device(): gathered = gathered.reshape(frame_count, owners, per_owner, columns)]
    unnamed x18 -> x19, local copies, waits for them, and re-layouts: 4.31 us -> 4.25 us
where the time goes in v8:
time: 153 us
  blocking collectives  56.7 us (37%)
  waiting for transfers between devices  27.4 us (18%)
  starting transfers between devices  22.7 us (15%)
  other arithmetic  15.7 us (10%)
  matrix products  15.4 us (10%)
  local copies, waits for them, and re-layouts  13.9 us (9%)
    all_to_all x1, blocking collectives, per_device(): lax.all_to_all(spread, 'frames', split_axis=0, concat_axis=0, tiled=True)  41.7 us
    all_to_all x1, waiting for transfers between devices, per_device(): lax.all_to_all(served, 'tex', split_axis=0, concat_axis=0, tiled=True)  18.7 us
    all_to_all x1, blocking collectives, per_device(): lax.all_to_all(partial, 'tex', 0, 0, tiled=True).astype(jnp.float32)  15 us
    all_to_all x1, starting transfers between devices, per_device(): lax.all_to_all(wanted_ids, 'tex', split_axis=0, concat_axis=0, tiled=True)  10.9 us
    convert_element_type x1, other arithmetic, sample_matrix(): return matrix.astype(jnp.bfloat16)  10.5 us
    all_to_all x1, waiting for transfers between devices, per_device(): lax.all_to_all(jnp.broadcast_to(chunk_total[None], (frame_count, chunk)),...  7.74 us
    all_to_all x1, starting transfers between devices, per_device(): lax.all_to_all(jnp.broadcast_to(chunk_total[None], (frame_count, chunk)),...  6.21 us
    dot_general x1, matrix products, render_flat(): jnp.einsum('qfm,qzm->fqz', selected_entries, lookup, preferred_element_ty...  5.66 us
  transfers between devices with their start and end apart: 3, of which 3 were waited for; matrix products, arithmetic and copies ran while one was open for 11% of the time, Pallas kernels for 0%

profile of v8, /device:TPU:1, one launch (start us, length us, event | category | flops | bytes accessed | tf_op | source)
XLA Modules:
  0.0 152.8 jit_solution(3740871765861905767)
XLA Ops:
  1.2 1.4 convert_bitcast_fusion
  2.6 0.7 all_to_all.19
  3.2 10.9 %all-to-all-start = ((s32[8,1,4]{2,1,0:T(1,128)}), s32[8,1,4]{2,1,0:T(1,128)S(1)}, u32[]{:S(2)}, u32[]{:S(2)}) async-start(s32[8,1,4]{2,1,0:T(1,128)} %bitcast.4), calls=%async_computation | async-start | bytes 8192 | tf_op jit(solution)/shard_map/all_to_all | solution.py:166
  14.1 0.8 compare_reduce_fusion
  14.9 0.8 broadcast_divide_fusion
  15.7 0.9 fusion.50
  16.7 2.8 %copy.59 = bf16[8,8,16,1024]{3,2,1,0:T(8,128)(2,1)S(1)} copy(bf16[8,8,16,1024]{3,1,2,0:T(8,128)(2,1)} %bitcast.105) | data formatting | bytes 4194304
  19.5 1.0 all-to-all-done
  21.3 1.7 %gather_fusion = bf16[32,16,1024]{2,1,0:T(8,128)(2,1)} fusion(bf16[64,16,1024]{2,1,0:T(8,128)(2,1)S(1)} %bitcast.102, s32[1024]{0:T(1024)S(1)} %pad_clamp_fusion.1), kind=kCustom, calls=%fused_computation | custom fusion | bytes 2097280 | tf_op jit(solution)/shard_map/jit(_take)/gather | solution.py:169
  23.0 5.6 %all-to-all-start.1 = ((bf16[8,64,1024]{2,1,0:T(8,128)(2,1)}), bf16[8,64,1024]{2,1,0:T(8,128)(2,1)S(1)}, u32[]{:S(2)}, u32[]{:S(2)}) async-start(bf16[8,64,1024]{2,1,0:T(8,128)(2,1)} %bitcast.5), calls=%async_computation.1 | async-start | bytes 2097152 | tf_op jit(solution)/shard_map/all_to_all | solution.py:172
  28.6 10.5 %add_convert_fusion = bf16[32,128,1024]{2,1,0:T(8,128)(2,1)} fusion(f32[32,128]{1,0:T(8,128)S(1)} %get-tuple-element.18, s32[32,128]{1,0:T(8,128)S(1)} %get-tuple-element.23, f32[32,128]{1,0:T(8,128)S(1)} %get-tuple-element.19, s32[32,128]{1,0:T(8,128)S(1)} %get-tuple-element.22, f32[32,128]{1,0:T(8,128)S(1)} %get-tuple-element.17, ...), kind=kLoop, calls=%fused_computation.2 | loop fusion | flops 50331648 | bytes 8519680 | tf_op jit(solution)/shard_map/convert_element_type | solution.py:37
  39.1 18.7 %all-to-all-done.1 = bf16[8,64,1024]{2,1,0:T(8,128)(2,1)S(1)} async-done(((bf16[8,64,1024]{2,1,0:T(8,128)(2,1)}), bf16[8,64,1024]{2,1,0:T(8,128)(2,1)S(1)}, u32[]{:S(2)}, u32[]{:S(2)}) %all-to-all-start.1) | async-done | bytes 1048608 | tf_op jit(solution)/shard_map/all_to_all | solution.py:172
  58.4 5.7 %fusion.9 = bf16[16,32,128]{2,0,1:T(8,128)(2,1)S(1)} fusion(bf16[32,128,1024]{2,1,0:T(8,128)(2,1)} %add_convert_fusion, bf16[32,16,1024]{2,1,0:T(8,128)(2,1)S(1)} %gather_fusion.1), kind=kOutput, calls=%fused_computation.19 | convolution fusion | flops 134283264 | bytes 9568256 | tf_op jit(solution)/shard_map/qfm,qzm->fqz/dot_general | solution.py:122
  66.8 4.6 %fusion.26 = f32[32,16,1024]{2,1,0:T(8,128)S(1)} fusion(bf16[32,128,1024]{2,1,0:T(8,128)(2,1)} %add_convert_fusion, f32[16,32,128]{2,0,1:T(8,128)S(1)} %get-tuple-element.37, f32[16,32,128]{2,0,1:T(8,128)S(1)} %get-tuple-element.36, f32[16,32,128]{2,0,1:T(8,128)S(1)} %get-tuple-element.35, f32[16,32,128]{2,0,1:T(8,128)S(1)} %get-tuple-element.34, ...), kind=kOutput, calls=%fused_computation.75 | convolution fusion | flops 134807552 | bytes 12845056 | tf_op jit(solution)/shard_map/zrs,rsu->rzu/dot_general | solution.py:144
  71.5 2.4 %fusion.2 = bf16[32,16,1024]{2,0,1:T(8,128)(2,1)S(1)} fusion(f32[32,16,1024]{2,1,0:T(8,128)S(1)} %fusion.26, s32[32]{0:T(128)S(1)} %bitcast.115), kind=kOutput, calls=%fused_computation.11 | convolution fusion | flops 201851904 | bytes 3145856 | tf_op jit(solution)/shard_map/gv,gct->vct/dot_general | solution.py:149
  74.5 0.7 convert_element_type.104
  76.3 41.7 %all_to_all.30 = bf16[64,66,128]{2,1,0:T(8,128)(2,1)S(1)} all-to-all(bf16[64,66,128]{2,1,0:T(8,128)(2,1)S(1)} %pad_maximum_fusion), channel_id=1, replica_groups=mesh['frames'=64,'tex'=8] {'frames'}, dimensions={0} | all-to-all | bytes 2162688 | tf_op jit(solution)/shard_map/all_to_all | solution.py:198
  118.4 0.7 reshape.231
  119.2 1.3 fusion.5
  120.8 15.0 %all_to_all.31 = bf16[8,130,128]{2,1,0:T(8,128)(2,1)S(1)} all-to-all(bf16[8,130,128]{2,1,0:T(8,128)(2,1)S(1)} %pad_maximum_fusion.1), channel_id=1, replica_groups=mesh['frames'=64,'tex'=8] {'tex'}, dimensions={0} | all-to-all | bytes 532480 | tf_op jit(solution)/shard_map/all_to_all | solution.py:224
  136.5 6.2 %all-to-all-start.4 = ((f32[64,1,72]{2,1,0:T(1,128)}), f32[64,1,72]{2,1,0:T(1,128)S(1)}, u32[]{:S(2)}, u32[]{:S(2)}) async-start(f32[64,1,72]{2,1,0:T(1,128)} %broadcast_in_dim.79), calls=%async_computation.4 | async-start | bytes 65536 | tf_op jit(solution)/shard_map/all_to_all | solution.py:230
  142.7 0.8 fusion.25
  144.2 7.7 %all-to-all-done.4 = f32[64,1,72]{2,1,0:T(1,128)S(1)} async-done(((f32[64,1,72]{2,1,0:T(1,128)}), f32[64,1,72]{2,1,0:T(1,128)S(1)}, u32[]{:S(2)}, u32[]{:S(2)}) %all-to-all-start.4) | async-done | bytes 18464 | tf_op jit(solution)/shard_map/all_to_all | solution.py:230
  152.1 0.7 mul.76
  (62 shorter events, 8.5 us)
Async XLA Ops:
  0.6 64.3 %copy-start = (bf16[32,144]{1,0:T(8,128)(2,1)S(1)}, bf16[32,144]{1,0:T(8,128)(2,1)}, u32[]{:S(2)}) copy-start(bf16[32,144]{1,0:T(8,128)(2,1)} %param.12) | copy-start | bytes 27652
  3.2 17.3 %all-to-all-start = ((s32[8,1,4]{2,1,0:T(1,128)}), s32[8,1,4]{2,1,0:T(1,128)S(1)}, u32[]{:S(2)}, u32[]{:S(2)}) async-start(s32[8,1,4]{2,1,0:T(1,128)} %bitcast.4), calls=%async_computation | async-start | bytes 8192 | tf_op jit(solution)/shard_map/all_to_all | solution.py:166
  23.0 34.8 %all-to-all-start.1 = ((bf16[8,64,1024]{2,1,0:T(8,128)(2,1)}), bf16[8,64,1024]{2,1,0:T(8,128)(2,1)S(1)}, u32[]{:S(2)}, u32[]{:S(2)}) async-start(bf16[8,64,1024]{2,1,0:T(8,128)(2,1)} %bitcast.5), calls=%async_computation.1 | async-start | bytes 2097152 | tf_op jit(solution)/shard_map/all_to_all | solution.py:172
  28.6 10.5 %copy-start.2 = (s32[1,32]{1,0:T(1,128)S(1)}, s32[1,32]{1,0:T(1,128)}, u32[]{:S(2)}) copy-start(s32[1,32]{1,0:T(1,128)} %param.9) | copy-start | bytes 388
  64.1 1.2 copy-start.1
  136.5 15.5 %all-to-all-start.4 = ((f32[64,1,72]{2,1,0:T(1,128)}), f32[64,1,72]{2,1,0:T(1,128)S(1)}, u32[]{:S(2)}, u32[]{:S(2)}) async-start(f32[64,1,72]{2,1,0:T(1,128)} %broadcast_in_dim.79), calls=%async_computation.4 | async-start | bytes 65536 | tf_op jit(solution)/shard_map/all_to_all | solution.py:230

commit v9 on v8

--- a/solution.py
+++ b/solution.py
@@ -141,13 +141,11 @@
         shift_y, shift_x = offsets[number]
         feat_grad = feat_grad + shifted(col_grad[number], -shift_y, -shift_x)
     feat_grad = feat_grad.astype(jnp.bfloat16)
-    texel_gradient = jnp.einsum(
-        "zrs,rsu->rzu", feat_grad, lookup, preferred_element_type=jnp.float32
-    )
     slot_numbers = jnp.arange(visible, dtype=jnp.int32)
-    selector = (slot_row[:, None] == slot_numbers[None, :]).astype(jnp.float32)
+    selector = (slot_numbers[:, None] == slot_row[None, :]).astype(jnp.bfloat16)
+    routed = selector[:, None, :, None] * feat_grad[None]
     slot_grad = jnp.einsum(
-        "gv,gct->vct", selector, texel_gradient, precision=lax.Precision.HIGHEST
+        "vcrs,rsu->vcu", routed, lookup, preferred_element_type=jnp.float32
     )
     return (rendered, slot_grad.reshape(visible, channels * texel), weight_local)
 

time: 153 us -> 155 us (1.013)
    dot_general x2 -> x1, matrix products: 7.09 us -> 7.91 us  [render_flat(): jnp.einsum('vcrs,rsu->vcu', routed, lookup, preferred_element_type=jnp.fl...]
    unnamed x19 -> x28, local copies, waits for them, and re-layouts: 4.25 us -> 4.74 us
where the time goes in v9:
time: 155 us; the launch traced here: 154 us
  blocking collectives  56.9 us (37%)
  waiting for transfers between devices  27.4 us (18%)
  starting transfers between devices  22.5 us (15%)
  matrix products  16.2 us (10%)
  other arithmetic  16.1 us (10%)
  local copies, waits for them, and re-layouts  13.7 us (9%)
    all_to_all x1, blocking collectives, per_device(): lax.all_to_all(spread, 'frames', split_axis=0, concat_axis=0, tiled=True)  41.9 us
    all_to_all x1, waiting for transfers between devices, per_device(): lax.all_to_all(served, 'tex', split_axis=0, concat_axis=0, tiled=True)  18.5 us
    all_to_all x1, blocking collectives, per_device(): lax.all_to_all(partial, 'tex', 0, 0, tiled=True).astype(jnp.float32)  15 us
    all_to_all x1, starting transfers between devices, per_device(): lax.all_to_all(wanted_ids, 'tex', split_axis=0, concat_axis=0, tiled=True)  10.9 us
    convert_element_type x1, other arithmetic, sample_matrix(): return matrix.astype(jnp.bfloat16)  10.5 us
    dot_general x1, matrix products, render_flat(): jnp.einsum('vcrs,rsu->vcu', routed, lookup, preferred_element_type=jnp.fl...  7.91 us
    all_to_all x1, waiting for transfers between devices, per_device(): lax.all_to_all(jnp.broadcast_to(chunk_total[None], (frame_count, chunk)),...  7.74 us
    all_to_all x1, starting transfers between devices, per_device(): lax.all_to_all(jnp.broadcast_to(chunk_total[None], (frame_count, chunk)),...  6.22 us
  transfers between devices with their start and end apart: 3, of which 3 were waited for; matrix products, arithmetic and copies ran while one was open for 11% of the time, Pallas kernels for 0%

profile of v9, /device:TPU:1, one launch (start us, length us, event | category | flops | bytes accessed | tf_op | source)
XLA Modules:
  0.0 154.0 jit_solution(16214501165074167416)
XLA Ops:
  1.2 1.4 convert_bitcast_fusion
  2.6 0.7 all_to_all.19
  3.2 10.9 %all-to-all-start = ((s32[8,1,4]{2,1,0:T(1,128)}), s32[8,1,4]{2,1,0:T(1,128)S(1)}, u32[]{:S(2)}, u32[]{:S(2)}) async-start(s32[8,1,4]{2,1,0:T(1,128)} %bitcast.4), calls=%async_computation | async-start | bytes 8192 | tf_op jit(solution)/shard_map/all_to_all | solution.py:164
  14.1 0.8 broadcast_divide_fusion
  14.9 0.8 compare_reduce_fusion
  15.7 0.9 fusion.49
  16.6 2.8 %copy.33 = bf16[8,8,16,1024]{3,2,1,0:T(8,128)(2,1)S(1)} copy(bf16[8,8,16,1024]{3,1,2,0:T(8,128)(2,1)} %bitcast.102) | data formatting | bytes 4194304
  19.4 1.2 all-to-all-done
  20.6 0.7 reduce.13
  21.3 1.7 %gather_fusion = bf16[32,16,1024]{2,1,0:T(8,128)(2,1)} fusion(bf16[64,16,1024]{2,1,0:T(8,128)(2,1)S(1)} %bitcast.99, s32[1024]{0:T(1024)S(1)} %pad_clamp_fusion.1), kind=kCustom, calls=%fused_computation | custom fusion | bytes 2097280 | tf_op jit(solution)/shard_map/jit(_take)/gather | solution.py:167
  23.0 5.5 %all-to-all-start.1 = ((bf16[8,64,1024]{2,1,0:T(8,128)(2,1)}), bf16[8,64,1024]{2,1,0:T(8,128)(2,1)S(1)}, u32[]{:S(2)}, u32[]{:S(2)}) async-start(bf16[8,64,1024]{2,1,0:T(8,128)(2,1)} %bitcast.5), calls=%async_computation.1 | async-start | bytes 2097152 | tf_op jit(solution)/shard_map/all_to_all | solution.py:170
  28.5 10.5 %add_convert_fusion = bf16[32,128,1024]{2,1,0:T(8,128)(2,1)} fusion(f32[32,128]{1,0:T(8,128)S(1)} %get-tuple-element.18, s32[32,128]{1,0:T(8,128)S(1)} %get-tuple-element.23, f32[32,128]{1,0:T(8,128)S(1)} %get-tuple-element.19, s32[32,128]{1,0:T(8,128)S(1)} %get-tuple-element.22, f32[32,128]{1,0:T(8,128)S(1)} %get-tuple-element.17, ...), kind=kLoop, calls=%fused_computation.2 | loop fusion | flops 50331648 | bytes 8519680 | tf_op jit(solution)/shard_map/convert_element_type | solution.py:37
  39.2 18.5 %all-to-all-done.1 = bf16[8,64,1024]{2,1,0:T(8,128)(2,1)S(1)} async-done(((bf16[8,64,1024]{2,1,0:T(8,128)(2,1)}), bf16[8,64,1024]{2,1,0:T(8,128)(2,1)S(1)}, u32[]{:S(2)}, u32[]{:S(2)}) %all-to-all-start.1) | async-done | bytes 1048608 | tf_op jit(solution)/shard_map/all_to_all | solution.py:170
  58.3 5.7 %fusion.13 = bf16[16,32,128]{2,0,1:T(8,128)(2,1)S(1)} fusion(bf16[32,128,1024]{2,1,0:T(8,128)(2,1)} %add_convert_fusion, bf16[32,16,1024]{2,1,0:T(8,128)(2,1)S(1)} %gather_fusion.1), kind=kOutput, calls=%fused_computation.22 | convolution fusion | flops 134283264 | bytes 9568256 | tf_op jit(solution)/shard_map/qfm,qzm->fqz/dot_general | solution.py:122
  67.6 7.9 %bitcast_convert_fusion = bf16[32,16,1024]{2,1,0:T(8,128)(2,1)S(1)} fusion(bf16[32,128,1024]{2,1,0:T(8,128)(2,1)} %add_convert_fusion, bf16[16,32,128]{2,0,1:T(8,128)(2,1)S(1)} %copy.25, bf16[32,32]{1,0:T(8,128)(2,1)S(1)} %fusion.41), kind=kOutput, calls=%fused_computation.12 | convolution fusion | flops 4297588736 | bytes 9570304 | tf_op jit(solution)/shard_map/vcrs,rsu->vcu/dot_general | solution.py:147
  75.5 0.7 convert_element_type.111
  77.3 41.9 %all_to_all.30 = bf16[64,66,128]{2,1,0:T(8,128)(2,1)S(1)} all-to-all(bf16[64,66,128]{2,1,0:T(8,128)(2,1)S(1)} %pad_maximum_fusion), channel_id=1, replica_groups=mesh['frames'=64,'tex'=8] {'frames'}, dimensions={0} | all-to-all | bytes 2162688 | tf_op jit(solution)/shard_map/all_to_all | solution.py:196
  119.6 0.7 reshape.251
  120.4 1.3 fusion.9
  121.9 15.0 %all_to_all.31 = bf16[8,130,128]{2,1,0:T(8,128)(2,1)S(1)} all-to-all(bf16[8,130,128]{2,1,0:T(8,128)(2,1)S(1)} %pad_maximum_fusion.1), channel_id=1, replica_groups=mesh['frames'=64,'tex'=8] {'tex'}, dimensions={0} | all-to-all | bytes 532480 | tf_op jit(solution)/shard_map/all_to_all | solution.py:222
  137.7 6.2 %all-to-all-start.4 = ((f32[64,1,72]{2,1,0:T(1,128)}), f32[64,1,72]{2,1,0:T(1,128)S(1)}, u32[]{:S(2)}, u32[]{:S(2)}) async-start(f32[64,1,72]{2,1,0:T(1,128)} %broadcast_in_dim.81), calls=%async_computation.4 | async-start | bytes 65536 | tf_op jit(solution)/shard_map/all_to_all | solution.py:228
  143.9 0.8 fusion.29
  145.4 7.7 %all-to-all-done.4 = f32[64,1,72]{2,1,0:T(1,128)S(1)} async-done(((f32[64,1,72]{2,1,0:T(1,128)}), f32[64,1,72]{2,1,0:T(1,128)S(1)}, u32[]{:S(2)}, u32[]{:S(2)}) %all-to-all-start.4) | async-done | bytes 18464 | tf_op jit(solution)/shard_map/all_to_all | solution.py:228
  153.3 0.7 mul.92
  (68 shorter events, 8.1 us)
Async XLA Ops:
  0.6 64.2 %copy-start = (bf16[32,144]{1,0:T(8,128)(2,1)S(1)}, bf16[32,144]{1,0:T(8,128)(2,1)}, u32[]{:S(2)}) copy-start(bf16[32,144]{1,0:T(8,128)(2,1)} %param.12) | copy-start | bytes 27652
  3.2 17.3 %all-to-all-start = ((s32[8,1,4]{2,1,0:T(1,128)}), s32[8,1,4]{2,1,0:T(1,128)S(1)}, u32[]{:S(2)}, u32[]{:S(2)}) async-start(s32[8,1,4]{2,1,0:T(1,128)} %bitcast.4), calls=%async_computation | async-start | bytes 8192 | tf_op jit(solution)/shard_map/all_to_all | solution.py:164
  23.0 34.7 %all-to-all-start.1 = ((bf16[8,64,1024]{2,1,0:T(8,128)(2,1)}), bf16[8,64,1024]{2,1,0:T(8,128)(2,1)S(1)}, u32[]{:S(2)}, u32[]{:S(2)}) async-start(bf16[8,64,1024]{2,1,0:T(8,128)(2,1)} %bitcast.5), calls=%async_computation.1 | async-start | bytes 2097152 | tf_op jit(solution)/shard_map/all_to_all | solution.py:170
  28.5 10.6 %copy-start.2 = (s32[1,32]{1,0:T(1,128)S(1)}, s32[1,32]{1,0:T(1,128)}, u32[]{:S(2)}) copy-start(s32[1,32]{1,0:T(1,128)} %param.9) | copy-start | bytes 388
  64.0 1.2 copy-start.1
  137.7 15.5 %all-to-all-start.4 = ((f32[64,1,72]{2,1,0:T(1,128)}), f32[64,1,72]{2,1,0:T(1,128)S(1)}, u32[]{:S(2)}, u32[]{:S(2)}) async-start(f32[64,1,72]{2,1,0:T(1,128)} %broadcast_in_dim.81), calls=%async_computation.4 | async-start | bytes 65536 | tf_op jit(solution)/shard_map/all_to_all | solution.py:228

commit v10 on v8

--- a/solution.py
+++ b/solution.py
@@ -201,12 +201,12 @@
     frame_weight = jnp.sum(side[:, :chunk] + side[:, chunk : 2 * chunk], axis=0)
     senders = side[:, 2 * chunk : 2 * chunk + request_count].astype(jnp.int32)
     senders = senders.reshape(frame_count, owners, per_owner)
-    gathered = gathered[:, :grad_rows].astype(jnp.float32)
+    gathered = gathered[:, :grad_rows]
     gathered = gathered.reshape(frame_count, owners, per_owner, columns)
     tile_numbers = jnp.arange(tile_count, dtype=jnp.int32)
-    selector = (senders[None] == tile_numbers[:, None, None, None]).astype(jnp.float32)
+    selector = (senders[None] == tile_numbers[:, None, None, None]).astype(jnp.bfloat16)
     partial = jnp.einsum(
-        "qfoj,fojc->oqc", selector, gathered, precision=lax.Precision.HIGHEST
+        "qfoj,fojc->oqc", selector, gathered, preferred_element_type=jnp.float32
     )
     weight_high = frame_weight.astype(jnp.bfloat16)
     weight_low = (frame_weight - weight_high.astype(jnp.float32)).astype(jnp.bfloat16)

time: 153 us -> 153 us (level)
  no operation moved by 1% of the time
where the time goes in v10:
time: 153 us
  blocking collectives  56.7 us (37%)
  waiting for transfers between devices  27.4 us (18%)
  starting transfers between devices  22.7 us (15%)
  other arithmetic  15.6 us (10%)
  matrix products  15.4 us (10%)
  local copies, waits for them, and re-layouts  13.9 us (9%)
    all_to_all x1, blocking collectives, per_device(): lax.all_to_all(spread, 'frames', split_axis=0, concat_axis=0, tiled=True)  41.7 us
    all_to_all x1, waiting for transfers between devices, per_device(): lax.all_to_all(served, 'tex', split_axis=0, concat_axis=0, tiled=True)  18.7 us
    all_to_all x1, blocking collectives, per_device(): lax.all_to_all(partial, 'tex', 0, 0, tiled=True).astype(jnp.float32)  15 us
    all_to_all x1, starting transfers between devices, per_device(): lax.all_to_all(wanted_ids, 'tex', split_axis=0, concat_axis=0, tiled=True)  10.9 us
    convert_element_type x1, other arithmetic, sample_matrix(): return matrix.astype(jnp.bfloat16)  10.5 us
    all_to_all x1, waiting for transfers between devices, per_device(): lax.all_to_all(jnp.broadcast_to(chunk_total[None], (frame_count, chunk)),...  7.74 us
    all_to_all x1, starting transfers between devices, per_device(): lax.all_to_all(jnp.broadcast_to(chunk_total[None], (frame_count, chunk)),...  6.21 us
    dot_general x1, matrix products, render_flat(): jnp.einsum('qfm,qzm->fqz', selected_entries, lookup, preferred_element_ty...  5.66 us
  transfers between devices with their start and end apart: 3, of which 3 were waited for; matrix products, arithmetic and copies ran while one was open for 11% of the time, Pallas kernels for 0%

profile of v10, /device:TPU:1, one launch (start us, length us, event | category | flops | bytes accessed | tf_op | source)
XLA Modules:
  0.0 152.8 jit_solution(3740871765861905767)
XLA Ops:
  1.2 1.4 convert_bitcast_fusion
  2.6 0.7 all_to_all.19
  3.2 10.9 %all-to-all-start = ((s32[8,1,4]{2,1,0:T(1,128)}), s32[8,1,4]{2,1,0:T(1,128)S(1)}, u32[]{:S(2)}, u32[]{:S(2)}) async-start(s32[8,1,4]{2,1,0:T(1,128)} %bitcast.4), calls=%async_computation | async-start | bytes 8192 | tf_op jit(solution)/shard_map/all_to_all | solution.py:166
  14.1 0.8 compare_reduce_fusion
  14.9 0.8 broadcast_divide_fusion
  15.7 0.9 fusion.50
  16.7 2.8 %copy.59 = bf16[8,8,16,1024]{3,2,1,0:T(8,128)(2,1)S(1)} copy(bf16[8,8,16,1024]{3,1,2,0:T(8,128)(2,1)} %bitcast.105) | data formatting | bytes 4194304
  19.5 1.0 all-to-all-done
  21.3 1.7 %gather_fusion = bf16[32,16,1024]{2,1,0:T(8,128)(2,1)} fusion(bf16[64,16,1024]{2,1,0:T(8,128)(2,1)S(1)} %bitcast.102, s32[1024]{0:T(1024)S(1)} %pad_clamp_fusion.1), kind=kCustom, calls=%fused_computation | custom fusion | bytes 2097280 | tf_op jit(solution)/shard_map/jit(_take)/gather | solution.py:169
  23.0 5.6 %all-to-all-start.1 = ((bf16[8,64,1024]{2,1,0:T(8,128)(2,1)}), bf16[8,64,1024]{2,1,0:T(8,128)(2,1)S(1)}, u32[]{:S(2)}, u32[]{:S(2)}) async-start(bf16[8,64,1024]{2,1,0:T(8,128)(2,1)} %bitcast.5), calls=%async_computation.1 | async-start | bytes 2097152 | tf_op jit(solution)/shard_map/all_to_all | solution.py:172
  28.6 10.5 %add_convert_fusion = bf16[32,128,1024]{2,1,0:T(8,128)(2,1)} fusion(f32[32,128]{1,0:T(8,128)S(1)} %get-tuple-element.18, s32[32,128]{1,0:T(8,128)S(1)} %get-tuple-element.23, f32[32,128]{1,0:T(8,128)S(1)} %get-tuple-element.19, s32[32,128]{1,0:T(8,128)S(1)} %get-tuple-element.22, f32[32,128]{1,0:T(8,128)S(1)} %get-tuple-element.17, ...), kind=kLoop, calls=%fused_computation.2 | loop fusion | flops 50331648 | bytes 8519680 | tf_op jit(solution)/shard_map/convert_element_type | solution.py:37
  39.1 18.7 %all-to-all-done.1 = bf16[8,64,1024]{2,1,0:T(8,128)(2,1)S(1)} async-done(((bf16[8,64,1024]{2,1,0:T(8,128)(2,1)}), bf16[8,64,1024]{2,1,0:T(8,128)(2,1)S(1)}, u32[]{:S(2)}, u32[]{:S(2)}) %all-to-all-start.1) | async-done | bytes 1048608 | tf_op jit(solution)/shard_map/all_to_all | solution.py:172
  58.4 5.7 %fusion.9 = bf16[16,32,128]{2,0,1:T(8,128)(2,1)S(1)} fusion(bf16[32,128,1024]{2,1,0:T(8,128)(2,1)} %add_convert_fusion, bf16[32,16,1024]{2,1,0:T(8,128)(2,1)S(1)} %gather_fusion.1), kind=kOutput, calls=%fused_computation.19 | convolution fusion | flops 134283264 | bytes 9568256 | tf_op jit(solution)/shard_map/qfm,qzm->fqz/dot_general | solution.py:122
  66.8 4.6 %fusion.26 = f32[32,16,1024]{2,1,0:T(8,128)S(1)} fusion(bf16[32,128,1024]{2,1,0:T(8,128)(2,1)} %add_convert_fusion, f32[16,32,128]{2,0,1:T(8,128)S(1)} %get-tuple-element.37, f32[16,32,128]{2,0,1:T(8,128)S(1)} %get-tuple-element.36, f32[16,32,128]{2,0,1:T(8,128)S(1)} %get-tuple-element.35, f32[16,32,128]{2,0,1:T(8,128)S(1)} %get-tuple-element.34, ...), kind=kOutput, calls=%fused_computation.75 | convolution fusion | flops 134807552 | bytes 12845056 | tf_op jit(solution)/shard_map/zrs,rsu->rzu/dot_general | solution.py:144
  71.5 2.4 %fusion.2 = bf16[32,16,1024]{2,0,1:T(8,128)(2,1)S(1)} fusion(f32[32,16,1024]{2,1,0:T(8,128)S(1)} %fusion.26, s32[32]{0:T(128)S(1)} %bitcast.115), kind=kOutput, calls=%fused_computation.11 | convolution fusion | flops 201851904 | bytes 3145856 | tf_op jit(solution)/shard_map/gv,gct->vct/dot_general | solution.py:149
  74.5 0.7 convert_element_type.103
  76.3 41.7 %all_to_all.30 = bf16[64,66,128]{2,1,0:T(8,128)(2,1)S(1)} all-to-all(bf16[64,66,128]{2,1,0:T(8,128)(2,1)S(1)} %pad_maximum_fusion), channel_id=1, replica_groups=mesh['frames'=64,'tex'=8] {'frames'}, dimensions={0} | all-to-all | bytes 2162688 | tf_op jit(solution)/shard_map/all_to_all | solution.py:198
  118.4 0.7 reshape.231
  119.2 1.3 fusion.5
  120.8 15.0 %all_to_all.31 = bf16[8,130,128]{2,1,0:T(8,128)(2,1)S(1)} all-to-all(bf16[8,130,128]{2,1,0:T(8,128)(2,1)S(1)} %pad_maximum_fusion.1), channel_id=1, replica_groups=mesh['frames'=64,'tex'=8] {'tex'}, dimensions={0} | all-to-all | bytes 532480 | tf_op jit(solution)/shard_map/all_to_all | solution.py:224
  136.5 6.2 %all-to-all-start.4 = ((f32[64,1,72]{2,1,0:T(1,128)}), f32[64,1,72]{2,1,0:T(1,128)S(1)}, u32[]{:S(2)}, u32[]{:S(2)}) async-start(f32[64,1,72]{2,1,0:T(1,128)} %broadcast_in_dim.79), calls=%async_computation.4 | async-start | bytes 65536 | tf_op jit(solution)/shard_map/all_to_all | solution.py:230
  142.7 0.8 fusion.25
  144.2 7.7 %all-to-all-done.4 = f32[64,1,72]{2,1,0:T(1,128)S(1)} async-done(((f32[64,1,72]{2,1,0:T(1,128)}), f32[64,1,72]{2,1,0:T(1,128)S(1)}, u32[]{:S(2)}, u32[]{:S(2)}) %all-to-all-start.4) | async-done | bytes 18464 | tf_op jit(solution)/shard_map/all_to_all | solution.py:230
  152.1 0.7 mul.76
  (62 shorter events, 8.5 us)
Async XLA Ops:
  0.6 64.3 %copy-start = (bf16[32,144]{1,0:T(8,128)(2,1)S(1)}, bf16[32,144]{1,0:T(8,128)(2,1)}, u32[]{:S(2)}) copy-start(bf16[32,144]{1,0:T(8,128)(2,1)} %param.12) | copy-start | bytes 27652
  3.2 17.3 %all-to-all-start = ((s32[8,1,4]{2,1,0:T(1,128)}), s32[8,1,4]{2,1,0:T(1,128)S(1)}, u32[]{:S(2)}, u32[]{:S(2)}) async-start(s32[8,1,4]{2,1,0:T(1,128)} %bitcast.4), calls=%async_computation | async-start | bytes 8192 | tf_op jit(solution)/shard_map/all_to_all | solution.py:166
  23.0 34.8 %all-to-all-start.1 = ((bf16[8,64,1024]{2,1,0:T(8,128)(2,1)}), bf16[8,64,1024]{2,1,0:T(8,128)(2,1)S(1)}, u32[]{:S(2)}, u32[]{:S(2)}) async-start(bf16[8,64,1024]{2,1,0:T(8,128)(2,1)} %bitcast.5), calls=%async_computation.1 | async-start | bytes 2097152 | tf_op jit(solution)/shard_map/all_to_all | solution.py:172
  28.6 10.5 %copy-start.2 = (s32[1,32]{1,0:T(1,128)S(1)}, s32[1,32]{1,0:T(1,128)}, u32[]{:S(2)}) copy-start(s32[1,32]{1,0:T(1,128)} %param.9) | copy-start | bytes 388
  64.1 1.2 copy-start.1
  136.5 15.5 %all-to-all-start.4 = ((f32[64,1,72]{2,1,0:T(1,128)}), f32[64,1,72]{2,1,0:T(1,128)S(1)}, u32[]{:S(2)}, u32[]{:S(2)}) async-start(f32[64,1,72]{2,1,0:T(1,128)} %broadcast_in_dim.79), calls=%async_computation.4 | async-start | bytes 65536 | tf_op jit(solution)/shard_map/all_to_all | solution.py:230

commit v11 on v8

--- a/solution.py
+++ b/solution.py
@@ -146,10 +146,14 @@
     )
     slot_numbers = jnp.arange(visible, dtype=jnp.int32)
     selector = (slot_row[:, None] == slot_numbers[None, :]).astype(jnp.float32)
+    blocks = texel // LANE // 2
     slot_grad = jnp.einsum(
-        "gv,gct->vct", selector, texel_gradient, precision=lax.Precision.HIGHEST
-    )
-    return (rendered, slot_grad.reshape(visible, channels * texel), weight_local)
+        "gv,gcbt->cbvt",
+        selector,
+        texel_gradient.reshape(height, channels, blocks, texel // blocks),
+        precision=lax.Precision.HIGHEST,
+    )
+    return (rendered, slot_grad, weight_local)
 
 
 def per_device(texture, requests, block_slot, texel_cell, uv_frac, conv_weight, cotangent):
@@ -192,7 +196,7 @@
         ],
         axis=1,
     ).reshape(frame_count, extra * columns // LANE, LANE)
-    spread = slot_grad.reshape(visible, frame_count, columns).transpose(1, 0, 2)
+    spread = slot_grad.reshape(frame_count, visible, columns)
     spread = spread.astype(jnp.bfloat16).reshape(frame_count, visible * columns // LANE, LANE)
     spread = jnp.concatenate([spread, side_row], axis=1)
     gathered = lax.all_to_all(spread, "frames", split_axis=0, concat_axis=0, tiled=True)

time: 153 us -> 155 us (1.013)
    reshape x1, local copies, waits for them, and re-layouts: 0.39 us -> 2.02 us  [render_flat(): texel_gradient.reshape(height, channels, blocks, texel // blocks)]
    unnamed x19 -> x17, local copies, waits for them, and re-layouts: 4.25 us -> 4.18 us
where the time goes in v11:
time: 155 us; the launch traced here: 154 us
  blocking collectives  56.7 us (37%)
  waiting for transfers between devices  27.4 us (18%)
  starting transfers between devices  22.7 us (15%)
  matrix products  16.9 us (11%)
  other arithmetic  15.7 us (10%)
  local copies, waits for them, and re-layouts  14 us (9%)
    all_to_all x1, blocking collectives, per_device(): lax.all_to_all(spread, 'frames', split_axis=0, concat_axis=0, tiled=True)  41.7 us
    all_to_all x1, waiting for transfers between devices, per_device(): lax.all_to_all(served, 'tex', split_axis=0, concat_axis=0, tiled=True)  18.7 us
    all_to_all x1, blocking collectives, per_device(): lax.all_to_all(partial, 'tex', 0, 0, tiled=True).astype(jnp.float32)  15 us
    all_to_all x1, starting transfers between devices, per_device(): lax.all_to_all(wanted_ids, 'tex', split_axis=0, concat_axis=0, tiled=True)  10.9 us
    convert_element_type x1, other arithmetic, sample_matrix(): return matrix.astype(jnp.bfloat16)  10.5 us
    all_to_all x1, waiting for transfers between devices, per_device(): lax.all_to_all(jnp.broadcast_to(chunk_total[None], (frame_count, chunk)),...  7.74 us
    all_to_all x1, starting transfers between devices, per_device(): lax.all_to_all(jnp.broadcast_to(chunk_total[None], (frame_count, chunk)),...  6.22 us
    dot_general x1, matrix products, render_flat(): jnp.einsum('qfm,qzm->fqz', selected_entries, lookup, preferred_element_ty...  5.66 us
  transfers between devices with their start and end apart: 3, of which 3 were waited for; matrix products, arithmetic and copies ran while one was open for 11% of the time, Pallas kernels for 0%

profile of v11, /device:TPU:1, one launch (start us, length us, event | category | flops | bytes accessed | tf_op | source)
XLA Modules:
  0.0 154.4 jit_solution(5234637118956917574)
XLA Ops:
  1.2 1.4 convert_bitcast_fusion.1
  2.6 0.7 all_to_all.19
  3.2 10.9 %all-to-all-start = ((s32[8,1,4]{2,1,0:T(1,128)}), s32[8,1,4]{2,1,0:T(1,128)S(1)}, u32[]{:S(2)}, u32[]{:S(2)}) async-start(s32[8,1,4]{2,1,0:T(1,128)} %bitcast.4), calls=%async_computation | async-start | bytes 8192 | tf_op jit(solution)/shard_map/all_to_all | solution.py:170
  14.1 0.8 compare_reduce_fusion
  14.9 0.8 broadcast_divide_fusion
  15.7 0.9 fusion.53
  16.7 2.8 %copy.123 = bf16[8,8,16,1024]{3,2,1,0:T(8,128)(2,1)S(1)} copy(bf16[8,8,16,1024]{3,1,2,0:T(8,128)(2,1)} %bitcast.110) | data formatting | bytes 4194304
  19.5 1.0 all-to-all-done
  21.3 1.7 %gather_fusion = bf16[32,16,1024]{2,1,0:T(8,128)(2,1)} fusion(bf16[64,16,1024]{2,1,0:T(8,128)(2,1)S(1)} %bitcast.108, s32[1024]{0:T(1024)S(1)} %pad_clamp_fusion.1), kind=kCustom, calls=%fused_computation | custom fusion | bytes 2097280 | tf_op jit(solution)/shard_map/jit(_take)/gather | solution.py:173
  23.0 5.6 %all-to-all-start.1 = ((bf16[8,64,1024]{2,1,0:T(8,128)(2,1)}), bf16[8,64,1024]{2,1,0:T(8,128)(2,1)S(1)}, u32[]{:S(2)}, u32[]{:S(2)}) async-start(bf16[8,64,1024]{2,1,0:T(8,128)(2,1)} %bitcast.5), calls=%async_computation.1 | async-start | bytes 2097152 | tf_op jit(solution)/shard_map/all_to_all | solution.py:176
  28.6 10.5 %add_convert_fusion = bf16[32,128,1024]{2,1,0:T(8,128)(2,1)} fusion(f32[32,128]{1,0:T(8,128)S(1)} %get-tuple-element.18, s32[32,128]{1,0:T(8,128)S(1)} %get-tuple-element.23, f32[32,128]{1,0:T(8,128)S(1)} %get-tuple-element.19, s32[32,128]{1,0:T(8,128)S(1)} %get-tuple-element.22, f32[32,128]{1,0:T(8,128)S(1)} %get-tuple-element.17, ...), kind=kLoop, calls=%fused_computation.2 | loop fusion | flops 50331648 | bytes 8519680 | tf_op jit(solution)/shard_map/convert_element_type | solution.py:37
  39.1 18.7 %all-to-all-done.1 = bf16[8,64,1024]{2,1,0:T(8,128)(2,1)S(1)} async-done(((bf16[8,64,1024]{2,1,0:T(8,128)(2,1)}), bf16[8,64,1024]{2,1,0:T(8,128)(2,1)S(1)}, u32[]{:S(2)}, u32[]{:S(2)}) %all-to-all-start.1) | async-done | bytes 1048608 | tf_op jit(solution)/shard_map/all_to_all | solution.py:176
  58.4 5.7 %fusion.12 = bf16[16,32,128]{2,0,1:T(8,128)(2,1)S(1)} fusion(bf16[32,128,1024]{2,1,0:T(8,128)(2,1)} %add_convert_fusion, bf16[32,16,1024]{2,1,0:T(8,128)(2,1)S(1)} %gather_fusion.1), kind=kOutput, calls=%fused_computation.20 | convolution fusion | flops 134283264 | bytes 9568256 | tf_op jit(solution)/shard_map/qfm,qzm->fqz/dot_general | solution.py:122
  66.8 4.6 %fusion.29 = f32[32,16,1024]{2,1,0:T(8,128)S(1)} fusion(bf16[32,128,1024]{2,1,0:T(8,128)(2,1)} %add_convert_fusion, f32[16,32,128]{2,0,1:T(8,128)S(1)} %get-tuple-element.37, f32[16,32,128]{2,0,1:T(8,128)S(1)} %get-tuple-element.36, f32[16,32,128]{2,0,1:T(8,128)S(1)} %get-tuple-element.35, f32[16,32,128]{2,0,1:T(8,128)S(1)} %get-tuple-element.34, ...), kind=kOutput, calls=%fused_computation.76 | convolution fusion | flops 134807552 | bytes 12845056 | tf_op jit(solution)/shard_map/zrs,rsu->rzu/dot_general | solution.py:144
  71.5 2.0 %reshape.231 = f32[32,16,4,256]{3,2,1,0:T(4,128)} reshape(f32[32,16,1024]{2,1,0:T(8,128)S(1)} %fusion.29) | data formatting | bytes 4194304 | tf_op jit(solution)/shard_map/reshape | solution.py:153
  73.5 3.9 %fusion.5 = bf16[16,4,32,256]{3,2,1,0:T(8,128)(2,1)S(1)} fusion(f32[32,16,4,256]{3,2,1,0:T(4,128)} %reshape.231, s32[32]{0:T(128)S(1)} %bitcast.117), kind=kOutput, calls=%fused_computation.12 | convolution fusion | flops 201851904 | bytes 3145856 | tf_op jit(solution)/shard_map/gv,gcbt->cbvt/dot_general | solution.py:150
  77.9 41.7 %all_to_all.30 = bf16[64,66,128]{2,1,0:T(8,128)(2,1)S(1)} all-to-all(bf16[64,66,128]{2,1,0:T(8,128)(2,1)S(1)} %pad_maximum_fusion), channel_id=1, replica_groups=mesh['frames'=64,'tex'=8] {'frames'}, dimensions={0} | all-to-all | bytes 2162688 | tf_op jit(solution)/shard_map/all_to_all | solution.py:202
  120.0 0.7 reshape.234
  120.8 1.3 fusion.8
  122.4 15.0 %all_to_all.31 = bf16[8,130,128]{2,1,0:T(8,128)(2,1)S(1)} all-to-all(bf16[8,130,128]{2,1,0:T(8,128)(2,1)S(1)} %pad_maximum_fusion.1), channel_id=1, replica_groups=mesh['frames'=64,'tex'=8] {'tex'}, dimensions={0} | all-to-all | bytes 532480 | tf_op jit(solution)/shard_map/all_to_all | solution.py:228
  138.1 6.2 %all-to-all-start.4 = ((f32[64,1,72]{2,1,0:T(1,128)}), f32[64,1,72]{2,1,0:T(1,128)S(1)}, u32[]{:S(2)}, u32[]{:S(2)}) async-start(f32[64,1,72]{2,1,0:T(1,128)} %broadcast_in_dim.79), calls=%async_computation.4 | async-start | bytes 65536 | tf_op jit(solution)/shard_map/all_to_all | solution.py:234
  144.4 0.8 fusion.28
  145.9 7.7 %all-to-all-done.4 = f32[64,1,72]{2,1,0:T(1,128)S(1)} async-done(((f32[64,1,72]{2,1,0:T(1,128)}), f32[64,1,72]{2,1,0:T(1,128)S(1)}, u32[]{:S(2)}, u32[]{:S(2)}) %all-to-all-start.4) | async-done | bytes 18464 | tf_op jit(solution)/shard_map/all_to_all | solution.py:234
  153.7 0.7 mul.76
  (59 shorter events, 7.3 us)
Async XLA Ops:
  0.6 64.3 %copy-start = (bf16[32,144]{1,0:T(8,128)(2,1)S(1)}, bf16[32,144]{1,0:T(8,128)(2,1)}, u32[]{:S(2)}) copy-start(bf16[32,144]{1,0:T(8,128)(2,1)} %param.12) | copy-start | bytes 27652
  3.2 17.3 %all-to-all-start = ((s32[8,1,4]{2,1,0:T(1,128)}), s32[8,1,4]{2,1,0:T(1,128)S(1)}, u32[]{:S(2)}, u32[]{:S(2)}) async-start(s32[8,1,4]{2,1,0:T(1,128)} %bitcast.4), calls=%async_computation | async-start | bytes 8192 | tf_op jit(solution)/shard_map/all_to_all | solution.py:170
  23.0 34.8 %all-to-all-start.1 = ((bf16[8,64,1024]{2,1,0:T(8,128)(2,1)}), bf16[8,64,1024]{2,1,0:T(8,128)(2,1)S(1)}, u32[]{:S(2)}, u32[]{:S(2)}) async-start(bf16[8,64,1024]{2,1,0:T(8,128)(2,1)} %bitcast.5), calls=%async_computation.1 | async-start | bytes 2097152 | tf_op jit(solution)/shard_map/all_to_all | solution.py:176
  28.6 10.5 %copy-start.2 = (s32[1,32]{1,0:T(1,128)S(1)}, s32[1,32]{1,0:T(1,128)}, u32[]{:S(2)}) copy-start(s32[1,32]{1,0:T(1,128)} %param.9) | copy-start | bytes 388
  64.1 1.2 copy-start.1
  138.1 15.5 %all-to-all-start.4 = ((f32[64,1,72]{2,1,0:T(1,128)}), f32[64,1,72]{2,1,0:T(1,128)S(1)}, u32[]{:S(2)}, u32[]{:S(2)}) async-start(f32[64,1,72]{2,1,0:T(1,128)} %broadcast_in_dim.79), calls=%async_computation.4 | async-start | bytes 65536 | tf_op jit(solution)/shard_map/all_to_all | solution.py:234

commit v12 on v8

--- a/solution.py
+++ b/solution.py
@@ -120,8 +120,9 @@
     width = lookup.shape[1]
     selected_entries = jnp.take(fetched, slot_row, axis=0, mode="clip")
     feature_maps = jnp.einsum(
-        "qfm,qzm->fqz", selected_entries, lookup, preferred_element_type=jnp.float32
+        "qfm,qzm->qfz", selected_entries, lookup, preferred_element_type=jnp.float32
     ).astype(jnp.bfloat16)
+    feature_maps = feature_maps.transpose(1, 0, 2)
     offsets = [(shift_y, shift_x) for shift_y in (-1, 0, 1) for shift_x in (-1, 0, 1)]
     columns = jnp.concatenate(
         [shifted(feature_maps, shift_y, shift_x) for shift_y, shift_x in offsets], axis=0

time: 153 us -> 153 us (level)
  no operation moved by 1% of the time
where the time goes in v12:
time: 153 us
  blocking collectives  56.7 us (37%)
  waiting for transfers between devices  27.4 us (18%)
  starting transfers between devices  22.7 us (15%)
  other arithmetic  15.6 us (10%)
  matrix products  15.4 us (10%)
  local copies, waits for them, and re-layouts  13.9 us (9%)
    all_to_all x1, blocking collectives, per_device(): lax.all_to_all(spread, 'frames', split_axis=0, concat_axis=0, tiled=True)  41.7 us
    all_to_all x1, waiting for transfers between devices, per_device(): lax.all_to_all(served, 'tex', split_axis=0, concat_axis=0, tiled=True)  18.7 us
    all_to_all x1, blocking collectives, per_device(): lax.all_to_all(partial, 'tex', 0, 0, tiled=True).astype(jnp.float32)  15 us
    all_to_all x1, starting transfers between devices, per_device(): lax.all_to_all(wanted_ids, 'tex', split_axis=0, concat_axis=0, tiled=True)  10.9 us
    convert_element_type x1, other arithmetic, sample_matrix(): return matrix.astype(jnp.bfloat16)  10.5 us
    all_to_all x1, waiting for transfers between devices, per_device(): lax.all_to_all(jnp.broadcast_to(chunk_total[None], (frame_count, chunk)),...  7.74 us
    all_to_all x1, starting transfers between devices, per_device(): lax.all_to_all(jnp.broadcast_to(chunk_total[None], (frame_count, chunk)),...  6.21 us
    dot_general x1, matrix products, render_flat(): jnp.einsum('qfm,qzm->qfz', selected_entries, lookup, preferred_element_ty...  5.66 us
  transfers between devices with their start and end apart: 3, of which 3 were waited for; matrix products, arithmetic and copies ran while one was open for 11% of the time, Pallas kernels for 0%

profile of v12, /device:TPU:1, one launch (start us, length us, event | category | flops | bytes accessed | tf_op | source)
XLA Modules:
  0.0 152.7 jit_solution(3487504900186699109)
XLA Ops:
  1.2 1.4 convert_bitcast_fusion
  2.6 0.7 all_to_all.19
  3.2 10.9 %all-to-all-start = ((s32[8,1,4]{2,1,0:T(1,128)}), s32[8,1,4]{2,1,0:T(1,128)S(1)}, u32[]{:S(2)}, u32[]{:S(2)}) async-start(s32[8,1,4]{2,1,0:T(1,128)} %bitcast), calls=%async_computation | async-start | bytes 8192 | tf_op jit(solution)/shard_map/all_to_all | solution.py:167
  14.1 0.8 compare_reduce_fusion
  14.9 0.8 broadcast_divide_fusion
  15.7 0.9 fusion.50
  16.7 2.8 %copy.59 = bf16[8,8,16,1024]{3,2,1,0:T(8,128)(2,1)S(1)} copy(bf16[8,8,16,1024]{3,1,2,0:T(8,128)(2,1)} %bitcast.105) | data formatting | bytes 4194304
  19.5 1.0 all-to-all-done
  21.3 1.7 %gather_fusion = bf16[32,16,1024]{2,1,0:T(8,128)(2,1)} fusion(bf16[64,16,1024]{2,1,0:T(8,128)(2,1)S(1)} %bitcast.102, s32[1024]{0:T(1024)S(1)} %pad_clamp_fusion.1), kind=kCustom, calls=%fused_computation | custom fusion | bytes 2097280 | tf_op jit(solution)/shard_map/jit(_take)/gather | solution.py:170
  23.0 5.6 %all-to-all-start.1 = ((bf16[8,64,1024]{2,1,0:T(8,128)(2,1)}), bf16[8,64,1024]{2,1,0:T(8,128)(2,1)S(1)}, u32[]{:S(2)}, u32[]{:S(2)}) async-start(bf16[8,64,1024]{2,1,0:T(8,128)(2,1)} %bitcast.1), calls=%async_computation.1 | async-start | bytes 2097152 | tf_op jit(solution)/shard_map/all_to_all | solution.py:173
  28.6 10.5 %add_convert_fusion = bf16[32,128,1024]{2,1,0:T(8,128)(2,1)} fusion(f32[32,128]{1,0:T(8,128)S(1)} %get-tuple-element.18, s32[32,128]{1,0:T(8,128)S(1)} %get-tuple-element.23, f32[32,128]{1,0:T(8,128)S(1)} %get-tuple-element.19, s32[32,128]{1,0:T(8,128)S(1)} %get-tuple-element.22, f32[32,128]{1,0:T(8,128)S(1)} %get-tuple-element.17, ...), kind=kLoop, calls=%fused_computation.2 | loop fusion | flops 50331648 | bytes 8519680 | tf_op jit(solution)/shard_map/convert_element_type | solution.py:37
  39.1 18.7 %all-to-all-done.1 = bf16[8,64,1024]{2,1,0:T(8,128)(2,1)S(1)} async-done(((bf16[8,64,1024]{2,1,0:T(8,128)(2,1)}), bf16[8,64,1024]{2,1,0:T(8,128)(2,1)S(1)}, u32[]{:S(2)}, u32[]{:S(2)}) %all-to-all-start.1) | async-done | bytes 1048608 | tf_op jit(solution)/shard_map/all_to_all | solution.py:173
  58.4 5.7 %fusion.9 = bf16[16,32,128]{2,0,1:T(8,128)(2,1)S(1)} fusion(bf16[32,16,1024]{2,1,0:T(8,128)(2,1)S(1)} %gather_fusion.1, bf16[32,128,1024]{2,1,0:T(8,128)(2,1)} %add_convert_fusion), kind=kOutput, calls=%fused_computation.19 | convolution fusion | flops 134283264 | bytes 9568256 | tf_op jit(solution)/shard_map/qfm,qzm->qfz/dot_general | solution.py:122
  66.8 4.6 %fusion.26 = f32[32,16,1024]{2,1,0:T(8,128)S(1)} fusion(bf16[32,128,1024]{2,1,0:T(8,128)(2,1)} %add_convert_fusion, f32[16,32,128]{2,0,1:T(8,128)S(1)} %get-tuple-element.37, f32[16,32,128]{2,0,1:T(8,128)S(1)} %get-tuple-element.36, f32[16,32,128]{2,0,1:T(8,128)S(1)} %get-tuple-element.35, f32[16,32,128]{2,0,1:T(8,128)S(1)} %get-tuple-element.34, ...), kind=kOutput, calls=%fused_computation.75 | convolution fusion | flops 134807552 | bytes 12845056 | tf_op jit(solution)/shard_map/zrs,rsu->rzu/dot_general | solution.py:145
  71.5 2.4 %fusion.2 = bf16[32,16,1024]{2,0,1:T(8,128)(2,1)S(1)} fusion(f32[32,16,1024]{2,1,0:T(8,128)S(1)} %fusion.26, s32[32]{0:T(128)S(1)} %bitcast.115), kind=kOutput, calls=%fused_computation.11 | convolution fusion | flops 201851904 | bytes 3145856 | tf_op jit(solution)/shard_map/gv,gct->vct/dot_general | solution.py:150
  74.5 0.7 convert_element_type.105
  76.3 41.7 %all_to_all.30 = bf16[64,66,128]{2,1,0:T(8,128)(2,1)S(1)} all-to-all(bf16[64,66,128]{2,1,0:T(8,128)(2,1)S(1)} %pad_maximum_fusion), channel_id=1, replica_groups=mesh['frames'=64,'tex'=8] {'frames'}, dimensions={0} | all-to-all | bytes 2162688 | tf_op jit(solution)/shard_map/all_to_all | solution.py:199
  118.4 0.7 reshape.231
  119.2 1.3 fusion.5
  120.7 15.0 %all_to_all.31 = bf16[8,130,128]{2,1,0:T(8,128)(2,1)S(1)} all-to-all(bf16[8,130,128]{2,1,0:T(8,128)(2,1)S(1)} %pad_maximum_fusion.1), channel_id=1, replica_groups=mesh['frames'=64,'tex'=8] {'tex'}, dimensions={0} | all-to-all | bytes 532480 | tf_op jit(solution)/shard_map/all_to_all | solution.py:225
  136.5 6.2 %all-to-all-start.4 = ((f32[64,1,72]{2,1,0:T(1,128)}), f32[64,1,72]{2,1,0:T(1,128)S(1)}, u32[]{:S(2)}, u32[]{:S(2)}) async-start(f32[64,1,72]{2,1,0:T(1,128)} %broadcast_in_dim.79), calls=%async_computation.4 | async-start | bytes 65536 | tf_op jit(solution)/shard_map/all_to_all | solution.py:231
  142.7 0.8 fusion.25
  144.2 7.7 %all-to-all-done.4 = f32[64,1,72]{2,1,0:T(1,128)S(1)} async-done(((f32[64,1,72]{2,1,0:T(1,128)}), f32[64,1,72]{2,1,0:T(1,128)S(1)}, u32[]{:S(2)}, u32[]{:S(2)}) %all-to-all-start.4) | async-done | bytes 18464 | tf_op jit(solution)/shard_map/all_to_all | solution.py:231
  152.1 0.7 mul.76
  (62 shorter events, 8.4 us)
Async XLA Ops:
  0.6 64.3 %copy-start = (bf16[32,144]{1,0:T(8,128)(2,1)S(1)}, bf16[32,144]{1,0:T(8,128)(2,1)}, u32[]{:S(2)}) copy-start(bf16[32,144]{1,0:T(8,128)(2,1)} %param.12) | copy-start | bytes 27652
  3.2 17.3 %all-to-all-start = ((s32[8,1,4]{2,1,0:T(1,128)}), s32[8,1,4]{2,1,0:T(1,128)S(1)}, u32[]{:S(2)}, u32[]{:S(2)}) async-start(s32[8,1,4]{2,1,0:T(1,128)} %bitcast), calls=%async_computation | async-start | bytes 8192 | tf_op jit(solution)/shard_map/all_to_all | solution.py:167
  23.0 34.8 %all-to-all-start.1 = ((bf16[8,64,1024]{2,1,0:T(8,128)(2,1)}), bf16[8,64,1024]{2,1,0:T(8,128)(2,1)S(1)}, u32[]{:S(2)}, u32[]{:S(2)}) async-start(bf16[8,64,1024]{2,1,0:T(8,128)(2,1)} %bitcast.1), calls=%async_computation.1 | async-start | bytes 2097152 | tf_op jit(solution)/shard_map/all_to_all | solution.py:173
  28.6 10.5 %copy-start.2 = (s32[1,32]{1,0:T(1,128)S(1)}, s32[1,32]{1,0:T(1,128)}, u32[]{:S(2)}) copy-start(s32[1,32]{1,0:T(1,128)} %param.9) | copy-start | bytes 388
  64.1 1.2 copy-start.1
  136.5 15.5 %all-to-all-start.4 = ((f32[64,1,72]{2,1,0:T(1,128)}), f32[64,1,72]{2,1,0:T(1,128)S(1)}, u32[]{:S(2)}, u32[]{:S(2)}) async-start(f32[64,1,72]{2,1,0:T(1,128)} %broadcast_in_dim.79), calls=%async_computation.4 | async-start | bytes 65536 | tf_op jit(solution)/shard_map/all_to_all | solution.py:231

commit v13 on v8

--- a/solution.py
+++ b/solution.py
@@ -195,7 +195,10 @@
     spread = slot_grad.reshape(visible, frame_count, columns).transpose(1, 0, 2)
     spread = spread.astype(jnp.bfloat16).reshape(frame_count, visible * columns // LANE, LANE)
     spread = jnp.concatenate([spread, side_row], axis=1)
-    gathered = lax.all_to_all(spread, "frames", split_axis=0, concat_axis=0, tiled=True)
+    payload_rows = spread.shape[1]
+    gathered = lax.all_to_all(
+        spread.reshape(frame_count, -1), "frames", split_axis=0, concat_axis=0, tiled=True
+    ).reshape(frame_count, payload_rows, LANE)
     grad_rows = visible * columns // LANE
     side = gathered[:, grad_rows:].reshape(frame_count, extra * columns).astype(jnp.float32)
     frame_weight = jnp.sum(side[:, :chunk] + side[:, chunk : 2 * chunk], axis=0)

time: 153 us -> 168 us (1.098)
  other arithmetic: 15.7 us -> 29.4 us
  local copies, waits for them, and re-layouts: 13.9 us -> 17.3 us
  blocking collectives: 56.7 us -> 54.6 us
    all_to_all x0 -> x2, other arithmetic: none -> 13.7 us  [per_device(): lax.all_to_all(spread.reshape(frame_count, -1), 'frames', split_axis=0, c...]
    all_to_all x1, blocking collectives: 41.7 us -> 39.6 us  [per_device(): lax.all_to_all(spread.reshape(frame_count, -1), 'frames', split_axis=0, c...]
    unnamed x19 -> x25, local copies, waits for them, and re-layouts: 4.25 us -> 5.85 us
  transfers between devices with their start and end apart: 3 -> 3, of which waited for: 3 -> 3; matrix products, arithmetic and copies ran while one was open for 11% -> 10% of each run, Pallas kernels for 0% -> 0%
where the time goes in v13:
time: 168 us
  blocking collectives  54.6 us (32%)
  other arithmetic  29.4 us (18%)
  waiting for transfers between devices  27.4 us (16%)
  starting transfers between devices  22.5 us (13%)
  local copies, waits for them, and re-layouts  17.3 us (10%)
  matrix products  15.4 us (9%)
    all_to_all x1, blocking collectives, per_device(): lax.all_to_all(spread.reshape(frame_count, -1), 'frames', split_axis=0, c...  39.6 us
    all_to_all x1, waiting for transfers between devices, per_device(): lax.all_to_all(served, 'tex', split_axis=0, concat_axis=0, tiled=True)  18.5 us
    all_to_all x1, blocking collectives, per_device(): lax.all_to_all(partial, 'tex', 0, 0, tiled=True).astype(jnp.float32)  15 us
    all_to_all x2, other arithmetic, per_device(): lax.all_to_all(spread.reshape(frame_count, -1), 'frames', split_axis=0, c...  13.7 us
    all_to_all x1, starting transfers between devices, per_device(): lax.all_to_all(wanted_ids, 'tex', split_axis=0, concat_axis=0, tiled=True)  10.9 us
    convert_element_type x1, other arithmetic, sample_matrix(): return matrix.astype(jnp.bfloat16)  10.5 us
    all_to_all x1, waiting for transfers between devices, per_device(): lax.all_to_all(jnp.broadcast_to(chunk_total[None], (frame_count, chunk)),...  7.73 us
    all_to_all x1, starting transfers between devices, per_device(): lax.all_to_all(jnp.broadcast_to(chunk_total[None], (frame_count, chunk)),...  6.2 us
  transfers between devices with their start and end apart: 3, of which 3 were waited for; matrix products, arithmetic and copies ran while one was open for 10% of the time, Pallas kernels for 0%

profile of v13, /device:TPU:1, one launch (start us, length us, event | category | flops | bytes accessed | tf_op | source)
XLA Modules:
  0.0 167.7 jit_solution(12740708140920740381)
XLA Ops:
  1.2 1.4 convert_bitcast_fusion
  3.2 10.9 %all-to-all-start = ((s32[8,1,4]{2,1,0:T(1,128)}), s32[8,1,4]{2,1,0:T(1,128)S(1)}, u32[]{:S(2)}, u32[]{:S(2)}) async-start(s32[8,1,4]{2,1,0:T(1,128)} %bitcast.4), calls=%async_computation | async-start | bytes 8192 | tf_op jit(solution)/shard_map/all_to_all | solution.py:166
  14.1 0.8 broadcast_divide_fusion
  14.9 0.8 compare_reduce_fusion
  15.7 0.9 fusion.50
  16.6 2.8 %copy.60 = bf16[8,8,16,1024]{3,2,1,0:T(8,128)(2,1)S(1)} copy(bf16[8,8,16,1024]{3,1,2,0:T(8,128)(2,1)} %bitcast.105) | data formatting | bytes 4194304
  19.4 1.2 all-to-all-done
  21.3 1.7 %gather_fusion = bf16[32,16,1024]{2,1,0:T(8,128)(2,1)} fusion(bf16[64,16,1024]{2,1,0:T(8,128)(2,1)S(1)} %bitcast.102, s32[1024]{0:T(1024)S(1)} %pad_clamp_fusion.1), kind=kCustom, calls=%fused_computation | custom fusion | bytes 2097280 | tf_op jit(solution)/shard_map/jit(_take)/gather | solution.py:169
  23.0 5.5 %all-to-all-start.1 = ((bf16[8,64,1024]{2,1,0:T(8,128)(2,1)}), bf16[8,64,1024]{2,1,0:T(8,128)(2,1)S(1)}, u32[]{:S(2)}, u32[]{:S(2)}) async-start(bf16[8,64,1024]{2,1,0:T(8,128)(2,1)} %bitcast.5), calls=%async_computation.1 | async-start | bytes 2097152 | tf_op jit(solution)/shard_map/all_to_all | solution.py:172
  28.5 10.5 %add_convert_fusion = bf16[32,128,1024]{2,1,0:T(8,128)(2,1)} fusion(f32[32,128]{1,0:T(8,128)S(1)} %get-tuple-element.18, s32[32,128]{1,0:T(8,128)S(1)} %get-tuple-element.23, f32[32,128]{1,0:T(8,128)S(1)} %get-tuple-element.19, s32[32,128]{1,0:T(8,128)S(1)} %get-tuple-element.22, f32[32,128]{1,0:T(8,128)S(1)} %get-tuple-element.17, ...), kind=kLoop, calls=%fused_computation.2 | loop fusion | flops 50331648 | bytes 8519680 | tf_op jit(solution)/shard_map/convert_element_type | solution.py:37
  39.1 18.5 %all-to-all-done.1 = bf16[8,64,1024]{2,1,0:T(8,128)(2,1)S(1)} async-done(((bf16[8,64,1024]{2,1,0:T(8,128)(2,1)}), bf16[8,64,1024]{2,1,0:T(8,128)(2,1)S(1)}, u32[]{:S(2)}, u32[]{:S(2)}) %all-to-all-start.1) | async-done | bytes 1048608 | tf_op jit(solution)/shard_map/all_to_all | solution.py:172
  58.3 5.7 %fusion.9 = bf16[16,32,128]{2,0,1:T(8,128)(2,1)S(1)} fusion(bf16[32,128,1024]{2,1,0:T(8,128)(2,1)} %add_convert_fusion, bf16[32,16,1024]{2,1,0:T(8,128)(2,1)S(1)} %gather_fusion.1), kind=kOutput, calls=%fused_computation.19 | convolution fusion | flops 134283264 | bytes 9568256 | tf_op jit(solution)/shard_map/qfm,qzm->fqz/dot_general | solution.py:122
  67.1 4.6 %fusion.26 = f32[32,16,1024]{2,1,0:T(8,128)S(1)} fusion(bf16[32,128,1024]{2,1,0:T(8,128)(2,1)} %add_convert_fusion, f32[16,32,128]{2,0,1:T(8,128)S(1)} %get-tuple-element.37, f32[16,32,128]{2,0,1:T(8,128)S(1)} %get-tuple-element.36, f32[16,32,128]{2,0,1:T(8,128)S(1)} %get-tuple-element.35, f32[16,32,128]{2,0,1:T(8,128)S(1)} %get-tuple-element.34, ...), kind=kOutput, calls=%fused_computation.75 | convolution fusion | flops 134807552 | bytes 12845056 | tf_op jit(solution)/shard_map/zrs,rsu->rzu/dot_general | solution.py:144
  71.7 2.4 %fusion.2 = bf16[32,16,1024]{2,0,1:T(8,128)(2,1)S(1)} fusion(f32[32,16,1024]{2,1,0:T(8,128)S(1)} %fusion.26, s32[32]{0:T(128)S(1)} %bitcast.115), kind=kOutput, calls=%fused_computation.11 | convolution fusion | flops 201851904 | bytes 3145856 | tf_op jit(solution)/shard_map/gv,gct->vct/dot_general | solution.py:149
  76.5 0.7 all_to_all.29
  77.8 7.2 %reduce.16 = bf16[64,8448]{1,0:T(8,128)(2,1)S(1)} reduce(bf16[64,1,8448]{2,1,0:T(2,128)(2,1)S(1)} %all_to_all.29, bf16[]{:T(256)} %broadcast.255), dimensions={1}, to_apply=%all_to_all.29.reduce_sub_computation | reduce | bytes 2162690 | tf_op jit(solution)/shard_map/all_to_all | solution.py:199
  85.3 39.6 %all_to_all.35 = bf16[64,2,4224]{2,1,0:T(2,128)(2,1)S(1)} all-to-all(bf16[64,2,4224]{2,1,0:T(2,128)(2,1)S(1)} %reshape.292), channel_id=1, replica_groups=mesh['frames'=64,'tex'=8] {'frames'}, dimensions={0} | all-to-all | bytes 2162688 | tf_op jit(solution)/shard_map/all_to_all | solution.py:199
  125.0 0.9 reshape.293
  125.9 6.5 %reduce.3 = bf16[64,8448]{1,0:T(8,128)(2,1)S(1)} reduce(bf16[64,1,8448]{2,1,0:T(2,128)(2,1)S(1)} %reshape.293, bf16[]{:T(256)} %constant.65), dimensions={1}, to_apply=%all_to_all.26.reduce_sub_computation | reduce | bytes 2162690 | tf_op jit(solution)/shard_map/all_to_all | solution.py:199
  134.1 1.3 fusion.5
  135.7 15.0 %all_to_all.36 = bf16[8,130,128]{2,1,0:T(8,128)(2,1)S(1)} all-to-all(bf16[8,130,128]{2,1,0:T(8,128)(2,1)S(1)} %pad_maximum_fusion.1), channel_id=1, replica_groups=mesh['frames'=64,'tex'=8] {'tex'}, dimensions={0} | all-to-all | bytes 532480 | tf_op jit(solution)/shard_map/all_to_all | solution.py:227
  151.5 6.2 %all-to-all-start.4 = ((f32[64,1,72]{2,1,0:T(1,128)}), f32[64,1,72]{2,1,0:T(1,128)S(1)}, u32[]{:S(2)}, u32[]{:S(2)}) async-start(f32[64,1,72]{2,1,0:T(1,128)} %broadcast_in_dim.79), calls=%async_computation.4 | async-start | bytes 65536 | tf_op jit(solution)/shard_map/all_to_all | solution.py:233
  157.7 0.8 fusion.25
  159.2 7.7 %all-to-all-done.4 = f32[64,1,72]{2,1,0:T(1,128)S(1)} async-done(((f32[64,1,72]{2,1,0:T(1,128)}), f32[64,1,72]{2,1,0:T(1,128)S(1)}, u32[]{:S(2)}, u32[]{:S(2)}) %all-to-all-start.4) | async-done | bytes 18464 | tf_op jit(solution)/shard_map/all_to_all | solution.py:233
  (73 shorter events, 13.0 us)
Async XLA Ops:
  0.6 64.2 %copy-start = (bf16[32,144]{1,0:T(8,128)(2,1)S(1)}, bf16[32,144]{1,0:T(8,128)(2,1)}, u32[]{:S(2)}) copy-start(bf16[32,144]{1,0:T(8,128)(2,1)} %param.12) | copy-start | bytes 27652
  3.2 17.3 %all-to-all-start = ((s32[8,1,4]{2,1,0:T(1,128)}), s32[8,1,4]{2,1,0:T(1,128)S(1)}, u32[]{:S(2)}, u32[]{:S(2)}) async-start(s32[8,1,4]{2,1,0:T(1,128)} %bitcast.4), calls=%async_computation | async-start | bytes 8192 | tf_op jit(solution)/shard_map/all_to_all | solution.py:166
  23.0 34.7 %all-to-all-start.1 = ((bf16[8,64,1024]{2,1,0:T(8,128)(2,1)}), bf16[8,64,1024]{2,1,0:T(8,128)(2,1)S(1)}, u32[]{:S(2)}, u32[]{:S(2)}) async-start(bf16[8,64,1024]{2,1,0:T(8,128)(2,1)} %bitcast.5), calls=%async_computation.1 | async-start | bytes 2097152 | tf_op jit(solution)/shard_map/all_to_all | solution.py:172
  28.5 10.6 %copy-start.4 = (s32[1,32]{1,0:T(1,128)S(1)}, s32[1,32]{1,0:T(1,128)}, u32[]{:S(2)}) copy-start(s32[1,32]{1,0:T(1,128)} %param.9) | copy-start | bytes 388
  64.0 1.2 copy-start.3
  65.1 0.9 copy-start.1
  134.1 23.6 %copy-start.2 = (f32[32,4096]{1,0:T(8,128)S(1)}, f32[32,4096]{1,0:T(8,128)}, u32[]{:S(2)}) copy-start(f32[32,4096]{1,0:T(8,128)} %copy-done.1) | copy-start | bytes 1572868
  151.5 15.5 %all-to-all-start.4 = ((f32[64,1,72]{2,1,0:T(1,128)}), f32[64,1,72]{2,1,0:T(1,128)S(1)}, u32[]{:S(2)}, u32[]{:S(2)}) async-start(f32[64,1,72]{2,1,0:T(1,128)} %broadcast_in_dim.79), calls=%async_computation.4 | async-start | bytes 65536 | tf_op jit(solution)/shard_map/all_to_all | solution.py:233
